TPU v7x, 256 devices: a whole 4x4x8 slice. The times are simulated.
256 devices in a mesh: snd: 32 (over z, y), map: 8 (over x, core).
Axes of the slice: x: 4, y: 4, z: 8, core: 2. Of those that a mesh axis runs over, the one named last changes fastest.
Arguments:
- sensitivity_blocks: bfloat16 [32768, 128, 128], P(('snd', 'map')), may hold values from -0.125 to 0.125
- block_placement_table: int32 [3, 32768], P(None, ('snd', 'map')), may hold values from 0 to 63, as said below
- needed_tile_lists: int32 [8192, 4], P(('snd', 'map')), may hold values from -1 to 127, as said below
- location_category: int32 [65536], P('map'), may hold values from 0 to 15
- ground_warmth_celsius: float32 [64, 65536], P('snd', 'map'), may hold values from -5 to 30
- wetness_factor: float32 [64, 65536], P('snd', 'map'), may hold values from 0.2 to 1
- carbon_reservoirs: float32 [3, 65536], P(None, 'map'), may hold values from 0.2 to 3
- category_sensitivity_effect: float32 [16], replicated, may hold values from -4 to 4
- reservoir_decay_effect: float32 [3, 16], replicated, may hold values from -4 to 4
- measured_anomaly: float32 [2048, 128], P(('snd', 'map')), may hold values from -6 to 6
- retrieval_precision: float32 [2048, 128], P(('snd', 'map')), may hold values from 0.5 to 2
Outputs:
- model_xco2: float32 [2048, 128], P(('snd', 'map'))
- flux_grad: float32 [64, 65536], P('snd', 'map')
- class_grad: float32 [4, 16], replicated
- cost: float32 [], replicated
Inputs may be any that keep to these rules, and one draw needn't show every extreme that they name: `block_placement_table`: row 0 is a block row below 64, row 1 a cell tile below 64, row 2 a slot below 64; each block's tile appears in its device's request list to the owner of its slot (slot // 2) as (slot % 2) * 64 + tile. `needed_tile_lists`: row o of a device's 32 rows lists distinct local tile ids of owner o followed by -1; every list has 1 to 4 ids, and on every device some list has exactly 4.
All inputs are finite; a program needn't handle non-finite values.
Results may differ from a plain program's by a relative error of at most 0.0039.
Values may be sent and summed in bfloat16 or wider, within the bound.
No kernel may reach another device: no remote copies, remote signals or barrier semaphores. Data moves between devices by JAX's collectives and lax.ppermute only.
A program may use at most 64 MiB of HBM per device.

v0:
```python
import jax
import jax.numpy as jnp
from jax import lax
from jax.sharding import PartitionSpec as P

BASELINE_CELSIUS = 15.0
LOG_BASE_Q = 0.6931471805599453
PRIOR_VAR = 0.09


def ground_efflux_forward(
    ground_warmth_celsius,
    wetness_factor,
    carbon_reservoirs,
    location_category,
    category_sensitivity_effect,
    reservoir_decay_effect,
):
    nclass = category_sensitivity_effect.shape[0]
    category_onehot = (
        location_category[None, :] == jnp.arange(nclass, dtype=jnp.int32)[:, None]
    ).astype(jnp.float32)
    log_q = (
        LOG_BASE_Q
        + jnp.dot(
            category_sensitivity_effect[None, :], category_onehot, precision=lax.Precision.HIGHEST
        )[0]
    )
    base = jnp.array([0.6, 0.25, 0.1], dtype=jnp.float32)
    rates = base[:, None] * jnp.exp(
        jnp.dot(reservoir_decay_effect, category_onehot, precision=lax.Precision.HIGHEST)
    )
    decay_lifetime = (ground_warmth_celsius - BASELINE_CELSIUS) / 10.0
    modifier = jnp.exp(log_q[None, :] * decay_lifetime) * wetness_factor
    device_number = (rates * carbon_reservoirs)[:, None, :] * modifier[None]
    return (category_onehot, decay_lifetime, device_number)


def shards(
    sensitivity_blocks,
    block_placement_table,
    needed_tile_lists,
    location_category,
    ground_warmth_celsius,
    wetness_factor,
    carbon_reservoirs,
    category_sensitivity_effect,
    reservoir_decay_effect,
    measured_anomaly,
    retrieval_precision,
):
    tile = sensitivity_blocks.shape[1]
    epochs_each_device, locations_each_device = ground_warmth_celsius.shape
    tiles_dev = locations_each_device // tile
    n_snd = lax.axis_size("snd")
    rows_dev = measured_anomaly.shape[0] * lax.axis_size("map")
    category_onehot, decay_lifetime, device_number = ground_efflux_forward(
        ground_warmth_celsius,
        wetness_factor,
        carbon_reservoirs,
        location_category,
        category_sensitivity_effect,
        reservoir_decay_effect,
    )
    flux = device_number[0] + device_number[1] + device_number[2]
    flux_low = flux.astype(jnp.bfloat16)
    block_row = block_placement_table[0]
    block_tile = block_placement_table[1]
    block_slot = block_placement_table[2]
    everything = lax.all_gather(flux_low, "snd", axis=0, tiled=True)
    position = block_slot * tiles_dev + block_tile
    vectors = jnp.take(
        everything.reshape(n_snd * epochs_each_device * tiles_dev, tile), position, axis=0
    )
    contrib = jnp.einsum(
        "bij,bj->bi", sensitivity_blocks, vectors, preferred_element_type=jnp.float32
    )
    row_hot = (jnp.arange(rows_dev, dtype=jnp.int32)[:, None] == block_row[None, :]).astype(
        jnp.float32
    )
    partial_rows = jnp.dot(row_hot, contrib, precision=lax.Precision.HIGHEST)
    model_xco2 = lax.psum_scatter(partial_rows, "map", scatter_dimension=0, tiled=True)
    diff = model_xco2 - measured_anomaly
    weighted = (diff * retrieval_precision).astype(jnp.bfloat16)
    misfit = 0.5 * jnp.sum(retrieval_precision * diff * diff)
    spread = lax.all_gather(weighted, "map", axis=0, tiled=True)
    back_rows = jnp.take(spread, block_row, axis=0)
    block_grads = jnp.einsum(
        "bij,bi->bj", sensitivity_blocks, back_rows, preferred_element_type=jnp.float32
    )
    dense = jax.ops.segment_sum(
        block_grads, position, num_segments=n_snd * epochs_each_device * tiles_dev
    )
    flux_grad = lax.psum_scatter(
        dense.reshape(n_snd * epochs_each_device, locations_each_device),
        "snd",
        scatter_dimension=0,
        tiled=True,
    )
    terms = jnp.stack(
        [
            jnp.sum(flux_grad * flux * decay_lifetime, axis=0),
            jnp.sum(flux_grad * device_number[0], axis=0),
            jnp.sum(flux_grad * device_number[1], axis=0),
            jnp.sum(flux_grad * device_number[2], axis=0),
        ]
    )
    class_part = jnp.dot(terms, category_onehot.T, precision=lax.Precision.HIGHEST)
    total_misfit = lax.psum(misfit, ("snd", "map"))
    class_total = lax.psum(class_part, ("snd", "map"))
    prior = (
        jnp.concatenate([category_sensitivity_effect[None, :], reservoir_decay_effect], axis=0)
        / PRIOR_VAR
    )
    class_grad = class_total + prior
    cost = (
        total_misfit
        + 0.5 * jnp.sum(category_sensitivity_effect * category_sensitivity_effect) / PRIOR_VAR
        + 0.5 * jnp.sum(reservoir_decay_effect * reservoir_decay_effect) / PRIOR_VAR
    )
    return (model_xco2, flux_grad, class_grad, cost)


def solution(mesh):
    in_specs = (
        P(("snd", "map"), None, None),
        P(None, ("snd", "map")),
        P(("snd", "map"), None),
        P("map"),
        P("snd", "map"),
        P("snd", "map"),
        P(None, "map"),
        P(),
        P(),
        P(("snd", "map"), None),
        P(("snd", "map"), None),
    )
    out_specs = (P(("snd", "map"), None), P("snd", "map"), P(), P())
    return jax.shard_map(shards, mesh=mesh, in_specs=in_specs, out_specs=out_specs, check_vma=False)
```

profile of v0, /device:TPU:1, one launch (start us, length us, event | category | flops | bytes accessed | tf_op | source)
XLA Modules:
  0.0 378.4 jit_solution(2134867576984081901)
XLA Ops:
  7.2 0.0 all-gather.3.cloned.1.call-start
  7.2 1.0 fusion.6
  8.3 0.9 exponential_multiply_fusion
  9.2 1.2 fusion.2
  10.5 0.1 broadcast_multiply_fusion
  10.5 0.7 convert_bitcast_fusion
  11.2 0.0 all-gather.3.cloned.1.call-update
  11.2 0.0 all-reduce.5.cloned.1.call-start
  11.3 1.3 dynamic-slice
  13.2 0.8 compare_and_fusion.1
  14.0 0.7 fusion.25
  14.7 0.7 slice_bitcast_fusion.3
  15.4 71.6 %all-gather.3.cloned.1.call-done = bf16[32,2,8192]{2,1,0:T(2,128)(2,1)} async-done(((bf16[1,2,8192]{2,1,0:T(2,128)(2,1)}), bf16[32,2,8192]{2,1,0:T(2,128)(2,1)}) %all-gather.3.cloned.1.call-update) | async-done | bytes 1048592 | tf_op jit(solution)/shard_map/all_gather | solution.py:70
  87.0 1.8 reshape.110
  88.9 0.7 gather_fusion
  89.6 0.1 select_bitcast_fusion.1
  89.7 0.0 copy-start.1
  89.7 0.0 copy-start.2
  89.7 4.4 %fusion.19 = f32[128,1,128]{2,1,0:T(1,128)S(1)} fusion(bf16[128,128,128]{2,1,0:T(8,128)(2,1)} %param.12, bf16[128,128,1]{1,0,2:T(8,128)(2,1)S(1)} %select_bitcast_fusion.1), kind=kOutput, calls=%fused_computation.28 | convolution fusion | flops 4194304 | bytes 4292608 | tf_op jit(solution)/shard_map/bij,bj->bi/dot_general | solution.py:75
  94.1 0.2 fusion.21
  94.3 25.1 %all-reduce = f32[64,128]{1,0:T(8,128)S(1)} all-reduce(f32[64,128]{1,0:T(8,128)S(1)} %fusion.21), channel_id=2, replica_groups=mesh['snd'=32,'map'=8] {'map'}, use_global_device_ids=true, to_apply=%region_0.1.clone | all-reduce | flops 8192 | bytes 65536
  119.4 0.0 copy-done.1
  119.4 0.0 copy-done.2
  119.5 0.6 multiply_reduce_fusion.4
  120.1 0.0 copy-start.3
  120.1 14.6 %all_gather.7 = bf16[64,128]{1,0:T(8,128)(2,1)S(1)} all-gather(bf16[8,128]{1,0:T(8,128)(2,1)S(1)} %multiply_convert_fusion), channel_id=1, replica_groups=mesh['snd'=32,'map'=8] {'map'}, dimensions={0}, use_global_device_ids=true | all-gather | bytes 18432 | tf_op jit(solution)/shard_map/all_gather | solution.py:86
  134.6 0.7 gather_fusion.1
  135.3 0.1 select_bitcast_fusion
  135.4 3.4 fusion.17
  138.8 0.0 copy-done.3
  138.8 1.5 scatter_custom_fusion
  140.3 1.5 reshape.111
  141.9 0.0 copy-start.7
  141.9 0.0 copy-start.6
  141.9 0.0 all-reduce.5.cloned.1.call-update
  141.9 0.6 copy-done.7
  142.5 0.6 dynamic-slice.2
  143.1 0.0 copy-done.5
  143.1 0.6 multiply_reduce_fusion.6
  144.4 0.0 copy-done.4
  144.4 0.6 multiply_reduce_fusion.5
  146.9 141.6 %all-reduce.5.cloned.1.call-done = f32[64,8192]{1,0:T(8,128)} async-done(((f32[64,8192]{1,0:T(8,128)}), f32[64,8192]{1,0:T(8,128)}) %all-reduce.5.cloned.1.call-update) | async-done | bytes 2097168
  288.5 0.0 copy-done
  288.5 1.7 multiply_reduce_fusion.2
  290.3 0.0 copy-done.6
  290.3 0.5 fusion.5
  290.8 78.4 %all-reduce.2 = (f32[4,16]{1,0:T(4,128)S(1)}, f32[]{:T(128)}) all-reduce(f32[4,16]{1,0:T(4,128)S(1)} %fusion.5, f32[]{:T(128)S(6)} %mul.123), channel_id=1, replica_groups=mesh['snd'=32,'map'=8] {'snd','map'}, use_global_device_ids=true, to_apply=%region_7.8 | all-reduce | flops 65 | bytes 520 | tf_op jit(solution)/shard_map/psum | solution.py:110
  369.2 0.6 fusion.23
  (8 shorter events, 0.0 us)
Async XLA Ops:
  7.2 79.8 %all-gather.3.cloned.1.call-start = ((), (), s32[]{:S(2)}) async-start(), calls=%async_computation | async-start | bytes 1081344 | tf_op jit(solution)/shard_map/all_gather | solution.py:70
  11.2 277.3 %all-reduce.5.cloned.1.call-start = ((), (), s32[]{:S(2)}) async-start(), calls=%async_computation.1 | async-start | bytes 4194304
  89.7 29.8 %copy-start.1 = (f32[8,128]{1,0:T(8,128)S(1)}, f32[8,128]{1,0:T(8,128)}, u32[]{:S(2)}) copy-start(f32[8,128]{1,0:T(8,128)} %param.21) | copy-start | bytes 12292
  89.7 29.8 %copy-start.2 = (f32[8,128]{1,0:T(8,128)S(1)}, f32[8,128]{1,0:T(8,128)}, u32[]{:S(2)}) copy-start(f32[8,128]{1,0:T(8,128)} %param.20) | copy-start | bytes 12292
  120.1 18.7 %copy-start.3 = (f32[8,128]{1,0:T(8,128)}, f32[8,128]{1,0:T(8,128)S(1)}, u32[]{:S(2)}) copy-start(f32[8,128]{1,0:T(8,128)S(1)} %get-tuple-element.11) | copy-start | bytes 12292
  141.9 0.7 copy-start.7
  141.9 1.3 copy-start.5
  141.9 2.5 copy-start.4
  141.9 146.7 %copy-start = (f32[2,8192]{1,0:T(2,128)S(1)}, f32[2,8192]{1,0:T(2,128)}, u32[]{:S(2)}) copy-start(f32[2,8192]{1,0:T(2,128)} %param.15) | copy-start | bytes 196612
  141.9 148.4 %copy-start.6 = (s32[8192]{0:T(1024)S(1)}, s32[8192]{0:T(1024)}, u32[]{:S(2)}) copy-start(s32[8192]{0:T(1024)} %param.14) | copy-start | bytes 98308
Sparse Core Ops, SparseCore 0:
  11.4 75.5 all-gather.2
  142.0 146.4 all-reduce.4
where the time goes:
time: 379 us; the launch traced here: 378 us
  waiting for transfers between devices  213 us (56%)
  blocking collectives  118 us (31%)
  between operations  19.2 us (5%)
  matrix products  10.8 us (3%)
  other arithmetic  9.06 us (2%)
  local copies, waits for them, and re-layouts  7.97 us (2%)
    unnamed x3, waiting for transfers between devices  142 us
    psum x1, blocking collectives, shards(): class_total = lax.psum(class_part, ('snd', 'map'))  78.4 us
    all_gather x1, waiting for transfers between devices, shards(): everything = lax.all_gather(flux_low, 'snd', axis=0, tiled=True)  71.6 us
    unnamed x1, blocking collectives  25.1 us
    all_gather x1, blocking collectives, shards(): spread = lax.all_gather(weighted, 'map', axis=0, tiled=True)  14.6 us
  transfers between devices with their start and end apart: 2, of which 2 were waited for; matrix products, arithmetic and copies ran while one was open for 1% of the time, Pallas kernels for 0%

commit v1 on v0

--- a/solution.py
+++ b/solution.py
@@ -52,8 +52,12 @@
     tile = sensitivity_blocks.shape[1]
     epochs_each_device, locations_each_device = ground_warmth_celsius.shape
     tiles_dev = locations_each_device // tile
+    local_ids = epochs_each_device * tiles_dev
     n_snd = lax.axis_size("snd")
-    rows_dev = measured_anomaly.shape[0] * lax.axis_size("map")
+    n_map = lax.axis_size("map")
+    cap = needed_tile_lists.shape[1]
+    rows_own = measured_anomaly.shape[0]
+    rows_dev = rows_own * n_map
     category_onehot, decay_lifetime, device_number = ground_efflux_forward(
         ground_warmth_celsius,
         wetness_factor,
@@ -64,14 +68,24 @@
     )
     flux = device_number[0] + device_number[1] + device_number[2]
     flux_low = flux.astype(jnp.bfloat16)
+
+    requests = lax.all_to_all(needed_tile_lists, "snd", 0, 0, tiled=True)
+    live = requests >= 0
+    own_tiles = flux_low.reshape(local_ids, tile)
+    answer = jnp.take(own_tiles, jnp.where(live, requests, 0).reshape(-1), axis=0)
+    received = lax.all_to_all(
+        answer.reshape(n_snd, cap, tile), "snd", 0, 0, tiled=True
+    ).reshape(n_snd * cap, tile)
+
     block_row = block_placement_table[0]
     block_tile = block_placement_table[1]
     block_slot = block_placement_table[2]
-    everything = lax.all_gather(flux_low, "snd", axis=0, tiled=True)
-    position = block_slot * tiles_dev + block_tile
-    vectors = jnp.take(
-        everything.reshape(n_snd * epochs_each_device * tiles_dev, tile), position, axis=0
-    )
+    owner = block_slot // epochs_each_device
+    wanted = (block_slot % epochs_each_device) * tiles_dev + block_tile
+    listed = jnp.take(needed_tile_lists, owner, axis=0)
+    within = jnp.argmax(listed == wanted[:, None], axis=1).astype(jnp.int32)
+    position = owner * cap + within
+    vectors = jnp.take(received, position, axis=0)
     contrib = jnp.einsum(
         "bij,bj->bi", sensitivity_blocks, vectors, preferred_element_type=jnp.float32
     )
@@ -79,24 +93,32 @@
         jnp.float32
     )
     partial_rows = jnp.dot(row_hot, contrib, precision=lax.Precision.HIGHEST)
-    model_xco2 = lax.psum_scatter(partial_rows, "map", scatter_dimension=0, tiled=True)
+
+    me_map = lax.axis_index("map")
+    first = me_map * rows_own
+    channels = jnp.zeros((3, rows_dev, tile), jnp.float32)
+    channels = channels.at[0].set(partial_rows)
+    channels = lax.dynamic_update_slice(channels, measured_anomaly[None], (1, first, 0))
+    channels = lax.dynamic_update_slice(channels, retrieval_precision[None], (2, first, 0))
+    summed = lax.psum(channels, "map")
+    model_rows = summed[0]
+    weighted_rows = ((model_rows - summed[1]) * summed[2]).astype(jnp.bfloat16)
+    model_xco2 = lax.dynamic_slice(model_rows, (first, 0), (rows_own, tile))
     diff = model_xco2 - measured_anomaly
-    weighted = (diff * retrieval_precision).astype(jnp.bfloat16)
     misfit = 0.5 * jnp.sum(retrieval_precision * diff * diff)
-    spread = lax.all_gather(weighted, "map", axis=0, tiled=True)
-    back_rows = jnp.take(spread, block_row, axis=0)
+
+    back_rows = jnp.take(weighted_rows, block_row, axis=0)
     block_grads = jnp.einsum(
         "bij,bi->bj", sensitivity_blocks, back_rows, preferred_element_type=jnp.float32
     )
-    dense = jax.ops.segment_sum(
-        block_grads, position, num_segments=n_snd * epochs_each_device * tiles_dev
-    )
-    flux_grad = lax.psum_scatter(
-        dense.reshape(n_snd * epochs_each_device, locations_each_device),
-        "snd",
-        scatter_dimension=0,
-        tiled=True,
-    )
+    outgoing = jax.ops.segment_sum(block_grads, position, num_segments=n_snd * cap)
+    incoming = lax.all_to_all(
+        outgoing.reshape(n_snd, cap, tile), "snd", 0, 0, tiled=True
+    ).reshape(n_snd * cap, tile)
+    target = jnp.where(live, requests, local_ids).reshape(-1)
+    grad_tiles = jax.ops.segment_sum(incoming, target, num_segments=local_ids + 1)[:local_ids]
+    flux_grad = grad_tiles.reshape(epochs_each_device, locations_each_device)
+
     terms = jnp.stack(
         [
             jnp.sum(flux_grad * flux * decay_lifetime, axis=0),
@@ -106,8 +128,15 @@
         ]
     )
     class_part = jnp.dot(terms, category_onehot.T, precision=lax.Precision.HIGHEST)
-    total_misfit = lax.psum(misfit, ("snd", "map"))
-    class_total = lax.psum(class_part, ("snd", "map"))
+    nclass = class_part.shape[1]
+    mine = jnp.concatenate([class_part.reshape(-1), misfit[None]])
+    n_all = n_snd * n_map
+    gathered = lax.all_to_all(
+        jnp.broadcast_to(mine[None], (n_all, mine.shape[0])), ("snd", "map"), 0, 0, tiled=True
+    )
+    totals = jnp.sum(gathered, axis=0)
+    class_total = totals[:-1].reshape(4, nclass)
+    total_misfit = totals[-1]
     prior = (
         jnp.concatenate([category_sensitivity_effect[None, :], reservoir_decay_effect], axis=0)
         / PRIOR_VAR

time: 379 us -> 174 us (0.46)
  waiting for transfers between devices: 213 us -> 85.7 us
  blocking collectives: 118 us -> 0 us
  starting transfers between devices: 0.08 us -> 37.7 us
    unnamed x3 -> x1, waiting for transfers between devices: 142 us -> 0.02 us
    psum x1 -> x0, blocking collectives: 78.4 us -> none  [shards(): class_total = lax.psum(class_part, ('snd', 'map'))]
    all_gather x1 -> x0, waiting for transfers between devices: 71.6 us -> none  [shards(): everything = lax.all_gather(flux_low, 'snd', axis=0, tiled=True)]
    psum x0 -> x1, waiting for transfers between devices: none -> 57.3 us  [shards(): summed = lax.psum(channels, 'map')]
    all_to_all x0 -> x4, starting transfers between devices: none -> 37.7 us  [the longest x1 12 us: shards(): requests = lax.all_to_all(needed_tile_lists, 'snd', 0, 0, tiled=True)]
    all_to_all x0 -> x4, waiting for transfers between devices: none -> 28.4 us  [the longest x1 10.6 us: shards(): lax.all_to_all(jnp.broadcast_to(mine[None], (n_all, mine.shape[0])), ('sn...]
    unnamed x1 -> x0, blocking collectives: 25.1 us -> none
    all_gather x1 -> x0, blocking collectives: 14.6 us -> none  [shards(): spread = lax.all_gather(weighted, 'map', axis=0, tiled=True)]
  transfers between devices with their start and end apart: 2 -> 5, of which waited for: 2 -> 5; matrix products, arithmetic and copies ran while one was open for 1% -> 5% of each run, Pallas kernels for 0% -> 0%
where the time goes in v1:
time: 174 us
  waiting for transfers between devices  85.7 us (49%)
  starting transfers between devices  37.7 us (22%)
  between operations  18.1 us (10%)
  other arithmetic  12.8 us (7%)
  matrix products  10.8 us (6%)
  local copies, waits for them, and re-layouts  8.55 us (5%)
    psum x1, waiting for transfers between devices, shards(): summed = lax.psum(channels, 'map')  57.3 us
    all_to_all x1, starting transfers between devices, shards(): requests = lax.all_to_all(needed_tile_lists, 'snd', 0, 0, tiled=True)  12 us
    all_to_all x1, waiting for transfers between devices, shards(): lax.all_to_all(jnp.broadcast_to(mine[None], (n_all, mine.shape[0])), ('sn...  10.6 us
    all_to_all x1, starting transfers between devices, shards(): lax.all_to_all(outgoing.reshape(n_snd, cap, tile), 'snd', 0, 0, tiled=True)  9.53 us
    all_to_all x1, starting transfers between devices, shards(): lax.all_to_all(jnp.broadcast_to(mine[None], (n_all, mine.shape[0])), ('sn...  9.08 us
    all_to_all x1, waiting for transfers between devices, shards(): lax.all_to_all(answer.reshape(n_snd, cap, tile), 'snd', 0, 0, tiled=True)  8.64 us
    all_to_all x1, starting transfers between devices, shards(): lax.all_to_all(answer.reshape(n_snd, cap, tile), 'snd', 0, 0, tiled=True)  7.03 us
    all_to_all x1, waiting for transfers between devices, shards(): lax.all_to_all(outgoing.reshape(n_snd, cap, tile), 'snd', 0, 0, tiled=True)  6.97 us
  transfers between devices with their start and end apart: 5, of which 5 were waited for; matrix products, arithmetic and copies ran while one was open for 5% of the time, Pallas kernels for 0%

profile of v1, /device:TPU:1, one launch (start us, length us, event | category | flops | bytes accessed | tf_op | source)
XLA Modules:
  0.0 173.7 jit_solution(15684750927249343460)
XLA Ops:
  7.2 1.4 copy.30
  8.6 12.0 %all-to-all-start = ((s32[32,1,4]{2,1,0:T(1,128)}), s32[32,1,4]{2,1,0:T(1,128)S(1)}, u32[]{:S(2)}, u32[]{:S(2)}) async-start(s32[32,1,4]{2,1,0:T(1,128)} %copy.30), calls=%async_computation | async-start | bytes 32768 | tf_op jit(solution)/shard_map/all_to_all | solution.py:72
  20.6 0.7 slice_bitcast_fusion
  21.3 0.8 fusion.38
  22.1 1.0 fusion.4
  23.1 0.9 exponential_multiply_fusion
  24.1 1.2 fusion.2
  25.5 0.8 copy.29
  26.3 0.6 gather_fusion
  26.9 2.2 %all-to-all-done = s32[32,1,4]{2,1,0:T(1,128)S(1)} async-done(((s32[32,1,4]{2,1,0:T(1,128)}), s32[32,1,4]{2,1,0:T(1,128)S(1)}, u32[]{:S(2)}, u32[]{:S(2)}) %all-to-all-start) | async-done | bytes 544 | tf_op jit(solution)/shard_map/all_to_all | solution.py:72
  29.1 0.1 all_to_all.24
  29.2 0.5 broadcast.241
  29.7 0.7 reduce.27
  30.4 0.1 all_to_all.22
  30.5 0.8 compare_and_fusion.1
  31.3 0.7 fusion.35
  32.0 0.7 iota_reduce_fusion
  32.7 0.7 gather_fusion.2
  33.4 0.7 broadcast_select_fusion
  34.1 7.0 %all-to-all-start.1 = ((bf16[32,4,128]{2,1,0:T(4,128)(2,1)}), bf16[32,4,128]{2,1,0:T(4,128)(2,1)S(1)}, u32[]{:S(2)}, u32[]{:S(2)}) async-start(bf16[32,4,128]{2,1,0:T(4,128)(2,1)} %bitcast.9), calls=%async_computation.1 | async-start | bytes 65536 | tf_op jit(solution)/shard_map/all_to_all | solution.py:76
  41.2 8.6 %all-to-all-done.1 = bf16[32,4,128]{2,1,0:T(4,128)(2,1)S(1)} async-done(((bf16[32,4,128]{2,1,0:T(4,128)(2,1)}), bf16[32,4,128]{2,1,0:T(4,128)(2,1)S(1)}, u32[]{:S(2)}, u32[]{:S(2)}) %all-to-all-start.1) | async-done | bytes 32800 | tf_op jit(solution)/shard_map/all_to_all | solution.py:76
  49.9 0.7 gather_fusion.3
  50.6 0.1 select_bitcast_fusion
  50.7 4.5 %fusion.23 = f32[128,1,128]{2,1,0:T(1,128)S(1)} fusion(bf16[128,128,128]{2,1,0:T(8,128)(2,1)} %param.16, bf16[128,128,1]{1,0,2:T(8,128)(2,1)S(1)} %select_bitcast_fusion), kind=kOutput, calls=%fused_computation.38 | convolution fusion | flops 4194304 | bytes 4292608 | tf_op jit(solution)/shard_map/bij,bj->bi/dot_general | solution.py:89
  55.2 0.2 convolution_bitcast_fusion
  55.5 0.6 copy-done
  56.1 57.3 %all-reduce.3.cloned.1.call-done = f32[3,64,128]{2,1,0:T(8,128)} async-done(((f32[3,64,128]{2,1,0:T(8,128)}), f32[3,64,128]{2,1,0:T(8,128)}) %all-reduce.3.cloned.1.call-update) | async-done | bytes 98320 | tf_op jit(solution)/shard_map/psum | solution.py:103
  113.4 0.8 fusion.30
  114.2 0.7 gather_fusion.1
  115.0 0.1 select_bitcast_fusion.1
  115.0 3.4 %fusion.21 = f32[128,1,128]{2,1,0:T(1,128)S(1)} fusion(bf16[128,128,128]{2,1,0:T(8,128)(2,1)} %param.16, bf16[128,128,1]{1,0,2:T(8,128)(2,1)S(1)} %select_bitcast_fusion.1), kind=kOutput, calls=%fused_computation.36 | convolution fusion | flops 4194304 | bytes 4292608 | tf_op jit(solution)/shard_map/bij,bi->bj/dot_general | solution.py:111
  118.4 1.6 scatter_custom_fusion
  120.0 9.5 %all-to-all-start.2 = ((f32[32,4,128]{2,1,0:T(4,128)}), f32[32,4,128]{2,1,0:T(4,128)S(1)}, u32[]{:S(2)}, u32[]{:S(2)}) async-start(f32[32,4,128]{2,1,0:T(4,128)} %bitcast.25), calls=%async_computation.2 | async-start | bytes 131072 | tf_op jit(solution)/shard_map/all_to_all | solution.py:115
  129.6 1.2 fusion.32
  131.4 7.0 %all-to-all-done.2 = f32[32,4,128]{2,1,0:T(4,128)S(1)} async-done(((f32[32,4,128]{2,1,0:T(4,128)}), f32[32,4,128]{2,1,0:T(4,128)S(1)}, u32[]{:S(2)}, u32[]{:S(2)}) %all-to-all-start.2) | async-done | bytes 65568 | tf_op jit(solution)/shard_map/all_to_all | solution.py:115
  138.4 1.0 scatter_custom_fusion.1
  139.5 0.4 fusion.17
  139.9 0.5 fusion.3
  140.4 0.1 reshape.271
  140.5 0.1 pad_maximum_fusion
  140.6 0.7 broadcast_in_dim.82
  141.3 9.1 %all-to-all-start.3 = ((f32[256,1,65]{2,1,0:T(1,128)}), f32[256,1,65]{2,1,0:T(1,128)S(1)}, u32[]{:S(2)}, u32[]{:S(2)}) async-start(f32[256,1,65]{2,1,0:T(1,128)} %broadcast_in_dim.82), calls=%async_computation.3 | async-start | bytes 262144 | tf_op jit(solution)/shard_map/all_to_all | solution.py:134
  150.4 0.6 multiply_reduce_fusion
  151.7 0.6 multiply_reduce_fusion.1
  152.9 10.6 %all-to-all-done.3 = f32[256,1,65]{2,1,0:T(1,128)S(1)} async-done(((f32[256,1,65]{2,1,0:T(1,128)}), f32[256,1,65]{2,1,0:T(1,128)S(1)}, u32[]{:S(2)}, u32[]{:S(2)}) %all-to-all-start.3) | async-done | bytes 66592 | tf_op jit(solution)/shard_map/all_to_all | solution.py:134
  163.5 0.3 reduce_sum.77
  163.8 0.6 slice.69
  165.1 0.6 fusion.33
  (34 shorter events, 0.5 us)
Async XLA Ops:
  7.2 48.2 %copy-start.4 = (f32[8,128]{1,0:T(8,128)S(1)}, f32[8,128]{1,0:T(8,128)}, u32[]{:S(2)}) copy-start(f32[8,128]{1,0:T(8,128)} %param.25) | copy-start | bytes 12292
  7.2 48.2 %copy-start.3 = (f32[8,128]{1,0:T(8,128)S(1)}, f32[8,128]{1,0:T(8,128)}, u32[]{:S(2)}) copy-start(f32[8,128]{1,0:T(8,128)} %param.26) | copy-start | bytes 12292
  8.6 20.6 %all-to-all-start = ((s32[32,1,4]{2,1,0:T(1,128)}), s32[32,1,4]{2,1,0:T(1,128)S(1)}, u32[]{:S(2)}, u32[]{:S(2)}) async-start(s32[32,1,4]{2,1,0:T(1,128)} %copy.30), calls=%async_computation | async-start | bytes 32768 | tf_op jit(solution)/shard_map/all_to_all | solution.py:72
  34.1 15.7 %all-to-all-start.1 = ((bf16[32,4,128]{2,1,0:T(4,128)(2,1)}), bf16[32,4,128]{2,1,0:T(4,128)(2,1)S(1)}, u32[]{:S(2)}, u32[]{:S(2)}) async-start(bf16[32,4,128]{2,1,0:T(4,128)(2,1)} %bitcast.9), calls=%async_computation.1 | async-start | bytes 65536 | tf_op jit(solution)/shard_map/all_to_all | solution.py:76
  41.2 72.3 %all-reduce.3.cloned.1.call-start = ((), (), s32[]{:S(2)}) async-start(), calls=%async_computation.4 | async-start | bytes 196608 | tf_op jit(solution)/shard_map/psum | solution.py:103
  50.7 88.8 %copy-start.1 = (f32[2,8192]{1,0:T(2,128)S(1)}, f32[2,8192]{1,0:T(2,128)}, u32[]{:S(2)}) copy-start(f32[2,8192]{1,0:T(2,128)} %param.20) | copy-start | bytes 196612
  50.7 89.2 %copy-start.7 = (s32[8192]{0:T(1024)S(1)}, s32[8192]{0:T(1024)}, u32[]{:S(2)}) copy-start(s32[8192]{0:T(1024)} %param.19) | copy-start | bytes 98308
  55.2 95.2 %copy-start.5 = (f32[3,16]{1,0:T(4,128)S(1)}, f32[3,16]{1,0:T(4,128)}, u32[]{:S(2)}) copy-start(f32[3,16]{1,0:T(4,128)} %param.24) | copy-start | bytes 580
  55.2 96.5 %copy-start.6 = (f32[16]{0:T(128)S(1)}, f32[16]{0:T(128)}, u32[]{:S(2)}) copy-start(f32[16]{0:T(128)} %param.23) | copy-start | bytes 196
  55.4 0.6 copy-start
  120.0 18.4 %all-to-all-start.2 = ((f32[32,4,128]{2,1,0:T(4,128)}), f32[32,4,128]{2,1,0:T(4,128)S(1)}, u32[]{:S(2)}, u32[]{:S(2)}) async-start(f32[32,4,128]{2,1,0:T(4,128)} %bitcast.25), calls=%async_computation.2 | async-start | bytes 131072 | tf_op jit(solution)/shard_map/all_to_all | solution.py:115
  139.5 26.2 %copy-start.2 = (f32[2,8192]{1,0:T(2,128)}, f32[2,8192]{1,0:T(2,128)S(1)}, u32[]{:S(2)}) copy-start(f32[2,8192]{1,0:T(2,128)S(1)} %reshape.270) | copy-start | bytes 196612
  141.3 22.2 %all-to-all-start.3 = ((f32[256,1,65]{2,1,0:T(1,128)}), f32[256,1,65]{2,1,0:T(1,128)S(1)}, u32[]{:S(2)}, u32[]{:S(2)}) async-start(f32[256,1,65]{2,1,0:T(1,128)} %broadcast_in_dim.82), calls=%async_computation.3 | async-start | bytes 262144 | tf_op jit(solution)/shard_map/all_to_all | solution.py:134
Sparse Core Ops, SparseCore 0:
  56.2 57.1 all-reduce.2

commit v2 on v1

--- a/solution.py
+++ b/solution.py
@@ -96,13 +96,14 @@
 
     me_map = lax.axis_index("map")
     first = me_map * rows_own
-    channels = jnp.zeros((3, rows_dev, tile), jnp.float32)
-    channels = channels.at[0].set(partial_rows)
-    channels = lax.dynamic_update_slice(channels, measured_anomaly[None], (1, first, 0))
-    channels = lax.dynamic_update_slice(channels, retrieval_precision[None], (2, first, 0))
-    summed = lax.psum(channels, "map")
-    model_rows = summed[0]
-    weighted_rows = ((model_rows - summed[1]) * summed[2]).astype(jnp.bfloat16)
+    payload = jnp.concatenate([partial_rows, measured_anomaly, retrieval_precision], axis=0)
+    swapped = lax.all_to_all(
+        jnp.broadcast_to(payload[None], (n_map,) + payload.shape), "map", 0, 0, tiled=True
+    )
+    model_rows = jnp.sum(swapped[:, :rows_dev], axis=0)
+    anomaly_rows = swapped[:, rows_dev : rows_dev + rows_own].reshape(rows_dev, tile)
+    precision_rows = swapped[:, rows_dev + rows_own :].reshape(rows_dev, tile)
+    weighted_rows = ((model_rows - anomaly_rows) * precision_rows).astype(jnp.bfloat16)
     model_xco2 = lax.dynamic_slice(model_rows, (first, 0), (rows_own, tile))
     diff = model_xco2 - measured_anomaly
     misfit = 0.5 * jnp.sum(retrieval_precision * diff * diff)

time: 174 us -> 110 us (0.63)
  waiting for transfers between devices: 85.7 us -> 33.3 us
  between operations: 18.1 us -> 4.67 us
    psum x1 -> x0, waiting for transfers between devices: 57.3 us -> none  [shards(): summed = lax.psum(channels, 'map')]
    all_to_all x0 -> x1, waiting for transfers between devices: none -> 6.99 us  [shards(): lax.all_to_all(jnp.broadcast_to(payload[None], (n_map,) + payload.shape),...]
    all_to_all x0 -> x1, starting transfers between devices: none -> 6.95 us  [shards(): lax.all_to_all(jnp.broadcast_to(payload[None], (n_map,) + payload.shape),...]
    all_to_all x1, starting transfers between devices: 9.53 us -> 3.86 us  [shards(): lax.all_to_all(outgoing.reshape(n_snd, cap, tile), 'snd', 0, 0, tiled=True)]
    all_to_all x1, starting transfers between devices: 7.03 us -> 9.2 us  [shards(): lax.all_to_all(answer.reshape(n_snd, cap, tile), 'snd', 0, 0, tiled=True)]
    all_to_all x1, waiting for transfers between devices: 2.19 us -> 0.03 us  [shards(): requests = lax.all_to_all(needed_tile_lists, 'snd', 0, 0, tiled=True)]
    all_to_all x1, starting transfers between devices: 9.08 us -> 7.32 us  [shards(): lax.all_to_all(jnp.broadcast_to(mine[None], (n_all, mine.shape[0])), ('sn...]
  transfers between devices with their start and end apart: 5 -> 5, of which waited for: 5 -> 4; matrix products, arithmetic and copies ran while one was open for 5% -> 10% of each run, Pallas kernels for 0% -> 0%
where the time goes in v2:
time: 110 us; the launch traced here: 109 us
  starting transfers between devices  39.4 us (36%)
  waiting for transfers between devices  33.3 us (30%)
  other arithmetic  12 us (11%)
  matrix products  10.8 us (10%)
  local copies, waits for them, and re-layouts  8.66 us (8%)
  between operations  4.67 us (4%)
    all_to_all x1, starting transfers between devices, shards(): requests = lax.all_to_all(needed_tile_lists, 'snd', 0, 0, tiled=True)  12 us
    all_to_all x1, waiting for transfers between devices, shards(): lax.all_to_all(jnp.broadcast_to(mine[None], (n_all, mine.shape[0])), ('sn...  10.6 us
    all_to_all x1, starting transfers between devices, shards(): lax.all_to_all(answer.reshape(n_snd, cap, tile), 'snd', 0, 0, tiled=True)  9.2 us
    all_to_all x1, waiting for transfers between devices, shards(): lax.all_to_all(answer.reshape(n_snd, cap, tile), 'snd', 0, 0, tiled=True)  8.69 us
    all_to_all x1, starting transfers between devices, shards(): lax.all_to_all(jnp.broadcast_to(mine[None], (n_all, mine.shape[0])), ('sn...  7.32 us
    all_to_all x1, waiting for transfers between devices, shards(): lax.all_to_all(outgoing.reshape(n_snd, cap, tile), 'snd', 0, 0, tiled=True)  7.02 us
    all_to_all x1, waiting for transfers between devices, shards(): lax.all_to_all(jnp.broadcast_to(payload[None], (n_map,) + payload.shape),...  6.99 us
    all_to_all x1, starting transfers between devices, shards(): lax.all_to_all(jnp.broadcast_to(payload[None], (n_map,) + payload.shape),...  6.95 us
  transfers between devices with their start and end apart: 5, of which 4 were waited for; matrix products, arithmetic and copies ran while one was open for 10% of the time, Pallas kernels for 0%

profile of v2, /device:TPU:1, one launch (start us, length us, event | category | flops | bytes accessed | tf_op | source)
XLA Modules:
  0.0 108.8 jit_solution(15896759058892738386)
XLA Ops:
  0.7 1.4 %copy.30 = s32[32,1,4]{2,1,0:T(1,128)} copy(s32[32,1,4]{0,2,1:T(4,128)} %bitcast.116) | data formatting | bytes 1024 | tf_op jit(solution)/shard_map/all_to_all | solution.py:72
  2.0 12.0 %all-to-all-start = ((s32[32,1,4]{2,1,0:T(1,128)}), s32[32,1,4]{2,1,0:T(1,128)S(1)}, u32[]{:S(2)}, u32[]{:S(2)}) async-start(s32[32,1,4]{2,1,0:T(1,128)} %copy.30), calls=%async_computation | async-start | bytes 32768 | tf_op jit(solution)/shard_map/all_to_all | solution.py:72
  14.1 0.7 slice_bitcast_fusion.2
  14.8 0.8 fusion.40
  15.5 0.8 compare_and_fusion.3
  16.3 0.8 copy.29
  17.1 0.7 fusion.37
  17.8 1.0 fusion.4
  18.8 0.9 exponential_multiply_fusion
  19.8 1.2 %fusion.2 = f32[3,8192]{1,0:T(4,128)S(1)} fusion(f32[3,8192]{1,0:T(4,128)} %param.20, f32[3,16]{1,0:T(4,128)} %param.22, s32[8192]{0:T(1024)} %param.17, f32[3]{0:T(128)} %constant.110.clone), kind=kOutput, calls=%fused_computation.9 | convolution fusion | flops 4898816 | bytes 229580 | tf_op jit(solution)/shard_map/dot_general | solution.py:31
  21.0 0.1 broadcast_multiply_fusion
  21.2 0.6 gather_fusion
  21.8 0.7 iota_reduce_fusion
  22.6 0.5 broadcast.204
  23.1 0.7 reduce.25
  23.8 0.1 all_to_all.25
  23.9 0.7 gather_fusion.2
  24.6 0.7 broadcast_select_fusion
  25.3 9.2 %all-to-all-start.1 = ((bf16[32,4,128]{2,1,0:T(4,128)(2,1)}), bf16[32,4,128]{2,1,0:T(4,128)(2,1)S(1)}, u32[]{:S(2)}, u32[]{:S(2)}) async-start(bf16[32,4,128]{2,1,0:T(4,128)(2,1)} %bitcast.9), calls=%async_computation.1 | async-start | bytes 65536 | tf_op jit(solution)/shard_map/all_to_all | solution.py:76
  34.6 8.7 %all-to-all-done.1 = bf16[32,4,128]{2,1,0:T(4,128)(2,1)S(1)} async-done(((bf16[32,4,128]{2,1,0:T(4,128)(2,1)}), bf16[32,4,128]{2,1,0:T(4,128)(2,1)S(1)}, u32[]{:S(2)}, u32[]{:S(2)}) %all-to-all-start.1) | async-done | bytes 32800 | tf_op jit(solution)/shard_map/all_to_all | solution.py:76
  43.2 0.7 gather_fusion.3
  44.0 0.1 select_bitcast_fusion
  44.0 4.4 %fusion.23 = f32[128,1,128]{2,1,0:T(1,128)S(1)} fusion(bf16[128,128,128]{2,1,0:T(8,128)(2,1)} %param.14, bf16[128,128,1]{1,0,2:T(8,128)(2,1)S(1)} %select_bitcast_fusion), kind=kOutput, calls=%fused_computation.38 | convolution fusion | flops 4194304 | bytes 4292608 | tf_op jit(solution)/shard_map/bij,bj->bi/dot_general | solution.py:89
  48.5 0.2 fusion.32
  48.7 0.7 broadcast_in_dim.72
  49.5 7.0 %all-to-all-start.2 = ((f32[8,80,128]{2,1,0:T(8,128)}), f32[8,80,128]{2,1,0:T(8,128)S(1)}, u32[]{:S(2)}, u32[]{:S(2)}) async-start(f32[8,80,128]{2,1,0:T(8,128)} %broadcast_in_dim.72), calls=%async_computation.2 | async-start | bytes 655360 | tf_op jit(solution)/shard_map/all_to_all | solution.py:100
  56.4 0.1 all_to_all.28
  56.5 7.0 %all-to-all-done.2 = f32[8,80,128]{2,1,0:T(8,128)S(1)} async-done(((f32[8,80,128]{2,1,0:T(8,128)}), f32[8,80,128]{2,1,0:T(8,128)S(1)}, u32[]{:S(2)}, u32[]{:S(2)}) %all-to-all-start.2) | async-done | bytes 327712 | tf_op jit(solution)/shard_map/all_to_all | solution.py:100
  63.6 0.7 gather_fusion.1
  64.3 0.1 select_bitcast_fusion.1
  64.4 3.4 %fusion.21 = f32[128,1,128]{2,1,0:T(1,128)S(1)} fusion(bf16[128,128,128]{2,1,0:T(8,128)(2,1)} %param.14, bf16[128,128,1]{1,0,2:T(8,128)(2,1)S(1)} %select_bitcast_fusion.1), kind=kOutput, calls=%fused_computation.36 | convolution fusion | flops 4194304 | bytes 4292608 | tf_op jit(solution)/shard_map/bij,bi->bj/dot_general | solution.py:112
  67.7 1.6 %scatter_custom_fusion = f32[128,128]{1,0:T(8,128)} fusion(s32[128]{0:T(128)S(1)} %get-tuple-element.14, f32[128,128]{1,0:T(8,128)S(1)} %bitcast.109, f32[]{:T(128)} %constant.101.clone.1), kind=kCustom, calls=%fused_computation.54 | custom fusion | flops 16384 | bytes 65540 | tf_op jit(solution)/shard_map/scatter-add | solution.py:115
  69.3 3.9 %all-to-all-start.3 = ((f32[32,4,128]{2,1,0:T(4,128)}), f32[32,4,128]{2,1,0:T(4,128)S(1)}, u32[]{:S(2)}, u32[]{:S(2)}) async-start(f32[32,4,128]{2,1,0:T(4,128)} %bitcast.22), calls=%async_computation.3 | async-start | bytes 131072 | tf_op jit(solution)/shard_map/all_to_all | solution.py:116
  73.2 1.2 %fusion.34 = (f32[]{:T(128)}, f32[8,128]{1,0:T(8,128)}) fusion(f32[8,128]{1,0:T(8,128)S(1)} %copy-done.2, f32[8,128]{1,0:T(8,128)S(1)} %copy-done.3, f32[64,128]{1,0:T(8,128)S(1)} %slice_reduce_fusion, s32[]{:T(128)S(6)} %select_n.100), kind=kLoop, calls=%fused_computation.62 | loop fusion | flops 4095 | bytes 16392 | tf_op jit(solution)/shard_map/reduce_sum | solution.py:109
  75.1 7.0 %all-to-all-done.3 = f32[32,4,128]{2,1,0:T(4,128)S(1)} async-done(((f32[32,4,128]{2,1,0:T(4,128)}), f32[32,4,128]{2,1,0:T(4,128)S(1)}, u32[]{:S(2)}, u32[]{:S(2)}) %all-to-all-start.3) | async-done | bytes 65568 | tf_op jit(solution)/shard_map/all_to_all | solution.py:116
  82.1 1.0 scatter_custom_fusion.1
  83.2 0.4 fusion.17
  83.6 0.5 fusion.3
  84.1 0.1 reshape.241
  84.2 0.1 pad_maximum_fusion.1
  84.3 0.7 broadcast_in_dim.80
  85.0 7.3 %all-to-all-start.4 = ((f32[256,1,65]{2,1,0:T(1,128)}), f32[256,1,65]{2,1,0:T(1,128)S(1)}, u32[]{:S(2)}, u32[]{:S(2)}) async-start(f32[256,1,65]{2,1,0:T(1,128)} %broadcast_in_dim.80), calls=%async_computation.4 | async-start | bytes 262144 | tf_op jit(solution)/shard_map/all_to_all | solution.py:135
  92.3 0.6 multiply_reduce_fusion
  93.6 0.6 multiply_reduce_fusion.1
  94.8 10.6 %all-to-all-done.4 = f32[256,1,65]{2,1,0:T(1,128)S(1)} async-done(((f32[256,1,65]{2,1,0:T(1,128)}), f32[256,1,65]{2,1,0:T(1,128)S(1)}, u32[]{:S(2)}, u32[]{:S(2)}) %all-to-all-start.4) | async-done | bytes 66592 | tf_op jit(solution)/shard_map/all_to_all | solution.py:135
  105.4 0.3 reduce_sum.87
  105.7 0.6 slice.50
  107.0 0.6 fusion.35
  (32 shorter events, 0.4 us)
Async XLA Ops:
  0.6 48.1 %copy-start.2 = (f32[8,128]{1,0:T(8,128)S(1)}, f32[8,128]{1,0:T(8,128)}, u32[]{:S(2)}) copy-start(f32[8,128]{1,0:T(8,128)} %param.24) | copy-start | bytes 12292
  0.6 48.1 %copy-start.3 = (f32[8,128]{1,0:T(8,128)S(1)}, f32[8,128]{1,0:T(8,128)}, u32[]{:S(2)}) copy-start(f32[8,128]{1,0:T(8,128)} %param.23) | copy-start | bytes 12292
  2.0 20.5 %all-to-all-start = ((s32[32,1,4]{2,1,0:T(1,128)}), s32[32,1,4]{2,1,0:T(1,128)S(1)}, u32[]{:S(2)}, u32[]{:S(2)}) async-start(s32[32,1,4]{2,1,0:T(1,128)} %copy.30), calls=%async_computation | async-start | bytes 32768 | tf_op jit(solution)/shard_map/all_to_all | solution.py:72
  25.3 17.9 %all-to-all-start.1 = ((bf16[32,4,128]{2,1,0:T(4,128)(2,1)}), bf16[32,4,128]{2,1,0:T(4,128)(2,1)S(1)}, u32[]{:S(2)}, u32[]{:S(2)}) async-start(bf16[32,4,128]{2,1,0:T(4,128)(2,1)} %bitcast.9), calls=%async_computation.1 | async-start | bytes 65536 | tf_op jit(solution)/shard_map/all_to_all | solution.py:76
  48.5 34.7 %copy-start = (f32[2,8192]{1,0:T(2,128)S(1)}, f32[2,8192]{1,0:T(2,128)}, u32[]{:S(2)}) copy-start(f32[2,8192]{1,0:T(2,128)} %param.18) | copy-start | bytes 196612
  48.5 35.1 %copy-start.6 = (s32[8192]{0:T(1024)S(1)}, s32[8192]{0:T(1024)}, u32[]{:S(2)}) copy-start(s32[8192]{0:T(1024)} %param.17) | copy-start | bytes 98308
  48.5 43.8 %copy-start.4 = (f32[3,16]{1,0:T(4,128)S(1)}, f32[3,16]{1,0:T(4,128)}, u32[]{:S(2)}) copy-start(f32[3,16]{1,0:T(4,128)} %param.22) | copy-start | bytes 580
  48.5 45.1 %copy-start.5 = (f32[16]{0:T(128)S(1)}, f32[16]{0:T(128)}, u32[]{:S(2)}) copy-start(f32[16]{0:T(128)} %param.21) | copy-start | bytes 196
  49.5 14.1 %all-to-all-start.2 = ((f32[8,80,128]{2,1,0:T(8,128)}), f32[8,80,128]{2,1,0:T(8,128)S(1)}, u32[]{:S(2)}, u32[]{:S(2)}) async-start(f32[8,80,128]{2,1,0:T(8,128)} %broadcast_in_dim.72), calls=%async_computation.2 | async-start | bytes 655360 | tf_op jit(solution)/shard_map/all_to_all | solution.py:100
  69.3 12.7 %all-to-all-start.3 = ((f32[32,4,128]{2,1,0:T(4,128)}), f32[32,4,128]{2,1,0:T(4,128)S(1)}, u32[]{:S(2)}, u32[]{:S(2)}) async-start(f32[32,4,128]{2,1,0:T(4,128)} %bitcast.22), calls=%async_computation.3 | async-start | bytes 131072 | tf_op jit(solution)/shard_map/all_to_all | solution.py:116
  83.2 24.5 %copy-start.1 = (f32[2,8192]{1,0:T(2,128)}, f32[2,8192]{1,0:T(2,128)S(1)}, u32[]{:S(2)}) copy-start(f32[2,8192]{1,0:T(2,128)S(1)} %reshape.240) | copy-start | bytes 196612
  85.0 20.4 %all-to-all-start.4 = ((f32[256,1,65]{2,1,0:T(1,128)}), f32[256,1,65]{2,1,0:T(1,128)S(1)}, u32[]{:S(2)}, u32[]{:S(2)}) async-start(f32[256,1,65]{2,1,0:T(1,128)} %broadcast_in_dim.80), calls=%async_computation.4 | async-start | bytes 262144 | tf_op jit(solution)/shard_map/all_to_all | solution.py:135

commit v3 on v2

--- a/solution.py
+++ b/solution.py
@@ -71,11 +71,24 @@
 
     requests = lax.all_to_all(needed_tile_lists, "snd", 0, 0, tiled=True)
     live = requests >= 0
-    own_tiles = flux_low.reshape(local_ids, tile)
-    answer = jnp.take(own_tiles, jnp.where(live, requests, 0).reshape(-1), axis=0)
+    nclass = category_sensitivity_effect.shape[0]
+    cell_class = jnp.broadcast_to(
+        location_category.astype(jnp.float32)[None], (epochs_each_device, locations_each_device)
+    )
+    own_fields = jnp.stack(
+        [
+            flux_low.astype(jnp.float32),
+            flux * decay_lifetime,
+            device_number[0],
+            device_number[1],
+            device_number[2],
+            cell_class,
+        ]
+    ).reshape(6, local_ids, tile)
+    answer = jnp.take(own_fields, jnp.where(live, requests, 0).reshape(-1), axis=1)
     received = lax.all_to_all(
-        answer.reshape(n_snd, cap, tile), "snd", 0, 0, tiled=True
-    ).reshape(n_snd * cap, tile)
+        answer.reshape(6, n_snd, cap, tile), "snd", 1, 1, tiled=True
+    ).reshape(6, n_snd * cap, tile)
 
     block_row = block_placement_table[0]
     block_tile = block_placement_table[1]
@@ -85,7 +98,7 @@
     listed = jnp.take(needed_tile_lists, owner, axis=0)
     within = jnp.argmax(listed == wanted[:, None], axis=1).astype(jnp.int32)
     position = owner * cap + within
-    vectors = jnp.take(received, position, axis=0)
+    vectors = jnp.take(received[0], position, axis=0).astype(jnp.bfloat16)
     contrib = jnp.einsum(
         "bij,bj->bi", sensitivity_blocks, vectors, preferred_element_type=jnp.float32
     )
@@ -113,29 +126,31 @@
         "bij,bi->bj", sensitivity_blocks, back_rows, preferred_element_type=jnp.float32
     )
     outgoing = jax.ops.segment_sum(block_grads, position, num_segments=n_snd * cap)
-    incoming = lax.all_to_all(
-        outgoing.reshape(n_snd, cap, tile), "snd", 0, 0, tiled=True
-    ).reshape(n_snd * cap, tile)
+
+    class_hot = (
+        received[5].reshape(-1)[:, None] == jnp.arange(nclass, dtype=jnp.float32)[None, :]
+    ).astype(jnp.float32)
+    weighted_fields = (outgoing[None] * received[1:5]).reshape(4, -1)
+    class_part = jnp.dot(weighted_fields, class_hot, precision=lax.Precision.HIGHEST)
+    mine = jnp.concatenate([class_part.reshape(-1), misfit[None]])
+    width = mine.shape[0]
+    parcel = jnp.concatenate(
+        [outgoing.reshape(n_snd, cap * tile), jnp.broadcast_to(mine[None], (n_snd, width))],
+        axis=1,
+    )
+    incoming = lax.all_to_all(parcel, "snd", 0, 0, tiled=True)
+    column = jnp.sum(incoming[:, cap * tile :], axis=0)
+    gathered = lax.all_to_all(
+        jnp.broadcast_to(column[None], (n_map, width)), "map", 0, 0, tiled=True
+    )
+    totals = jnp.sum(gathered, axis=0)
+
     target = jnp.where(live, requests, local_ids).reshape(-1)
-    grad_tiles = jax.ops.segment_sum(incoming, target, num_segments=local_ids + 1)[:local_ids]
+    grad_tiles = jax.ops.segment_sum(
+        incoming[:, : cap * tile].reshape(n_snd * cap, tile), target, num_segments=local_ids + 1
+    )[:local_ids]
     flux_grad = grad_tiles.reshape(epochs_each_device, locations_each_device)
 
-    terms = jnp.stack(
-        [
-            jnp.sum(flux_grad * flux * decay_lifetime, axis=0),
-            jnp.sum(flux_grad * device_number[0], axis=0),
-            jnp.sum(flux_grad * device_number[1], axis=0),
-            jnp.sum(flux_grad * device_number[2], axis=0),
-        ]
-    )
-    class_part = jnp.dot(terms, category_onehot.T, precision=lax.Precision.HIGHEST)
-    nclass = class_part.shape[1]
-    mine = jnp.concatenate([class_part.reshape(-1), misfit[None]])
-    n_all = n_snd * n_map
-    gathered = lax.all_to_all(
-        jnp.broadcast_to(mine[None], (n_all, mine.shape[0])), ("snd", "map"), 0, 0, tiled=True
-    )
-    totals = jnp.sum(gathered, axis=0)
     class_total = totals[:-1].reshape(4, nclass)
     total_misfit = totals[-1]
     prior = (

time: 110 us -> 108 us (0.982)
  waiting for transfers between devices: 33.3 us -> 28.5 us
  local copies, waits for them, and re-layouts: 8.66 us -> 10.7 us
    all_to_all x3, waiting for transfers between devices: 26.3 us -> 21.6 us  [the longest x1 12.3 us: shards(): lax.all_to_all(answer.reshape(6, n_snd, cap, tile), 'snd', 1, 1, tiled=True)]
    all_to_all x3, starting transfers between devices: 20.4 us -> 19 us  [the longest x1 9.21 us: shards(): lax.all_to_all(answer.reshape(6, n_snd, cap, tile), 'snd', 1, 1, tiled=True)]
  transfers between devices with their start and end apart: 5 -> 5, of which waited for: 4 -> 4; matrix products, arithmetic and copies ran while one was open for 10% -> 13% of each run, Pallas kernels for 0% -> 0%
where the time goes in v3:
time: 108 us; the launch traced here: 107 us
  starting transfers between devices  38.7 us (36%)
  waiting for transfers between devices  28.5 us (26%)
  other arithmetic  13.1 us (12%)
  matrix products  10.9 us (10%)
  local copies, waits for them, and re-layouts  10.7 us (10%)
  between operations  4.75 us (4%)
    all_to_all x1, waiting for transfers between devices, shards(): lax.all_to_all(answer.reshape(6, n_snd, cap, tile), 'snd', 1, 1, tiled=True)  12.3 us
    all_to_all x1, starting transfers between devices, shards(): requests = lax.all_to_all(needed_tile_lists, 'snd', 0, 0, tiled=True)  12 us
    all_to_all x1, starting transfers between devices, shards(): lax.all_to_all(answer.reshape(6, n_snd, cap, tile), 'snd', 1, 1, tiled=True)  9.21 us
    all_to_all x1, waiting for transfers between devices, shards(): incoming = lax.all_to_all(parcel, 'snd', 0, 0, tiled=True)  8.34 us
    all_to_all x1, starting transfers between devices, shards(): lax.all_to_all(jnp.broadcast_to(payload[None], (n_map,) + payload.shape),...  7.7 us
    all_to_all x1, waiting for transfers between devices, shards(): lax.all_to_all(jnp.broadcast_to(payload[None], (n_map,) + payload.shape),...  6.85 us
    all_to_all x1, starting transfers between devices, shards(): lax.all_to_all(jnp.broadcast_to(column[None], (n_map, width)), 'map', 0,...  5.82 us
    dot_general x1, matrix products, shards(): jnp.einsum('bij,bj->bi', sensitivity_blocks, vectors, preferred_element_t...  4.43 us
  transfers between devices with their start and end apart: 5, of which 4 were waited for; matrix products, arithmetic and copies ran while one was open for 13% of the time, Pallas kernels for 0%

profile of v3, /device:TPU:1, one launch (start us, length us, event | category | flops | bytes accessed | tf_op | source)
XLA Modules:
  0.0 106.7 jit_solution(17539925516333328217)
XLA Ops:
  0.6 1.4 %copy.47 = s32[32,1,4]{2,1,0:T(1,128)} copy(s32[32,1,4]{0,2,1:T(4,128)} %bitcast.106) | data formatting | bytes 1024 | tf_op jit(solution)/shard_map/all_to_all | solution.py:72
  2.0 12.0 %all-to-all-start = ((s32[32,1,4]{2,1,0:T(1,128)}), s32[32,1,4]{2,1,0:T(1,128)S(1)}, u32[]{:S(2)}, u32[]{:S(2)}) async-start(s32[32,1,4]{2,1,0:T(1,128)} %copy.47), calls=%async_computation | async-start | bytes 32768 | tf_op jit(solution)/shard_map/all_to_all | solution.py:72
  14.0 0.8 fusion.30
  14.8 0.8 compare_and_fusion.3
  15.6 0.8 copy.46
  16.4 0.7 fusion.27
  17.0 0.8 convert_bitcast_fusion
  17.8 1.0 fusion.5
  18.9 0.9 exponential_multiply_fusion
  19.9 1.2 %fusion.2 = f32[3,8192]{1,0:T(4,128)S(1)} fusion(f32[3,8192]{1,0:T(4,128)} %param.18, f32[3,16]{1,0:T(4,128)} %param.20, s32[8192]{0:T(1024)} %param.15, f32[3]{0:T(128)} %constant.126.clone), kind=kOutput, calls=%fused_computation.9 | convolution fusion | flops 4898816 | bytes 229580 | tf_op jit(solution)/shard_map/dot_general | solution.py:31
  21.4 0.9 bitcast_multiply_fusion
  22.5 0.2 mul.123
  22.7 0.6 gather_fusion
  23.3 0.2 copy_multiply_fusion
  23.5 0.7 iota_reduce_fusion
  24.2 0.2 pad_maximum_fusion
  24.5 0.5 broadcast.284
  25.1 0.7 reduce.23
  25.9 0.1 copy.49
  26.0 0.8 gather_fusion.1
  26.8 0.9 copy_select_fusion
  27.7 9.2 %all-to-all-start.1 = ((f32[6,32,4,128]{3,2,0,1:T(4,128)}), f32[6,32,4,128]{3,2,0,1:T(4,128)S(1)}, u32[]{:S(2)}, u32[]{:S(2)}) async-start(f32[6,32,4,128]{3,2,0,1:T(4,128)} %copy_select_fusion), calls=%async_computation.1 | async-start | bytes 786432 | tf_op jit(solution)/shard_map/all_to_all | solution.py:89
  36.9 0.7 slice_bitcast_fusion.2
  37.6 12.3 %all-to-all-done.1 = f32[6,32,4,128]{3,2,0,1:T(4,128)S(1)} async-done(((f32[6,32,4,128]{3,2,0,1:T(4,128)}), f32[6,32,4,128]{3,2,0,1:T(4,128)S(1)}, u32[]{:S(2)}, u32[]{:S(2)}) %all-to-all-start.1) | async-done | bytes 393248 | tf_op jit(solution)/shard_map/all_to_all | solution.py:89
  49.9 0.7 gather_fusion.2
  50.7 4.4 %fusion.12 = f32[128,1,128]{2,1,0:T(1,128)S(1)} fusion(bf16[128,128,128]{2,1,0:T(8,128)(2,1)} %param.12, bf16[128,128,1]{1,0,2:T(8,128)(2,1)S(1)} %fusion.16), kind=kOutput, calls=%fused_computation.31 | convolution fusion | flops 4194304 | bytes 4292608 | tf_op jit(solution)/shard_map/bij,bj->bi/dot_general | solution.py:102
  55.2 0.2 fusion.22
  55.4 0.7 broadcast_in_dim.97
  56.1 7.7 %all-to-all-start.2 = ((f32[8,80,128]{2,1,0:T(8,128)}), f32[8,80,128]{2,1,0:T(8,128)S(1)}, u32[]{:S(2)}, u32[]{:S(2)}) async-start(f32[8,80,128]{2,1,0:T(8,128)} %broadcast_in_dim.97), calls=%async_computation.2 | async-start | bytes 655360 | tf_op jit(solution)/shard_map/all_to_all | solution.py:113
  63.9 0.2 slice.71
  64.1 6.9 %all-to-all-done.2 = f32[8,80,128]{2,1,0:T(8,128)S(1)} async-done(((f32[8,80,128]{2,1,0:T(8,128)}), f32[8,80,128]{2,1,0:T(8,128)S(1)}, u32[]{:S(2)}, u32[]{:S(2)}) %all-to-all-start.2) | async-done | bytes 327712 | tf_op jit(solution)/shard_map/all_to_all | solution.py:113
  71.0 1.2 %fusion.24 = (f32[]{:T(128)}, f32[8,128]{1,0:T(8,128)}) fusion(f32[8,128]{1,0:T(8,128)S(1)} %copy-done.1, f32[8,128]{1,0:T(8,128)S(1)} %copy-done.2, f32[64,128]{1,0:T(8,128)S(1)} %slice_reduce_fusion, s32[]{:T(128)S(6)} %select_n.141), kind=kLoop, calls=%fused_computation.59 | loop fusion | flops 4095 | bytes 16392 | tf_op jit(solution)/shard_map/reduce_sum | solution.py:122
  72.2 0.7 gather_fusion.3
  73.0 3.4 %fusion.10 = f32[128,1,128]{2,1,0:T(1,128)S(1)} fusion(bf16[128,128,128]{2,1,0:T(8,128)(2,1)} %param.12, bf16[128,128,1]{1,0,2:T(8,128)(2,1)S(1)} %select_bitcast_fusion), kind=kOutput, calls=%fused_computation.29 | convolution fusion | flops 4194304 | bytes 4292608 | tf_op jit(solution)/shard_map/bij,bi->bj/dot_general | solution.py:125
  76.4 1.0 scatter_custom_fusion
  77.5 0.7 fusion.3
  79.0 0.7 all_to_all.34
  79.7 3.9 %all-to-all-start.3 = ((f32[32,1,577]{2,1,0:T(1,128)}), f32[32,1,577]{2,1,0:T(1,128)S(1)}, u32[]{:S(2)}, u32[]{:S(2)}) async-start(f32[32,1,577]{2,1,0:T(1,128)} %all_to_all.34), calls=%async_computation.3 | async-start | bytes 163840 | tf_op jit(solution)/shard_map/all_to_all | solution.py:141
  83.7 0.6 multiply_reduce_fusion
  84.3 8.3 %all-to-all-done.3 = f32[32,1,577]{2,1,0:T(1,128)S(1)} async-done(((f32[32,1,577]{2,1,0:T(1,128)}), f32[32,1,577]{2,1,0:T(1,128)S(1)}, u32[]{:S(2)}, u32[]{:S(2)}) %all-to-all-start.3) | async-done | bytes 73888 | tf_op jit(solution)/shard_map/all_to_all | solution.py:141
  92.6 0.6 broadcast_in_dim.105
  93.2 5.8 %all-to-all-start.4 = ((f32[8,1,65]{2,1,0:T(1,128)}), f32[8,1,65]{2,1,0:T(1,128)S(1)}, u32[]{:S(2)}, u32[]{:S(2)}) async-start(f32[8,1,65]{2,1,0:T(1,128)} %broadcast_in_dim.105), calls=%async_computation.4 | async-start | bytes 8192 | tf_op jit(solution)/shard_map/all_to_all | solution.py:143
  99.1 0.6 multiply_reduce_fusion.1
  101.0 1.0 scatter_custom_fusion.1
  102.0 0.7 reshape.291
  102.7 1.0 all-to-all-done.4
  103.7 0.6 slice.77
  105.0 0.6 fusion.25
  (50 shorter events, 1.4 us)
Async XLA Ops:
  2.0 22.4 %all-to-all-start = ((s32[32,1,4]{2,1,0:T(1,128)}), s32[32,1,4]{2,1,0:T(1,128)S(1)}, u32[]{:S(2)}, u32[]{:S(2)}) async-start(s32[32,1,4]{2,1,0:T(1,128)} %copy.47), calls=%async_computation | async-start | bytes 32768 | tf_op jit(solution)/shard_map/all_to_all | solution.py:72
  24.2 31.2 %copy-start.1 = (f32[8,128]{1,0:T(8,128)S(1)}, f32[8,128]{1,0:T(8,128)}, u32[]{:S(2)}) copy-start(f32[8,128]{1,0:T(8,128)} %param.22) | copy-start | bytes 12292
  24.2 31.2 %copy-start.2 = (f32[8,128]{1,0:T(8,128)S(1)}, f32[8,128]{1,0:T(8,128)}, u32[]{:S(2)}) copy-start(f32[8,128]{1,0:T(8,128)} %param.21) | copy-start | bytes 12292
  27.7 22.3 %all-to-all-start.1 = ((f32[6,32,4,128]{3,2,0,1:T(4,128)}), f32[6,32,4,128]{3,2,0,1:T(4,128)S(1)}, u32[]{:S(2)}, u32[]{:S(2)}) async-start(f32[6,32,4,128]{3,2,0,1:T(4,128)} %copy_select_fusion), calls=%async_computation.1 | async-start | bytes 786432 | tf_op jit(solution)/shard_map/all_to_all | solution.py:89
  49.9 23.0 %copy-start = (f32[6,32,4,128]{3,2,0,1:T(4,128)}, f32[6,32,4,128]{3,2,0,1:T(4,128)S(1)}, u32[]{:S(2)}) copy-start(f32[6,32,4,128]{3,2,0,1:T(4,128)S(1)} %all-to-all-done.1) | copy-start | bytes 1179652
  56.1 27.5 %copy-start.3 = (f32[3,16]{1,0:T(4,128)S(1)}, f32[3,16]{1,0:T(4,128)}, u32[]{:S(2)}) copy-start(f32[3,16]{1,0:T(4,128)} %param.20) | copy-start | bytes 580
  56.1 14.8 %all-to-all-start.2 = ((f32[8,80,128]{2,1,0:T(8,128)}), f32[8,80,128]{2,1,0:T(8,128)S(1)}, u32[]{:S(2)}, u32[]{:S(2)}) async-start(f32[8,80,128]{2,1,0:T(8,128)} %broadcast_in_dim.97), calls=%async_computation.2 | async-start | bytes 655360 | tf_op jit(solution)/shard_map/all_to_all | solution.py:113
  63.9 35.2 %copy-start.4 = (f32[16]{0:T(128)S(1)}, f32[16]{0:T(128)}, u32[]{:S(2)}) copy-start(f32[16]{0:T(128)} %param.19) | copy-start | bytes 196
  72.9 4.5 %slice-start = ((f32[6,32,4,128]{3,2,0,1:T(4,128)}), f32[1,32,4,128]{3,2,0,1:T(4,128)S(1)}, s32[]{:S(2)}) async-start(f32[6,32,4,128]{3,2,0,1:T(4,128)} %copy-done), calls=%async_computation.5 | async-start | bytes 131072 | tf_op jit(solution)/shard_map/slice | solution.py:131
  79.7 12.9 %all-to-all-start.3 = ((f32[32,1,577]{2,1,0:T(1,128)}), f32[32,1,577]{2,1,0:T(1,128)S(1)}, u32[]{:S(2)}, u32[]{:S(2)}) async-start(f32[32,1,577]{2,1,0:T(1,128)} %all_to_all.34), calls=%async_computation.3 | async-start | bytes 163840 | tf_op jit(solution)/shard_map/all_to_all | solution.py:141
  93.2 10.4 %all-to-all-start.4 = ((f32[8,1,65]{2,1,0:T(1,128)}), f32[8,1,65]{2,1,0:T(1,128)S(1)}, u32[]{:S(2)}, u32[]{:S(2)}) async-start(f32[8,1,65]{2,1,0:T(1,128)} %broadcast_in_dim.105), calls=%async_computation.4 | async-start | bytes 8192 | tf_op jit(solution)/shard_map/all_to_all | solution.py:143

commit v4 on v3

--- a/solution.py
+++ b/solution.py
@@ -17,23 +17,19 @@
     reservoir_decay_effect,
 ):
     nclass = category_sensitivity_effect.shape[0]
-    category_onehot = (
-        location_category[None, :] == jnp.arange(nclass, dtype=jnp.int32)[:, None]
-    ).astype(jnp.float32)
-    log_q = (
-        LOG_BASE_Q
-        + jnp.dot(
-            category_sensitivity_effect[None, :], category_onehot, precision=lax.Precision.HIGHEST
-        )[0]
-    )
+    picked_q = jnp.zeros(location_category.shape, jnp.float32)
+    picked_rate = jnp.zeros((3,) + location_category.shape, jnp.float32)
+    for c in range(nclass):
+        hit = location_category == c
+        picked_q = jnp.where(hit, category_sensitivity_effect[c], picked_q)
+        picked_rate = jnp.where(hit[None], reservoir_decay_effect[:, c : c + 1], picked_rate)
+    log_q = LOG_BASE_Q + picked_q
     base = jnp.array([0.6, 0.25, 0.1], dtype=jnp.float32)
-    rates = base[:, None] * jnp.exp(
-        jnp.dot(reservoir_decay_effect, category_onehot, precision=lax.Precision.HIGHEST)
-    )
+    rates = base[:, None] * jnp.exp(picked_rate)
     decay_lifetime = (ground_warmth_celsius - BASELINE_CELSIUS) / 10.0
     modifier = jnp.exp(log_q[None, :] * decay_lifetime) * wetness_factor
     device_number = (rates * carbon_reservoirs)[:, None, :] * modifier[None]
-    return (category_onehot, decay_lifetime, device_number)
+    return (decay_lifetime, device_number)
 
 
 def shards(
@@ -58,7 +54,7 @@
     cap = needed_tile_lists.shape[1]
     rows_own = measured_anomaly.shape[0]
     rows_dev = rows_own * n_map
-    category_onehot, decay_lifetime, device_number = ground_efflux_forward(
+    decay_lifetime, device_number = ground_efflux_forward(
         ground_warmth_celsius,
         wetness_factor,
         carbon_reservoirs,

time: 108 us -> 122 us (1.13)
  other arithmetic: 13.1 us -> 25.6 us
  local copies, waits for them, and re-layouts: 10.7 us -> 14.4 us
  matrix products: 10.9 us -> 8.69 us
    mul x2, other arithmetic: 0.96 us -> 11.8 us  [ground_efflux_forward(): modifier = jnp.exp(log_q[None, :] * decay_lifetime) * wetness_factor]
    slice x0 -> x2, local copies, waits for them, and re-layouts: none -> 3.67 us  [the longest x1 1.95 us: ground_efflux_forward(): picked_q = jnp.where(hit, category_sensitivity_effect[c], picked_q)]
    dot_general x2 -> x0, matrix products: 2.26 us -> none  [the longest x1 1.23 us: ground_efflux_forward(): jnp.dot(reservoir_decay_effect, category_onehot, precision=lax.Precision....]
    mul x2 -> x3, other arithmetic: 0.25 us -> 1.78 us  [ground_efflux_forward(): device_number = (rates * carbon_reservoirs)[:, None, :] * modifier[None]]
  transfers between devices with their start and end apart: 5 -> 5, of which waited for: 4 -> 4; matrix products, arithmetic and copies ran while one was open for 13% -> 23% of each run, Pallas kernels for 0% -> 0%
where the time goes in v4:
time: 122 us; the launch traced here: 121 us
  starting transfers between devices  38.7 us (32%)
  waiting for transfers between devices  28.5 us (23%)
  other arithmetic  25.6 us (21%)
  local copies, waits for them, and re-layouts  14.4 us (12%)
  matrix products  8.69 us (7%)
  between operations  4.73 us (4%)
    all_to_all x1, waiting for transfers between devices, shards(): lax.all_to_all(answer.reshape(6, n_snd, cap, tile), 'snd', 1, 1, tiled=True)  12.3 us
    all_to_all x1, starting transfers between devices, shards(): requests = lax.all_to_all(needed_tile_lists, 'snd', 0, 0, tiled=True)  12 us
    mul x2, other arithmetic, ground_efflux_forward(): modifier = jnp.exp(log_q[None, :] * decay_lifetime) * wetness_factor  11.8 us
    all_to_all x1, starting transfers between devices, shards(): lax.all_to_all(answer.reshape(6, n_snd, cap, tile), 'snd', 1, 1, tiled=True)  9.21 us
    all_to_all x1, waiting for transfers between devices, shards(): incoming = lax.all_to_all(parcel, 'snd', 0, 0, tiled=True)  8.34 us
    all_to_all x1, starting transfers between devices, shards(): lax.all_to_all(jnp.broadcast_to(payload[None], (n_map,) + payload.shape),...  7.7 us
    all_to_all x1, waiting for transfers between devices, shards(): lax.all_to_all(jnp.broadcast_to(payload[None], (n_map,) + payload.shape),...  6.85 us
    all_to_all x1, starting transfers between devices, shards(): lax.all_to_all(jnp.broadcast_to(column[None], (n_map, width)), 'map', 0,...  5.82 us
  transfers between devices with their start and end apart: 5, of which 4 were waited for; matrix products, arithmetic and copies ran while one was open for 23% of the time, Pallas kernels for 0%

profile of v4, /device:TPU:1, one launch (start us, length us, event | category | flops | bytes accessed | tf_op | source)
XLA Modules:
  0.0 120.5 jit_solution(4682710173983943848)
XLA Ops:
  0.6 1.4 %copy.47 = s32[32,1,4]{2,1,0:T(1,128)} copy(s32[32,1,4]{0,2,1:T(4,128)} %bitcast.113) | data formatting | bytes 1024 | tf_op jit(solution)/shard_map/all_to_all | solution.py:68
  2.0 12.0 %all-to-all-start = ((s32[32,1,4]{2,1,0:T(1,128)}), s32[32,1,4]{2,1,0:T(1,128)S(1)}, u32[]{:S(2)}, u32[]{:S(2)}) async-start(s32[32,1,4]{2,1,0:T(1,128)} %copy.47), calls=%async_computation | async-start | bytes 32768 | tf_op jit(solution)/shard_map/all_to_all | solution.py:68
  14.0 0.8 fusion.24
  14.8 0.8 compare_and_fusion.3
  15.6 0.8 copy.46
  16.4 0.7 fusion.21
  17.0 2.0 %fusion.26 = (f32[1]{0:T(128)}, f32[1]{0:T(128)}, f32[1]{0:T(128)}, f32[1]{0:T(128)}, f32[1]{0:T(128)}, /*index=5*/f32[1]{0:T(128)}, f32[1]{0:T(128)}, f32[1]{0:...) fusion(f32[16]{0:T(128)} %param.19), kind=kLoop, calls=%fused_computation.126 | loop fusion | bytes 128 | tf_op jit(solution)/shard_map/slice | solution.py:24
  19.0 1.7 %slice_reduce_fusion.17 = (f32[3]{0:T(128)S(1)}, f32[3]{0:T(128)S(1)}, f32[3]{0:T(128)S(1)}, f32[3]{0:T(128)S(1)}, f32[3]{0:T(128)S(1)}, /*index=5*/f32[3]{0:T(1...) fusion(f32[3,16]{1,0:T(4,128)} %param.20), kind=kLoop, calls=%fused_computation.100 | loop fusion | bytes 384 | tf_op jit(solution)/shard_map/slice | solution.py:25
  20.7 0.8 convert_bitcast_fusion
  21.5 10.9 %add_multiply_fusion = (f32[8192]{0:T(1024)S(1)}, pred[8192]{0:T(1024)(128)(4,1)S(1)}, pred[8192]{0:T(1024)(128)(4,1)S(1)}, pred[8192]{0:T(1024)(128)(4,1)S(1)},...) fusion(f32[]{:T(128)} %bitcast.22, f32[]{:T(128)} %bitcast.21, ...), kind=kLoop, calls=%fused_computation.44 | loop fusion | flops 278528 | bytes 196672 | tf_op jit(solution)/shard_map/mul | solution.py:30
  32.4 0.9 exponential_multiply_fusion
  33.4 1.5 %multiply_multiply_fusion = f32[3,8192]{1,0:T(4,128)S(1)} fusion(f32[3,8192]{1,0:T(4,128)} %param.18, f32[3]{0:T(128)S(1)} %get-tuple-element.7, f32[3]{0:T(128)S(1)} %get-tuple-element.8, f32[3]{0:T(128)S(1)} %get-tuple-element.9, f32[3]{0:T(128)S(1)} %get-tuple-element.10, f32[3]{0:T(128)S(1)} %get-tuple-element.11, f32[3]{0:T(128)S(1)} %get-tuple-element.12, ...), kind=kLoop, calls=%fused_computation.15 | loop fusion | flops 442368 | bytes 327884 | tf_op jit(solution)/shard_map/mul | solution.py:31
  35.2 0.9 bitcast_multiply_fusion
  36.3 0.2 mul.119
  36.5 0.6 gather_fusion
  37.1 0.2 copy_multiply_fusion
  37.3 0.7 iota_reduce_fusion
  38.0 0.2 pad_maximum_fusion
  38.4 0.5 broadcast.320
  38.9 0.7 reduce.55
  39.8 0.8 gather_fusion.1
  40.6 0.9 copy_select_fusion
  41.5 9.2 %all-to-all-start.1 = ((f32[6,32,4,128]{3,2,0,1:T(4,128)}), f32[6,32,4,128]{3,2,0,1:T(4,128)S(1)}, u32[]{:S(2)}, u32[]{:S(2)}) async-start(f32[6,32,4,128]{3,2,0,1:T(4,128)} %copy_select_fusion), calls=%async_computation.1 | async-start | bytes 786432 | tf_op jit(solution)/shard_map/all_to_all | solution.py:85
  50.7 0.7 slice_bitcast_fusion.2
  51.4 12.3 %all-to-all-done.1 = f32[6,32,4,128]{3,2,0,1:T(4,128)S(1)} async-done(((f32[6,32,4,128]{3,2,0,1:T(4,128)}), f32[6,32,4,128]{3,2,0,1:T(4,128)S(1)}, u32[]{:S(2)}, u32[]{:S(2)}) %all-to-all-start.1) | async-done | bytes 393248 | tf_op jit(solution)/shard_map/all_to_all | solution.py:85
  63.8 0.7 gather_fusion.2
  64.6 4.4 %fusion.6 = f32[128,1,128]{2,1,0:T(1,128)S(1)} fusion(bf16[128,128,128]{2,1,0:T(8,128)(2,1)} %param.12, bf16[128,128,1]{1,0,2:T(8,128)(2,1)S(1)} %fusion.10), kind=kOutput, calls=%fused_computation.24 | convolution fusion | flops 4194304 | bytes 4292608 | tf_op jit(solution)/shard_map/bij,bj->bi/dot_general | solution.py:98
  69.0 0.2 fusion.16
  69.2 0.7 broadcast_in_dim.429
  70.0 7.7 %all-to-all-start.2 = ((f32[8,80,128]{2,1,0:T(8,128)}), f32[8,80,128]{2,1,0:T(8,128)S(1)}, u32[]{:S(2)}, u32[]{:S(2)}) async-start(f32[8,80,128]{2,1,0:T(8,128)} %broadcast_in_dim.429), calls=%async_computation.2 | async-start | bytes 655360 | tf_op jit(solution)/shard_map/all_to_all | solution.py:109
  77.9 6.9 %all-to-all-done.2 = f32[8,80,128]{2,1,0:T(8,128)S(1)} async-done(((f32[8,80,128]{2,1,0:T(8,128)}), f32[8,80,128]{2,1,0:T(8,128)S(1)}, u32[]{:S(2)}, u32[]{:S(2)}) %all-to-all-start.2) | async-done | bytes 327712 | tf_op jit(solution)/shard_map/all_to_all | solution.py:109
  84.8 1.2 fusion.18
  86.0 0.7 gather_fusion.3
  86.8 3.4 %fusion.4 = f32[128,1,128]{2,1,0:T(1,128)S(1)} fusion(bf16[128,128,128]{2,1,0:T(8,128)(2,1)} %param.12, bf16[128,128,1]{1,0,2:T(8,128)(2,1)S(1)} %select_bitcast_fusion), kind=kOutput, calls=%fused_computation.22 | convolution fusion | flops 4194304 | bytes 4292608 | tf_op jit(solution)/shard_map/bij,bi->bj/dot_general | solution.py:121
  90.2 1.0 scatter_custom_fusion
  91.3 0.7 fusion
  92.8 0.7 all_to_all.34
  93.5 3.9 %all-to-all-start.3 = ((f32[32,1,577]{2,1,0:T(1,128)}), f32[32,1,577]{2,1,0:T(1,128)S(1)}, u32[]{:S(2)}, u32[]{:S(2)}) async-start(f32[32,1,577]{2,1,0:T(1,128)} %all_to_all.34), calls=%async_computation.3 | async-start | bytes 163840 | tf_op jit(solution)/shard_map/all_to_all | solution.py:137
  97.5 0.6 multiply_reduce_fusion
  98.1 8.3 %all-to-all-done.3 = f32[32,1,577]{2,1,0:T(1,128)S(1)} async-done(((f32[32,1,577]{2,1,0:T(1,128)}), f32[32,1,577]{2,1,0:T(1,128)S(1)}, u32[]{:S(2)}, u32[]{:S(2)}) %all-to-all-start.3) | async-done | bytes 73888 | tf_op jit(solution)/shard_map/all_to_all | solution.py:137
  106.5 0.6 broadcast_in_dim.437
  107.1 5.8 %all-to-all-start.4 = ((f32[8,1,65]{2,1,0:T(1,128)}), f32[8,1,65]{2,1,0:T(1,128)S(1)}, u32[]{:S(2)}, u32[]{:S(2)}) async-start(f32[8,1,65]{2,1,0:T(1,128)} %broadcast_in_dim.437), calls=%async_computation.4 | async-start | bytes 8192 | tf_op jit(solution)/shard_map/all_to_all | solution.py:139
  112.9 0.6 multiply_reduce_fusion.1
  114.8 1.0 scatter_custom_fusion.1
  115.8 0.7 reshape.300
  116.5 1.0 all-to-all-done.4
  117.5 0.6 slice.205
  118.8 0.6 fusion.19
  (51 shorter events, 1.6 us)
Async XLA Ops:
  2.0 36.3 %all-to-all-start = ((s32[32,1,4]{2,1,0:T(1,128)}), s32[32,1,4]{2,1,0:T(1,128)S(1)}, u32[]{:S(2)}, u32[]{:S(2)}) async-start(s32[32,1,4]{2,1,0:T(1,128)} %copy.47), calls=%async_computation | async-start | bytes 32768 | tf_op jit(solution)/shard_map/all_to_all | solution.py:68
  38.0 31.2 %copy-start.3 = (f32[8,128]{1,0:T(8,128)S(1)}, f32[8,128]{1,0:T(8,128)}, u32[]{:S(2)}) copy-start(f32[8,128]{1,0:T(8,128)} %param.22) | copy-start | bytes 12292
  38.0 31.2 %copy-start.4 = (f32[8,128]{1,0:T(8,128)S(1)}, f32[8,128]{1,0:T(8,128)}, u32[]{:S(2)}) copy-start(f32[8,128]{1,0:T(8,128)} %param.21) | copy-start | bytes 12292
  41.5 22.3 %all-to-all-start.1 = ((f32[6,32,4,128]{3,2,0,1:T(4,128)}), f32[6,32,4,128]{3,2,0,1:T(4,128)S(1)}, u32[]{:S(2)}, u32[]{:S(2)}) async-start(f32[6,32,4,128]{3,2,0,1:T(4,128)} %copy_select_fusion), calls=%async_computation.1 | async-start | bytes 786432 | tf_op jit(solution)/shard_map/all_to_all | solution.py:85
  63.7 23.0 %copy-start = (f32[6,32,4,128]{3,2,0,1:T(4,128)}, f32[6,32,4,128]{3,2,0,1:T(4,128)S(1)}, u32[]{:S(2)}) copy-start(f32[6,32,4,128]{3,2,0,1:T(4,128)S(1)} %all-to-all-done.1) | copy-start | bytes 1179652
  70.0 27.5 %copy-start.1 = (f32[3,16]{1,0:T(4,128)S(1)}, f32[3,16]{1,0:T(4,128)}, u32[]{:S(2)}) copy-start(f32[3,16]{1,0:T(4,128)} %param.20) | copy-start | bytes 580
  70.0 14.8 %all-to-all-start.2 = ((f32[8,80,128]{2,1,0:T(8,128)}), f32[8,80,128]{2,1,0:T(8,128)S(1)}, u32[]{:S(2)}, u32[]{:S(2)}) async-start(f32[8,80,128]{2,1,0:T(8,128)} %broadcast_in_dim.429), calls=%async_computation.2 | async-start | bytes 655360 | tf_op jit(solution)/shard_map/all_to_all | solution.py:109
  77.7 35.2 %copy-start.2 = (f32[16]{0:T(128)S(1)}, f32[16]{0:T(128)}, u32[]{:S(2)}) copy-start(f32[16]{0:T(128)} %param.19) | copy-start | bytes 196
  86.7 4.5 %slice-start = ((f32[6,32,4,128]{3,2,0,1:T(4,128)}), f32[1,32,4,128]{3,2,0,1:T(4,128)S(1)}, s32[]{:S(2)}) async-start(f32[6,32,4,128]{3,2,0,1:T(4,128)} %copy-done), calls=%async_computation.5 | async-start | bytes 131072 | tf_op jit(solution)/shard_map/slice | solution.py:127
  93.5 12.9 %all-to-all-start.3 = ((f32[32,1,577]{2,1,0:T(1,128)}), f32[32,1,577]{2,1,0:T(1,128)S(1)}, u32[]{:S(2)}, u32[]{:S(2)}) async-start(f32[32,1,577]{2,1,0:T(1,128)} %all_to_all.34), calls=%async_computation.3 | async-start | bytes 163840 | tf_op jit(solution)/shard_map/all_to_all | solution.py:137
  107.1 10.4 %all-to-all-start.4 = ((f32[8,1,65]{2,1,0:T(1,128)}), f32[8,1,65]{2,1,0:T(1,128)S(1)}, u32[]{:S(2)}, u32[]{:S(2)}) async-start(f32[8,1,65]{2,1,0:T(1,128)} %broadcast_in_dim.437), calls=%async_computation.4 | async-start | bytes 8192 | tf_op jit(solution)/shard_map/all_to_all | solution.py:139

commit v5 on v3

--- a/solution.py
+++ b/solution.py
@@ -2,6 +2,8 @@
 import jax.numpy as jnp
 from jax import lax
 from jax.sharding import PartitionSpec as P
+from jax.experimental import pallas as pl
+from jax.experimental.pallas import tpu as pltpu
 
 BASELINE_CELSIUS = 15.0
 LOG_BASE_Q = 0.6931471805599453
@@ -34,6 +36,61 @@
     modifier = jnp.exp(log_q[None, :] * decay_lifetime) * wetness_factor
     device_number = (rates * carbon_reservoirs)[:, None, :] * modifier[None]
     return (category_onehot, decay_lifetime, device_number)
+
+
+def _fields_kernel(cse_ref, rde_ref, cat_ref, warm_ref, wet_ref, carbon_ref, out_ref):
+    nclass = cse_ref.shape[0]
+    cat = cat_ref[...]
+    picked_q = jnp.zeros(cat.shape, jnp.float32)
+    picked = [jnp.zeros(cat.shape, jnp.float32) for _ in range(3)]
+    for c in range(nclass):
+        hit = cat == c
+        picked_q = jnp.where(hit, cse_ref[c], picked_q)
+        for p in range(3):
+            picked[p] = jnp.where(hit, rde_ref[p * nclass + c], picked[p])
+    log_q = LOG_BASE_Q + picked_q
+    base = (0.6, 0.25, 0.1)
+    held = [base[p] * jnp.exp(picked[p]) * carbon_ref[p] for p in range(3)]
+    category = cat.astype(jnp.float32)
+    for t in range(warm_ref.shape[0]):
+        tau = (warm_ref[t] - BASELINE_CELSIUS) / 10.0
+        modifier = jnp.exp(log_q * tau) * wet_ref[t]
+        parts = [held[p] * modifier for p in range(3)]
+        flux = parts[0] + parts[1] + parts[2]
+        out_ref[0, t] = flux.astype(jnp.bfloat16).astype(jnp.float32)
+        out_ref[1, t] = flux * tau
+        out_ref[2, t] = parts[0]
+        out_ref[3, t] = parts[1]
+        out_ref[4, t] = parts[2]
+        out_ref[5, t] = category
+
+
+def owner_fields(
+    ground_warmth_celsius,
+    wetness_factor,
+    carbon_reservoirs,
+    location_category,
+    category_sensitivity_effect,
+    reservoir_decay_effect,
+    tile,
+):
+    epochs, cells = ground_warmth_celsius.shape
+    rows = cells // tile
+    smem = pl.BlockSpec(memory_space=pltpu.SMEM)
+    vmem = pl.BlockSpec(memory_space=pltpu.VMEM)
+    return pl.pallas_call(
+        _fields_kernel,
+        out_shape=jax.ShapeDtypeStruct((6, epochs, rows, tile), jnp.float32),
+        in_specs=[smem, smem, vmem, vmem, vmem, vmem],
+        out_specs=vmem,
+    )(
+        category_sensitivity_effect,
+        reservoir_decay_effect.reshape(-1),
+        location_category.reshape(rows, tile),
+        ground_warmth_celsius.reshape(epochs, rows, tile),
+        wetness_factor.reshape(epochs, rows, tile),
+        carbon_reservoirs.reshape(3, rows, tile),
+    )
 
 
 def shards(
@@ -58,32 +115,17 @@
     cap = needed_tile_lists.shape[1]
     rows_own = measured_anomaly.shape[0]
     rows_dev = rows_own * n_map
-    category_onehot, decay_lifetime, device_number = ground_efflux_forward(
+    requests = lax.all_to_all(needed_tile_lists, "snd", 0, 0, tiled=True)
+    live = requests >= 0
+    nclass = category_sensitivity_effect.shape[0]
+    own_fields = owner_fields(
         ground_warmth_celsius,
         wetness_factor,
         carbon_reservoirs,
         location_category,
         category_sensitivity_effect,
         reservoir_decay_effect,
-    )
-    flux = device_number[0] + device_number[1] + device_number[2]
-    flux_low = flux.astype(jnp.bfloat16)
-
-    requests = lax.all_to_all(needed_tile_lists, "snd", 0, 0, tiled=True)
-    live = requests >= 0
-    nclass = category_sensitivity_effect.shape[0]
-    cell_class = jnp.broadcast_to(
-        location_category.astype(jnp.float32)[None], (epochs_each_device, locations_each_device)
-    )
-    own_fields = jnp.stack(
-        [
-            flux_low.astype(jnp.float32),
-            flux * decay_lifetime,
-            device_number[0],
-            device_number[1],
-            device_number[2],
-            cell_class,
-        ]
+        tile,
     ).reshape(6, local_ids, tile)
     answer = jnp.take(own_fields, jnp.where(live, requests, 0).reshape(-1), axis=1)
     received = lax.all_to_all(

time: 108 us -> 109 us (level)
  local copies, waits for them, and re-layouts: 10.7 us -> 15.8 us
  other arithmetic: 13.1 us -> 9.96 us
  matrix products: 10.9 us -> 8.69 us
  Pallas kernels: 0 us -> 1.87 us
    reshape x0 -> x3, local copies, waits for them, and re-layouts: none -> 4.05 us  [the longest x1 1.51 us: owner_fields(): wetness_factor.reshape(epochs, rows, tile)]
    dot_general x2 -> x0, matrix products: 2.26 us -> none  [the longest x1 1.23 us: ground_efflux_forward(): jnp.dot(reservoir_decay_effect, category_onehot, precision=lax.Precision....]
    mul x5 -> x0, other arithmetic: 2.11 us -> none  [the longest x2 0.96 us: ground_efflux_forward(): modifier = jnp.exp(log_q[None, :] * decay_lifetime) * wetness_factor]
    pallas_call x0 -> x1, Pallas kernels: none -> 1.87 us  [owner_fields(): pl.pallas_call(_fields_kernel, out_shape=jax.ShapeDtypeStruct((6, epochs,...]
    unnamed x12 -> x13, local copies, waits for them, and re-layouts: 0.79 us -> 2.33 us
  transfers between devices with their start and end apart: 5 -> 5, of which waited for: 4 -> 4; matrix products, arithmetic and copies ran while one was open for 13% -> 13% of each run, Pallas kernels for 0% -> 2%
where the time goes in v5:
time: 109 us; the launch traced here: 108 us
  starting transfers between devices  38.7 us (36%)
  waiting for transfers between devices  28.5 us (26%)
  local copies, waits for them, and re-layouts  15.8 us (14%)
  other arithmetic  9.96 us (9%)
  matrix products  8.69 us (8%)
  between operations  4.65 us (4%)
  Pallas kernels  1.87 us (2%)
    all_to_all x1, waiting for transfers between devices, shards(): lax.all_to_all(answer.reshape(6, n_snd, cap, tile), 'snd', 1, 1, tiled=True)  12.3 us
    all_to_all x1, starting transfers between devices, shards(): requests = lax.all_to_all(needed_tile_lists, 'snd', 0, 0, tiled=True)  12 us
    all_to_all x1, starting transfers between devices, shards(): lax.all_to_all(answer.reshape(6, n_snd, cap, tile), 'snd', 1, 1, tiled=True)  9.22 us
    all_to_all x1, waiting for transfers between devices, shards(): incoming = lax.all_to_all(parcel, 'snd', 0, 0, tiled=True)  8.34 us
    all_to_all x1, starting transfers between devices, shards(): lax.all_to_all(jnp.broadcast_to(payload[None], (n_map,) + payload.shape),...  7.7 us
    all_to_all x1, waiting for transfers between devices, shards(): lax.all_to_all(jnp.broadcast_to(payload[None], (n_map,) + payload.shape),...  6.85 us
    all_to_all x1, starting transfers between devices, shards(): lax.all_to_all(jnp.broadcast_to(column[None], (n_map, width)), 'map', 0,...  5.82 us
    dot_general x1, matrix products, shards(): jnp.einsum('bij,bj->bi', sensitivity_blocks, vectors, preferred_element_t...  4.43 us
  transfers between devices with their start and end apart: 5, of which 4 were waited for; matrix products, arithmetic and copies ran while one was open for 13% of the time, Pallas kernels for 2%

profile of v5, /device:TPU:1, one launch (start us, length us, event | category | flops | bytes accessed | tf_op | source)
XLA Modules:
  0.0 108.1 jit_solution(10944308676438474272)
XLA Ops:
  0.6 1.4 %copy.43 = s32[32,1,4]{2,1,0:T(1,128)} copy(s32[32,1,4]{0,2,1:T(4,128)} %bitcast.108) | data formatting | bytes 1024 | tf_op jit(solution)/shard_map/all_to_all | solution.py:118
  2.0 12.0 %all-to-all-start = ((s32[32,1,4]{2,1,0:T(1,128)}), s32[32,1,4]{2,1,0:T(1,128)S(1)}, u32[]{:S(2)}, u32[]{:S(2)}) async-start(s32[32,1,4]{2,1,0:T(1,128)} %copy.43), calls=%async_computation | async-start | bytes 32768 | tf_op jit(solution)/shard_map/all_to_all | solution.py:118
  14.0 0.8 fusion.24
  14.8 0.8 compare_and_fusion.3
  15.6 0.8 copy.42
  16.4 0.7 fusion.21
  17.0 0.6 gather_fusion
  17.7 1.5 %copy_bitcast_fusion.2 = (f32[2,64,128]{2,1,0:T(8,128)}, f32[2,64,128]{2,1,0:T(8,128)}) fusion(f32[1,2,64,128]{3,1,2,0:T(2,128)} %bitcast.104, f32[1,2,64,128]{3,1,2,0:T(2,128)} %bitcast.105), kind=kLoop, calls=%fused_computation.16 | loop fusion | bytes 262144 | tf_op jit(solution)/shard_map/reshape | solution.py:91
  19.2 0.7 iota_reduce_fusion
  19.9 1.3 %reshape.275.rde_ref = f32[48]{0:T(128)} reshape(f32[3,16]{1,0:T(4,128)} %param.19) | data formatting | bytes 384 | tf_op jit(solution)/shard_map/reshape | solution.py:88
  21.2 1.5 %copy.67 = f32[1,3,64,128]{3,2,1,0:T(8,128)} copy(f32[1,3,64,128]{3,1,2,0:T(4,128)} %bitcast.102) | data formatting | bytes 196608
  22.7 1.9 %shard_map.138 = f32[6,2,64,128]{3,2,1,0:T(8,128)} custom-call(f32[16]{0:T(128)} %cse_ref.1, f32[48]{0:T(128)} %reshape.275.rde_ref, s32[64,128]{1,0:T(8,128)} %bitcast.106, f32[2,64,128]{2,1,0:T(8,128)} %get-tuple-element.19.warm_ref, f32[2,64,128]{2,1,0:T(8,128)} %get-tuple-element.18.wet_ref, f32[3,64,128]{2,1,0:T(8,128)} %bitcast.97), custom_call_target="tpu_custom_call" | custom-call | tf_op jit(solution)/shard_map/pallas_call | solution.py:81
  24.6 1.3 %copy.46 = f32[6,128,128]{2,0,1:T(8,128)S(1)} copy(f32[6,128,128]{2,1,0:T(8,128)} %bitcast.95) | data formatting | bytes 786432 | tf_op jit(solution)/shard_map/reshape | solution.py:129
  26.0 0.5 broadcast.259
  26.5 0.7 reduce.23
  27.2 0.1 all_to_all.31
  27.3 0.1 copy.45
  27.4 0.8 gather_fusion.1
  28.2 0.9 copy_select_fusion
  29.1 9.2 %all-to-all-start.1 = ((f32[6,32,4,128]{3,2,0,1:T(4,128)}), f32[6,32,4,128]{3,2,0,1:T(4,128)S(1)}, u32[]{:S(2)}, u32[]{:S(2)}) async-start(f32[6,32,4,128]{3,2,0,1:T(4,128)} %copy_select_fusion), calls=%async_computation.1 | async-start | bytes 786432 | tf_op jit(solution)/shard_map/all_to_all | solution.py:131
  38.3 0.7 slice_bitcast_fusion.2
  39.0 12.3 %all-to-all-done.1 = f32[6,32,4,128]{3,2,0,1:T(4,128)S(1)} async-done(((f32[6,32,4,128]{3,2,0,1:T(4,128)}), f32[6,32,4,128]{3,2,0,1:T(4,128)S(1)}, u32[]{:S(2)}, u32[]{:S(2)}) %all-to-all-start.1) | async-done | bytes 393248 | tf_op jit(solution)/shard_map/all_to_all | solution.py:131
  51.4 0.7 gather_fusion.2
  52.1 0.1 fusion.10
  52.2 4.4 %fusion.6 = f32[128,1,128]{2,1,0:T(1,128)S(1)} fusion(bf16[128,128,128]{2,1,0:T(8,128)(2,1)} %param.11, bf16[128,128,1]{1,0,2:T(8,128)(2,1)S(1)} %fusion.10), kind=kOutput, calls=%fused_computation.20 | convolution fusion | flops 4194304 | bytes 4292608 | tf_op jit(solution)/shard_map/bij,bj->bi/dot_general | solution.py:144
  56.6 0.2 fusion.16
  56.8 0.7 broadcast_in_dim.89
  57.6 7.7 %all-to-all-start.2 = ((f32[8,80,128]{2,1,0:T(8,128)}), f32[8,80,128]{2,1,0:T(8,128)S(1)}, u32[]{:S(2)}, u32[]{:S(2)}) async-start(f32[8,80,128]{2,1,0:T(8,128)} %broadcast_in_dim.89), calls=%async_computation.2 | async-start | bytes 655360 | tf_op jit(solution)/shard_map/all_to_all | solution.py:155
  65.4 0.2 slice.55
  65.5 6.9 %all-to-all-done.2 = f32[8,80,128]{2,1,0:T(8,128)S(1)} async-done(((f32[8,80,128]{2,1,0:T(8,128)}), f32[8,80,128]{2,1,0:T(8,128)S(1)}, u32[]{:S(2)}, u32[]{:S(2)}) %all-to-all-start.2) | async-done | bytes 327712 | tf_op jit(solution)/shard_map/all_to_all | solution.py:155
  72.4 1.2 %fusion.18 = (f32[]{:T(128)}, f32[8,128]{1,0:T(8,128)}) fusion(f32[8,128]{1,0:T(8,128)S(1)} %copy-done.2, f32[8,128]{1,0:T(8,128)S(1)} %copy-done.3, f32[64,128]{1,0:T(8,128)S(1)} %slice_reduce_fusion, s32[]{:T(128)S(6)} %select_n.141), kind=kLoop, calls=%fused_computation.44 | loop fusion | flops 4095 | bytes 16392 | tf_op jit(solution)/shard_map/reduce_sum | solution.py:164
  73.6 0.7 gather_fusion.3
  74.4 0.1 select_bitcast_fusion
  74.4 3.4 %fusion.4 = f32[128,1,128]{2,1,0:T(1,128)S(1)} fusion(bf16[128,128,128]{2,1,0:T(8,128)(2,1)} %param.11, bf16[128,128,1]{1,0,2:T(8,128)(2,1)S(1)} %select_bitcast_fusion), kind=kOutput, calls=%fused_computation.18 | convolution fusion | flops 4194304 | bytes 4292608 | tf_op jit(solution)/shard_map/bij,bi->bj/dot_general | solution.py:167
  77.8 1.0 scatter_custom_fusion
  78.9 0.7 fusion
  80.4 0.7 all_to_all.34
  81.1 3.9 %all-to-all-start.3 = ((f32[32,1,577]{2,1,0:T(1,128)}), f32[32,1,577]{2,1,0:T(1,128)S(1)}, u32[]{:S(2)}, u32[]{:S(2)}) async-start(f32[32,1,577]{2,1,0:T(1,128)} %all_to_all.34), calls=%async_computation.3 | async-start | bytes 163840 | tf_op jit(solution)/shard_map/all_to_all | solution.py:183
  85.1 0.6 multiply_reduce_fusion
  85.7 8.3 %all-to-all-done.3 = f32[32,1,577]{2,1,0:T(1,128)S(1)} async-done(((f32[32,1,577]{2,1,0:T(1,128)}), f32[32,1,577]{2,1,0:T(1,128)S(1)}, u32[]{:S(2)}, u32[]{:S(2)}) %all-to-all-start.3) | async-done | bytes 73888 | tf_op jit(solution)/shard_map/all_to_all | solution.py:183
  94.1 0.6 broadcast_in_dim.97
  94.7 5.8 %all-to-all-start.4 = ((f32[8,1,65]{2,1,0:T(1,128)}), f32[8,1,65]{2,1,0:T(1,128)S(1)}, u32[]{:S(2)}, u32[]{:S(2)}) async-start(f32[8,1,65]{2,1,0:T(1,128)} %broadcast_in_dim.97), calls=%async_computation.4 | async-start | bytes 8192 | tf_op jit(solution)/shard_map/all_to_all | solution.py:185
  100.5 0.6 multiply_reduce_fusion.1
  102.4 1.0 scatter_custom_fusion.1
  103.4 0.7 reshape.286
  104.1 1.0 all-to-all-done.4
  105.1 0.6 slice.61
  106.4 0.6 fusion.19
  (39 shorter events, 0.6 us)
Async XLA Ops:
  2.0 23.9 %all-to-all-start = ((s32[32,1,4]{2,1,0:T(1,128)}), s32[32,1,4]{2,1,0:T(1,128)S(1)}, u32[]{:S(2)}, u32[]{:S(2)}) async-start(s32[32,1,4]{2,1,0:T(1,128)} %copy.43), calls=%async_computation | async-start | bytes 32768 | tf_op jit(solution)/shard_map/all_to_all | solution.py:118
  24.6 32.2 %copy-start.2 = (f32[8,128]{1,0:T(8,128)S(1)}, f32[8,128]{1,0:T(8,128)}, u32[]{:S(2)}) copy-start(f32[8,128]{1,0:T(8,128)} %param.21) | copy-start | bytes 12292
  24.6 32.2 %copy-start.3 = (f32[8,128]{1,0:T(8,128)S(1)}, f32[8,128]{1,0:T(8,128)}, u32[]{:S(2)}) copy-start(f32[8,128]{1,0:T(8,128)} %param.20) | copy-start | bytes 12292
  29.1 22.3 %all-to-all-start.1 = ((f32[6,32,4,128]{3,2,0,1:T(4,128)}), f32[6,32,4,128]{3,2,0,1:T(4,128)S(1)}, u32[]{:S(2)}, u32[]{:S(2)}) async-start(f32[6,32,4,128]{3,2,0,1:T(4,128)} %copy_select_fusion), calls=%async_computation.1 | async-start | bytes 786432 | tf_op jit(solution)/shard_map/all_to_all | solution.py:131
  51.4 23.0 %copy-start = (f32[6,32,4,128]{3,2,0,1:T(4,128)}, f32[6,32,4,128]{3,2,0,1:T(4,128)S(1)}, u32[]{:S(2)}) copy-start(f32[6,32,4,128]{3,2,0,1:T(4,128)S(1)} %all-to-all-done.1) | copy-start | bytes 1179652
  57.6 27.5 %copy-start.1 = (f32[3,16]{1,0:T(4,128)S(1)}, f32[3,16]{1,0:T(4,128)}, u32[]{:S(2)}) copy-start(f32[3,16]{1,0:T(4,128)} %param.19) | copy-start | bytes 580
  57.6 14.8 %all-to-all-start.2 = ((f32[8,80,128]{2,1,0:T(8,128)}), f32[8,80,128]{2,1,0:T(8,128)S(1)}, u32[]{:S(2)}, u32[]{:S(2)}) async-start(f32[8,80,128]{2,1,0:T(8,128)} %broadcast_in_dim.89), calls=%async_computation.2 | async-start | bytes 655360 | tf_op jit(solution)/shard_map/all_to_all | solution.py:155
  65.3 35.2 %copy-start.4 = (f32[16]{0:T(128)S(1)}, f32[16]{0:T(128)}, u32[]{:S(2)}) copy-start(f32[16]{0:T(128)} %cse_ref.1) | copy-start | bytes 196
  74.3 4.5 %slice-start = ((f32[6,32,4,128]{3,2,0,1:T(4,128)}), f32[1,32,4,128]{3,2,0,1:T(4,128)S(1)}, s32[]{:S(2)}) async-start(f32[6,32,4,128]{3,2,0,1:T(4,128)} %copy-done), calls=%async_computation.5 | async-start | bytes 131072 | tf_op jit(solution)/shard_map/slice | solution.py:173
  81.1 12.9 %all-to-all-start.3 = ((f32[32,1,577]{2,1,0:T(1,128)}), f32[32,1,577]{2,1,0:T(1,128)S(1)}, u32[]{:S(2)}, u32[]{:S(2)}) async-start(f32[32,1,577]{2,1,0:T(1,128)} %all_to_all.34), calls=%async_computation.3 | async-start | bytes 163840 | tf_op jit(solution)/shard_map/all_to_all | solution.py:183
  94.7 10.4 %all-to-all-start.4 = ((f32[8,1,65]{2,1,0:T(1,128)}), f32[8,1,65]{2,1,0:T(1,128)S(1)}, u32[]{:S(2)}, u32[]{:S(2)}) async-start(f32[8,1,65]{2,1,0:T(1,128)} %broadcast_in_dim.97), calls=%async_computation.4 | async-start | bytes 8192 | tf_op jit(solution)/shard_map/all_to_all | solution.py:185

commit v6 on v5

--- a/solution.py
+++ b/solution.py
@@ -47,22 +47,26 @@
         hit = cat == c
         picked_q = jnp.where(hit, cse_ref[c], picked_q)
         for p in range(3):
-            picked[p] = jnp.where(hit, rde_ref[p * nclass + c], picked[p])
+            picked[p] = jnp.where(hit, rde_ref[p, c], picked[p])
     log_q = LOG_BASE_Q + picked_q
     base = (0.6, 0.25, 0.1)
-    held = [base[p] * jnp.exp(picked[p]) * carbon_ref[p] for p in range(3)]
+    held = [base[p] * jnp.exp(picked[p]) * carbon_ref[p : p + 1, :] for p in range(3)]
     category = cat.astype(jnp.float32)
     for t in range(warm_ref.shape[0]):
-        tau = (warm_ref[t] - BASELINE_CELSIUS) / 10.0
-        modifier = jnp.exp(log_q * tau) * wet_ref[t]
+        tau = (warm_ref[t : t + 1, :] - BASELINE_CELSIUS) / 10.0
+        modifier = jnp.exp(log_q * tau) * wet_ref[t : t + 1, :]
         parts = [held[p] * modifier for p in range(3)]
         flux = parts[0] + parts[1] + parts[2]
-        out_ref[0, t] = flux.astype(jnp.bfloat16).astype(jnp.float32)
-        out_ref[1, t] = flux * tau
-        out_ref[2, t] = parts[0]
-        out_ref[3, t] = parts[1]
-        out_ref[4, t] = parts[2]
-        out_ref[5, t] = category
+        fields = (
+            flux.astype(jnp.bfloat16).astype(jnp.float32),
+            flux * tau,
+            parts[0],
+            parts[1],
+            parts[2],
+            category,
+        )
+        for q, value in enumerate(fields):
+            out_ref[q, t : t + 1, :] = value
 
 
 def owner_fields(
@@ -72,24 +76,22 @@
     location_category,
     category_sensitivity_effect,
     reservoir_decay_effect,
-    tile,
 ):
     epochs, cells = ground_warmth_celsius.shape
-    rows = cells // tile
     smem = pl.BlockSpec(memory_space=pltpu.SMEM)
     vmem = pl.BlockSpec(memory_space=pltpu.VMEM)
     return pl.pallas_call(
         _fields_kernel,
-        out_shape=jax.ShapeDtypeStruct((6, epochs, rows, tile), jnp.float32),
+        out_shape=jax.ShapeDtypeStruct((6, epochs, cells), jnp.float32),
         in_specs=[smem, smem, vmem, vmem, vmem, vmem],
         out_specs=vmem,
     )(
         category_sensitivity_effect,
-        reservoir_decay_effect.reshape(-1),
-        location_category.reshape(rows, tile),
-        ground_warmth_celsius.reshape(epochs, rows, tile),
-        wetness_factor.reshape(epochs, rows, tile),
-        carbon_reservoirs.reshape(3, rows, tile),
+        reservoir_decay_effect,
+        location_category.reshape(1, cells),
+        ground_warmth_celsius,
+        wetness_factor,
+        carbon_reservoirs,
     )
 
 
@@ -125,12 +127,14 @@
         location_category,
         category_sensitivity_effect,
         reservoir_decay_effect,
-        tile,
     ).reshape(6, local_ids, tile)
-    answer = jnp.take(own_fields, jnp.where(live, requests, 0).reshape(-1), axis=1)
+    asked = (
+        requests.reshape(-1)[:, None] == jnp.arange(local_ids, dtype=jnp.int32)[None, :]
+    ).astype(jnp.float32)
+    answer = jnp.einsum("rl,qlc->rqc", asked, own_fields, precision=lax.Precision.HIGHEST)
     received = lax.all_to_all(
-        answer.reshape(6, n_snd, cap, tile), "snd", 1, 1, tiled=True
-    ).reshape(6, n_snd * cap, tile)
+        answer.reshape(n_snd, cap * 6 * tile), "snd", 0, 0, tiled=True
+    ).reshape(n_snd * cap, 6, tile)
 
     block_row = block_placement_table[0]
     block_tile = block_placement_table[1]
@@ -140,7 +144,7 @@
     listed = jnp.take(needed_tile_lists, owner, axis=0)
     within = jnp.argmax(listed == wanted[:, None], axis=1).astype(jnp.int32)
     position = owner * cap + within
-    vectors = jnp.take(received[0], position, axis=0).astype(jnp.bfloat16)
+    vectors = jnp.take(received[:, 0], position, axis=0).astype(jnp.bfloat16)
     contrib = jnp.einsum(
         "bij,bj->bi", sensitivity_blocks, vectors, preferred_element_type=jnp.float32
     )
@@ -170,10 +174,12 @@
     outgoing = jax.ops.segment_sum(block_grads, position, num_segments=n_snd * cap)
 
     class_hot = (
-        received[5].reshape(-1)[:, None] == jnp.arange(nclass, dtype=jnp.float32)[None, :]
+        received[:, 5][:, :, None] == jnp.arange(nclass, dtype=jnp.float32)[None, None, :]
     ).astype(jnp.float32)
-    weighted_fields = (outgoing[None] * received[1:5]).reshape(4, -1)
-    class_part = jnp.dot(weighted_fields, class_hot, precision=lax.Precision.HIGHEST)
+    weighted_fields = outgoing[:, None, :] * received[:, 1:5]
+    class_part = jnp.einsum(
+        "pqc,pck->qk", weighted_fields, class_hot, precision=lax.Precision.HIGHEST
+    )
     mine = jnp.concatenate([class_part.reshape(-1), misfit[None]])
     width = mine.shape[0]
     parcel = jnp.concatenate(

time: 109 us -> 106 us (0.972)
  local copies, waits for them, and re-layouts: 15.8 us -> 12 us
    reshape x2 -> x1, local copies, waits for them, and re-layouts: 2.78 us -> 0.2 us  [shards(): received = lax.all_to_all(answer.reshape(n_snd, cap * 6 * tile), 'snd', 0...]
    all_to_all x1, waiting for transfers between devices: 8.34 us -> 6.32 us  [shards(): incoming = lax.all_to_all(parcel, 'snd', 0, 0, tiled=True)]
    all_to_all x1, waiting for transfers between devices: 0.95 us -> 2.88 us  [shards(): lax.all_to_all(jnp.broadcast_to(column[None], (n_map, width)), 'map', 0,...]
    unnamed x13 -> x10, local copies, waits for them, and re-layouts: 2.33 us -> 0.79 us
    all_to_all x0 -> x1, local copies, waits for them, and re-layouts: none -> 1.13 us  [shards(): lax.all_to_all(answer.reshape(n_snd, cap * 6 * tile), 'snd', 0, 0, tiled=...]
  transfers between devices with their start and end apart: 5 -> 5, of which waited for: 4 -> 5; matrix products, arithmetic and copies ran while one was open for 13% -> 9% of each run, Pallas kernels for 2% -> 2%
where the time goes in v6:
time: 106 us; the launch traced here: 105 us
  starting transfers between devices  37.7 us (36%)
  waiting for transfers between devices  29.5 us (28%)
  local copies, waits for them, and re-layouts  12 us (11%)
  other arithmetic  9.94 us (9%)
  matrix products  9.24 us (9%)
  between operations  4.64 us (4%)
  Pallas kernels  1.96 us (2%)
    all_to_all x1, waiting for transfers between devices, shards(): lax.all_to_all(answer.reshape(n_snd, cap * 6 * tile), 'snd', 0, 0, tiled=...  12.3 us
    all_to_all x1, starting transfers between devices, shards(): requests = lax.all_to_all(needed_tile_lists, 'snd', 0, 0, tiled=True)  12 us
    all_to_all x1, starting transfers between devices, shards(): lax.all_to_all(answer.reshape(n_snd, cap * 6 * tile), 'snd', 0, 0, tiled=...  8.38 us
    all_to_all x1, starting transfers between devices, shards(): lax.all_to_all(jnp.broadcast_to(payload[None], (n_map,) + payload.shape),...  7.56 us
    all_to_all x1, waiting for transfers between devices, shards(): lax.all_to_all(jnp.broadcast_to(payload[None], (n_map,) + payload.shape),...  7.11 us
    all_to_all x1, waiting for transfers between devices, shards(): incoming = lax.all_to_all(parcel, 'snd', 0, 0, tiled=True)  6.32 us
    all_to_all x1, starting transfers between devices, shards(): lax.all_to_all(jnp.broadcast_to(column[None], (n_map, width)), 'map', 0,...  5.82 us
    dot_general x1, matrix products, shards(): jnp.einsum('bij,bj->bi', sensitivity_blocks, vectors, preferred_element_t...  4.43 us
  transfers between devices with their start and end apart: 5, of which 5 were waited for; matrix products, arithmetic and copies ran while one was open for 9% of the time, Pallas kernels for 2%

profile of v6, /device:TPU:1, one launch (start us, length us, event | category | flops | bytes accessed | tf_op | source)
XLA Modules:
  0.0 105.0 jit_solution(12679185767085953187)
XLA Ops:
  0.6 1.4 %copy.38 = s32[32,1,4]{2,1,0:T(1,128)} copy(s32[32,1,4]{0,2,1:T(4,128)} %bitcast.90) | data formatting | bytes 1024 | tf_op jit(solution)/shard_map/all_to_all | solution.py:120
  2.0 12.0 %all-to-all-start = ((s32[32,1,4]{2,1,0:T(1,128)}), s32[32,1,4]{2,1,0:T(1,128)S(1)}, u32[]{:S(2)}, u32[]{:S(2)}) async-start(s32[32,1,4]{2,1,0:T(1,128)} %copy.38), calls=%async_computation | async-start | bytes 32768 | tf_op jit(solution)/shard_map/all_to_all | solution.py:120
  14.0 0.8 fusion.26
  14.8 0.8 compare_and_fusion.2
  15.6 0.8 copy.37
  16.4 0.7 fusion.23
  17.0 0.6 gather_fusion
  17.7 0.7 iota_reduce_fusion
  18.4 2.0 %shard_map.138 = f32[6,2,8192]{2,1,0:T(2,128)} custom-call(f32[16]{0:T(128)} %cse_ref.1, f32[3,16]{1,0:T(4,128)} %rde_ref.1, s32[1,8192]{1,0:T(1,128)} %bitcast.88, f32[2,8192]{1,0:T(2,128)} %warm_ref.1, f32[2,8192]{1,0:T(2,128)} %wet_ref.1, f32[3,8192]{1,0:T(4,128)} %carbon_ref.1), custom_call_target="tpu_custom_call" | custom-call | tf_op jit(solution)/shard_map/pallas_call | solution.py:83
  20.4 1.3 %reshape.230 = f32[6,128,128]{2,1,0:T(8,128)S(1)} reshape(f32[6,2,8192]{2,1,0:T(2,128)} %shard_map.138) | data formatting | bytes 786432 | tf_op jit(solution)/shard_map/reshape | solution.py:130
  21.7 0.9 all-to-all-done
  22.5 0.5 broadcast.204
  23.1 0.7 reduce.26
  23.8 0.1 eq.63
  23.9 0.4 fusion.7
  24.2 0.2 copy.39
  24.5 1.1 %all_to_all.39 = f32[32,1,3072]{2,1,0:T(1,128)} reshape(f32[128,6,128]{2,1,0:T(8,128)S(1)} %copy.39) | data formatting | bytes 786432 | tf_op jit(solution)/shard_map/all_to_all | solution.py:135
  25.6 8.4 %all-to-all-start.1 = ((f32[32,1,3072]{2,1,0:T(1,128)}), f32[32,1,3072]{2,1,0:T(1,128)S(1)}, u32[]{:S(2)}, u32[]{:S(2)}) async-start(f32[32,1,3072]{2,1,0:T(1,128)} %all_to_all.39), calls=%async_computation.1 | async-start | bytes 786432 | tf_op jit(solution)/shard_map/all_to_all | solution.py:135
  34.1 0.7 slice_bitcast_fusion.2
  34.8 12.3 %all-to-all-done.1 = f32[32,1,3072]{2,1,0:T(1,128)S(1)} async-done(((f32[32,1,3072]{2,1,0:T(1,128)}), f32[32,1,3072]{2,1,0:T(1,128)S(1)}, u32[]{:S(2)}, u32[]{:S(2)}) %all-to-all-start.1) | async-done | bytes 393248 | tf_op jit(solution)/shard_map/all_to_all | solution.py:135
  47.1 0.9 reduce.20
  48.0 0.2 reshape.231
  48.2 0.1 fusion.27
  48.3 0.6 gather_fusion.1
  49.0 0.1 fusion.11
  49.1 4.4 %fusion.4 = f32[128,1,128]{2,1,0:T(1,128)S(1)} fusion(bf16[128,128,128]{2,1,0:T(8,128)(2,1)} %param.11, bf16[128,128,1]{1,0,2:T(8,128)(2,1)S(1)} %fusion.11), kind=kOutput, calls=%fused_computation.15 | convolution fusion | flops 4194304 | bytes 4292608 | tf_op jit(solution)/shard_map/bij,bj->bi/dot_general | solution.py:148
  53.5 0.2 fusion.18
  53.7 0.7 broadcast_in_dim.79
  54.5 7.6 %all-to-all-start.2 = ((f32[8,80,128]{2,1,0:T(8,128)}), f32[8,80,128]{2,1,0:T(8,128)S(1)}, u32[]{:S(2)}, u32[]{:S(2)}) async-start(f32[8,80,128]{2,1,0:T(8,128)} %broadcast_in_dim.79), calls=%async_computation.2 | async-start | bytes 655360 | tf_op jit(solution)/shard_map/all_to_all | solution.py:159
  62.0 7.1 %all-to-all-done.2 = f32[8,80,128]{2,1,0:T(8,128)S(1)} async-done(((f32[8,80,128]{2,1,0:T(8,128)}), f32[8,80,128]{2,1,0:T(8,128)S(1)}, u32[]{:S(2)}, u32[]{:S(2)}) %all-to-all-start.2) | async-done | bytes 327712 | tf_op jit(solution)/shard_map/all_to_all | solution.py:159
  69.2 1.2 %fusion.20 = (f32[]{:T(128)}, f32[8,128]{1,0:T(8,128)}) fusion(f32[8,128]{1,0:T(8,128)S(1)} %copy-done.1, f32[8,128]{1,0:T(8,128)S(1)} %copy-done.2, f32[64,128]{1,0:T(8,128)S(1)} %slice_reduce_fusion, s32[]{:T(128)S(6)} %select_n.99), kind=kLoop, calls=%fused_computation.41 | loop fusion | flops 4095 | bytes 16392 | tf_op jit(solution)/shard_map/reduce_sum | solution.py:168
  70.4 0.7 gather_fusion.2
  71.2 3.4 %fusion.2 = f32[128,1,128]{2,1,0:T(1,128)S(1)} fusion(bf16[128,128,128]{2,1,0:T(8,128)(2,1)} %param.11, bf16[128,128,1]{1,0,2:T(8,128)(2,1)S(1)} %select_bitcast_fusion), kind=kOutput, calls=%fused_computation.13 | convolution fusion | flops 4194304 | bytes 4292608 | tf_op jit(solution)/shard_map/bij,bi->bj/dot_general | solution.py:171
  74.6 1.0 scatter_custom_fusion
  75.6 0.9 convolution_bitcast_fusion
  77.4 0.7 all_to_all.35
  78.0 3.9 %all-to-all-start.3 = ((f32[32,1,577]{2,1,0:T(1,128)}), f32[32,1,577]{2,1,0:T(1,128)S(1)}, u32[]{:S(2)}, u32[]{:S(2)}) async-start(f32[32,1,577]{2,1,0:T(1,128)} %all_to_all.35), calls=%async_computation.3 | async-start | bytes 163840 | tf_op jit(solution)/shard_map/all_to_all | solution.py:189
  82.0 0.6 multiply_reduce_fusion
  83.3 0.6 multiply_reduce_fusion.1
  84.5 0.1 all_to_all.34
  84.6 6.3 %all-to-all-done.3 = f32[32,1,577]{2,1,0:T(1,128)S(1)} async-done(((f32[32,1,577]{2,1,0:T(1,128)}), f32[32,1,577]{2,1,0:T(1,128)S(1)}, u32[]{:S(2)}, u32[]{:S(2)}) %all-to-all-start.3) | async-done | bytes 73888 | tf_op jit(solution)/shard_map/all_to_all | solution.py:189
  91.0 0.6 broadcast_in_dim.88
  91.6 5.8 %all-to-all-start.4 = ((f32[8,1,65]{2,1,0:T(1,128)}), f32[8,1,65]{2,1,0:T(1,128)S(1)}, u32[]{:S(2)}, u32[]{:S(2)}) async-start(f32[8,1,65]{2,1,0:T(1,128)} %broadcast_in_dim.88), calls=%async_computation.4 | async-start | bytes 8192 | tf_op jit(solution)/shard_map/all_to_all | solution.py:191
  97.4 1.0 scatter_custom_fusion.1
  98.4 0.7 reshape.237
  99.1 2.9 %all-to-all-done.4 = f32[8,1,65]{2,1,0:T(1,128)S(1)} async-done(((f32[8,1,65]{2,1,0:T(1,128)}), f32[8,1,65]{2,1,0:T(1,128)S(1)}, u32[]{:S(2)}, u32[]{:S(2)}) %all-to-all-start.4) | async-done | bytes 2112 | tf_op jit(solution)/shard_map/all_to_all | solution.py:191
  102.0 0.6 slice.55
  103.3 0.6 fusion.21
  (29 shorter events, 0.5 us)
Async XLA Ops:
  2.0 20.5 %all-to-all-start = ((s32[32,1,4]{2,1,0:T(1,128)}), s32[32,1,4]{2,1,0:T(1,128)S(1)}, u32[]{:S(2)}, u32[]{:S(2)}) async-start(s32[32,1,4]{2,1,0:T(1,128)} %copy.38), calls=%async_computation | async-start | bytes 32768 | tf_op jit(solution)/shard_map/all_to_all | solution.py:120
  24.5 29.2 %copy-start.1 = (f32[8,128]{1,0:T(8,128)S(1)}, f32[8,128]{1,0:T(8,128)}, u32[]{:S(2)}) copy-start(f32[8,128]{1,0:T(8,128)} %param.21) | copy-start | bytes 12292
  24.5 29.2 %copy-start.2 = (f32[8,128]{1,0:T(8,128)S(1)}, f32[8,128]{1,0:T(8,128)}, u32[]{:S(2)}) copy-start(f32[8,128]{1,0:T(8,128)} %param.20) | copy-start | bytes 12292
  25.6 21.4 %all-to-all-start.1 = ((f32[32,1,3072]{2,1,0:T(1,128)}), f32[32,1,3072]{2,1,0:T(1,128)S(1)}, u32[]{:S(2)}, u32[]{:S(2)}) async-start(f32[32,1,3072]{2,1,0:T(1,128)} %all_to_all.39), calls=%async_computation.1 | async-start | bytes 786432 | tf_op jit(solution)/shard_map/all_to_all | solution.py:135
  53.5 28.5 %copy-start = (f32[3,16]{1,0:T(4,128)S(1)}, f32[3,16]{1,0:T(4,128)}, u32[]{:S(2)}) copy-start(f32[3,16]{1,0:T(4,128)} %rde_ref.1) | copy-start | bytes 580
  53.5 29.7 %copy-start.3 = (f32[16]{0:T(128)S(1)}, f32[16]{0:T(128)}, u32[]{:S(2)}) copy-start(f32[16]{0:T(128)} %cse_ref.1) | copy-start | bytes 196
  54.5 14.7 %all-to-all-start.2 = ((f32[8,80,128]{2,1,0:T(8,128)}), f32[8,80,128]{2,1,0:T(8,128)S(1)}, u32[]{:S(2)}, u32[]{:S(2)}) async-start(f32[8,80,128]{2,1,0:T(8,128)} %broadcast_in_dim.79), calls=%async_computation.2 | async-start | bytes 655360 | tf_op jit(solution)/shard_map/all_to_all | solution.py:159
  78.0 12.9 %all-to-all-start.3 = ((f32[32,1,577]{2,1,0:T(1,128)}), f32[32,1,577]{2,1,0:T(1,128)S(1)}, u32[]{:S(2)}, u32[]{:S(2)}) async-start(f32[32,1,577]{2,1,0:T(1,128)} %all_to_all.35), calls=%async_computation.3 | async-start | bytes 163840 | tf_op jit(solution)/shard_map/all_to_all | solution.py:189
  91.6 10.4 %all-to-all-start.4 = ((f32[8,1,65]{2,1,0:T(1,128)}), f32[8,1,65]{2,1,0:T(1,128)S(1)}, u32[]{:S(2)}, u32[]{:S(2)}) async-start(f32[8,1,65]{2,1,0:T(1,128)} %broadcast_in_dim.88), calls=%async_computation.4 | async-start | bytes 8192 | tf_op jit(solution)/shard_map/all_to_all | solution.py:191

commit v7 on v6

--- a/solution.py
+++ b/solution.py
@@ -132,6 +132,9 @@
         requests.reshape(-1)[:, None] == jnp.arange(local_ids, dtype=jnp.int32)[None, :]
     ).astype(jnp.float32)
     answer = jnp.einsum("rl,qlc->rqc", asked, own_fields, precision=lax.Precision.HIGHEST)
+    answer, block_placement_table, needed_tile_lists = lax.optimization_barrier(
+        (answer, block_placement_table, needed_tile_lists)
+    )
     received = lax.all_to_all(
         answer.reshape(n_snd, cap * 6 * tile), "snd", 0, 0, tiled=True
     ).reshape(n_snd * cap, 6, tile)

time: 106 us -> 105 us (level)
  starting transfers between devices: 37.7 us -> 33.8 us
  waiting for transfers between devices: 29.5 us -> 32.2 us
    all_to_all x1, waiting for transfers between devices: 0.85 us -> 5.2 us  [shards(): requests = lax.all_to_all(needed_tile_lists, 'snd', 0, 0, tiled=True)]
    all_to_all x1, starting transfers between devices: 8.38 us -> 4.16 us  [shards(): lax.all_to_all(answer.reshape(n_snd, cap * 6 * tile), 'snd', 0, 0, tiled=...]
    all_to_all x1, waiting for transfers between devices: 12.3 us -> 10.7 us  [shards(): lax.all_to_all(answer.reshape(n_snd, cap * 6 * tile), 'snd', 0, 0, tiled=...]
  transfers between devices with their start and end apart: 5 -> 5, of which waited for: 5 -> 5; matrix products, arithmetic and copies ran while one was open for 9% -> 6% of each run, Pallas kernels for 2% -> 2%
where the time goes in v7:
time: 105 us; the launch traced here: 104 us
  starting transfers between devices  33.8 us (32%)
  waiting for transfers between devices  32.2 us (31%)
  local copies, waits for them, and re-layouts  12 us (11%)
  other arithmetic  9.98 us (10%)
  matrix products  9.24 us (9%)
  between operations  4.61 us (4%)
  Pallas kernels  1.97 us (2%)
    all_to_all x1, starting transfers between devices, shards(): requests = lax.all_to_all(needed_tile_lists, 'snd', 0, 0, tiled=True)  12 us
    all_to_all x1, waiting for transfers between devices, shards(): lax.all_to_all(answer.reshape(n_snd, cap * 6 * tile), 'snd', 0, 0, tiled=...  10.7 us
    all_to_all x1, starting transfers between devices, shards(): lax.all_to_all(jnp.broadcast_to(payload[None], (n_map,) + payload.shape),...  7.77 us
    all_to_all x1, waiting for transfers between devices, shards(): lax.all_to_all(jnp.broadcast_to(payload[None], (n_map,) + payload.shape),...  7.11 us
    all_to_all x1, waiting for transfers between devices, shards(): incoming = lax.all_to_all(parcel, 'snd', 0, 0, tiled=True)  6.33 us
    all_to_all x1, starting transfers between devices, shards(): lax.all_to_all(jnp.broadcast_to(column[None], (n_map, width)), 'map', 0,...  5.82 us
    all_to_all x1, waiting for transfers between devices, shards(): requests = lax.all_to_all(needed_tile_lists, 'snd', 0, 0, tiled=True)  5.2 us
    dot_general x1, matrix products, shards(): jnp.einsum('bij,bj->bi', sensitivity_blocks, vectors, preferred_element_t...  4.43 us
  transfers between devices with their start and end apart: 5, of which 5 were waited for; matrix products, arithmetic and copies ran while one was open for 6% of the time, Pallas kernels for 2%

profile of v7, /device:TPU:1, one launch (start us, length us, event | category | flops | bytes accessed | tf_op | source)
XLA Modules:
  0.0 103.8 jit_solution(10411846034377499536)
XLA Ops:
  0.6 1.4 %copy.37 = s32[32,1,4]{2,1,0:T(1,128)} copy(s32[32,1,4]{0,2,1:T(4,128)} %bitcast.90) | data formatting | bytes 1024 | tf_op jit(solution)/shard_map/all_to_all | solution.py:120
  2.0 12.0 %all-to-all-start = ((s32[32,1,4]{2,1,0:T(1,128)}), s32[32,1,4]{2,1,0:T(1,128)S(1)}, u32[]{:S(2)}, u32[]{:S(2)}) async-start(s32[32,1,4]{2,1,0:T(1,128)} %copy.37), calls=%async_computation | async-start | bytes 32768 | tf_op jit(solution)/shard_map/all_to_all | solution.py:120
  14.0 2.0 %shard_map.138 = f32[6,2,8192]{2,1,0:T(2,128)} custom-call(f32[16]{0:T(128)} %cse_ref.1, f32[3,16]{1,0:T(4,128)} %rde_ref.1, s32[1,8192]{1,0:T(1,128)} %bitcast.88, f32[2,8192]{1,0:T(2,128)} %warm_ref.1, f32[2,8192]{1,0:T(2,128)} %wet_ref.1, f32[3,8192]{1,0:T(4,128)} %carbon_ref.1), custom_call_target="tpu_custom_call" | custom-call | tf_op jit(solution)/shard_map/pallas_call | solution.py:83
  16.0 1.3 %reshape.230 = f32[6,128,128]{2,1,0:T(8,128)S(1)} reshape(f32[6,2,8192]{2,1,0:T(2,128)} %shard_map.138) | data formatting | bytes 786432 | tf_op jit(solution)/shard_map/reshape | solution.py:130
  17.3 5.2 %all-to-all-done = s32[32,1,4]{2,1,0:T(1,128)S(1)} async-done(((s32[32,1,4]{2,1,0:T(1,128)}), s32[32,1,4]{2,1,0:T(1,128)S(1)}, u32[]{:S(2)}, u32[]{:S(2)}) %all-to-all-start) | async-done | bytes 544 | tf_op jit(solution)/shard_map/all_to_all | solution.py:120
  22.5 0.5 broadcast.204
  23.1 0.7 reduce.26
  23.8 0.1 eq.58
  23.9 0.4 fusion.7
  24.2 0.8 fusion.26
  25.0 0.8 compare_and_fusion.2
  25.8 0.7 fusion.23
  26.5 0.8 copy.38
  27.2 0.2 copy.39
  27.5 1.1 %all_to_all.39 = f32[32,1,3072]{2,1,0:T(1,128)} reshape(f32[128,6,128]{2,1,0:T(8,128)S(1)} %copy.39) | data formatting | bytes 786432 | tf_op jit(solution)/shard_map/all_to_all | solution.py:138
  28.6 4.2 %all-to-all-start.1 = ((f32[32,1,3072]{2,1,0:T(1,128)}), f32[32,1,3072]{2,1,0:T(1,128)S(1)}, u32[]{:S(2)}, u32[]{:S(2)}) async-start(f32[32,1,3072]{2,1,0:T(1,128)} %all_to_all.39), calls=%async_computation.1 | async-start | bytes 786432 | tf_op jit(solution)/shard_map/all_to_all | solution.py:138
  32.8 0.6 gather_fusion
  33.4 0.7 iota_reduce_fusion
  34.2 0.7 slice_bitcast_fusion.2
  34.8 10.7 %all-to-all-done.1 = f32[32,1,3072]{2,1,0:T(1,128)S(1)} async-done(((f32[32,1,3072]{2,1,0:T(1,128)}), f32[32,1,3072]{2,1,0:T(1,128)S(1)}, u32[]{:S(2)}, u32[]{:S(2)}) %all-to-all-start.1) | async-done | bytes 393248 | tf_op jit(solution)/shard_map/all_to_all | solution.py:138
  45.5 0.9 reduce.20
  46.5 0.2 reshape.231
  46.7 0.1 fusion.27
  46.8 0.6 gather_fusion.1
  47.5 0.1 fusion.11
  47.5 4.4 %fusion.4 = f32[128,1,128]{2,1,0:T(1,128)S(1)} fusion(bf16[128,128,128]{2,1,0:T(8,128)(2,1)} %param.11, bf16[128,128,1]{1,0,2:T(8,128)(2,1)S(1)} %fusion.11), kind=kOutput, calls=%fused_computation.15 | convolution fusion | flops 4194304 | bytes 4292608 | tf_op jit(solution)/shard_map/bij,bj->bi/dot_general | solution.py:151
  52.0 0.2 fusion.18
  52.2 0.7 broadcast_in_dim.79
  52.9 7.8 %all-to-all-start.2 = ((f32[8,80,128]{2,1,0:T(8,128)}), f32[8,80,128]{2,1,0:T(8,128)S(1)}, u32[]{:S(2)}, u32[]{:S(2)}) async-start(f32[8,80,128]{2,1,0:T(8,128)} %broadcast_in_dim.79), calls=%async_computation.2 | async-start | bytes 655360 | tf_op jit(solution)/shard_map/all_to_all | solution.py:162
  60.7 7.1 %all-to-all-done.2 = f32[8,80,128]{2,1,0:T(8,128)S(1)} async-done(((f32[8,80,128]{2,1,0:T(8,128)}), f32[8,80,128]{2,1,0:T(8,128)S(1)}, u32[]{:S(2)}, u32[]{:S(2)}) %all-to-all-start.2) | async-done | bytes 327712 | tf_op jit(solution)/shard_map/all_to_all | solution.py:162
  67.8 1.2 %fusion.20 = (f32[]{:T(128)}, f32[8,128]{1,0:T(8,128)}) fusion(f32[8,128]{1,0:T(8,128)S(1)} %copy-done.1, f32[8,128]{1,0:T(8,128)S(1)} %copy-done.2, f32[64,128]{1,0:T(8,128)S(1)} %slice_reduce_fusion, s32[]{:T(128)S(6)} %select_n.99), kind=kLoop, calls=%fused_computation.41 | loop fusion | flops 4095 | bytes 16392 | tf_op jit(solution)/shard_map/reduce_sum | solution.py:171
  69.1 0.7 gather_fusion.2
  69.9 3.4 %fusion.2 = f32[128,1,128]{2,1,0:T(1,128)S(1)} fusion(bf16[128,128,128]{2,1,0:T(8,128)(2,1)} %param.11, bf16[128,128,1]{1,0,2:T(8,128)(2,1)S(1)} %select_bitcast_fusion), kind=kOutput, calls=%fused_computation.13 | convolution fusion | flops 4194304 | bytes 4292608 | tf_op jit(solution)/shard_map/bij,bi->bj/dot_general | solution.py:174
  73.2 1.0 %scatter_custom_fusion = f32[128,128]{1,0:T(8,128)S(1)} fusion(s32[128]{0:T(128)S(1)} %get-tuple-element.15, f32[128,128]{1,0:T(8,128)S(1)} %bitcast.86, f32[]{:T(128)} %constant.96.clone.1), kind=kCustom, calls=%fused_computation.33 | custom fusion | flops 16384 | bytes 65540 | tf_op jit(solution)/shard_map/scatter-add | solution.py:177
  74.3 0.9 convolution_bitcast_fusion
  76.0 0.7 all_to_all.35
  76.7 4.0 %all-to-all-start.3 = ((f32[32,1,577]{2,1,0:T(1,128)}), f32[32,1,577]{2,1,0:T(1,128)S(1)}, u32[]{:S(2)}, u32[]{:S(2)}) async-start(f32[32,1,577]{2,1,0:T(1,128)} %all_to_all.35), calls=%async_computation.3 | async-start | bytes 163840 | tf_op jit(solution)/shard_map/all_to_all | solution.py:192
  80.8 0.6 multiply_reduce_fusion
  82.0 0.6 multiply_reduce_fusion.1
  83.3 0.1 all_to_all.34
  83.4 6.3 %all-to-all-done.3 = f32[32,1,577]{2,1,0:T(1,128)S(1)} async-done(((f32[32,1,577]{2,1,0:T(1,128)}), f32[32,1,577]{2,1,0:T(1,128)S(1)}, u32[]{:S(2)}, u32[]{:S(2)}) %all-to-all-start.3) | async-done | bytes 73888 | tf_op jit(solution)/shard_map/all_to_all | solution.py:192
  89.7 0.6 broadcast_in_dim.88
  90.3 5.8 %all-to-all-start.4 = ((f32[8,1,65]{2,1,0:T(1,128)}), f32[8,1,65]{2,1,0:T(1,128)S(1)}, u32[]{:S(2)}, u32[]{:S(2)}) async-start(f32[8,1,65]{2,1,0:T(1,128)} %broadcast_in_dim.88), calls=%async_computation.4 | async-start | bytes 8192 | tf_op jit(solution)/shard_map/all_to_all | solution.py:194
  96.2 1.0 scatter_custom_fusion.1
  97.2 0.7 reshape.237
  97.9 2.8 %all-to-all-done.4 = f32[8,1,65]{2,1,0:T(1,128)S(1)} async-done(((f32[8,1,65]{2,1,0:T(1,128)}), f32[8,1,65]{2,1,0:T(1,128)S(1)}, u32[]{:S(2)}, u32[]{:S(2)}) %all-to-all-start.4) | async-done | bytes 2112 | tf_op jit(solution)/shard_map/all_to_all | solution.py:194
  100.8 0.6 slice.55
  102.1 0.6 fusion.21
  (29 shorter events, 0.5 us)
Async XLA Ops:
  2.0 20.5 %all-to-all-start = ((s32[32,1,4]{2,1,0:T(1,128)}), s32[32,1,4]{2,1,0:T(1,128)S(1)}, u32[]{:S(2)}, u32[]{:S(2)}) async-start(s32[32,1,4]{2,1,0:T(1,128)} %copy.37), calls=%async_computation | async-start | bytes 32768 | tf_op jit(solution)/shard_map/all_to_all | solution.py:120
  28.6 23.6 %copy-start.1 = (f32[8,128]{1,0:T(8,128)S(1)}, f32[8,128]{1,0:T(8,128)}, u32[]{:S(2)}) copy-start(f32[8,128]{1,0:T(8,128)} %param.21) | copy-start | bytes 12292
  28.6 23.6 %copy-start.2 = (f32[8,128]{1,0:T(8,128)S(1)}, f32[8,128]{1,0:T(8,128)}, u32[]{:S(2)}) copy-start(f32[8,128]{1,0:T(8,128)} %param.20) | copy-start | bytes 12292
  28.6 16.9 %all-to-all-start.1 = ((f32[32,1,3072]{2,1,0:T(1,128)}), f32[32,1,3072]{2,1,0:T(1,128)S(1)}, u32[]{:S(2)}, u32[]{:S(2)}) async-start(f32[32,1,3072]{2,1,0:T(1,128)} %all_to_all.39), calls=%async_computation.1 | async-start | bytes 786432 | tf_op jit(solution)/shard_map/all_to_all | solution.py:138
  52.0 28.8 %copy-start = (f32[3,16]{1,0:T(4,128)S(1)}, f32[3,16]{1,0:T(4,128)}, u32[]{:S(2)}) copy-start(f32[3,16]{1,0:T(4,128)} %rde_ref.1) | copy-start | bytes 580
  52.0 30.0 %copy-start.3 = (f32[16]{0:T(128)S(1)}, f32[16]{0:T(128)}, u32[]{:S(2)}) copy-start(f32[16]{0:T(128)} %cse_ref.1) | copy-start | bytes 196
  52.9 14.9 %all-to-all-start.2 = ((f32[8,80,128]{2,1,0:T(8,128)}), f32[8,80,128]{2,1,0:T(8,128)S(1)}, u32[]{:S(2)}, u32[]{:S(2)}) async-start(f32[8,80,128]{2,1,0:T(8,128)} %broadcast_in_dim.79), calls=%async_computation.2 | async-start | bytes 655360 | tf_op jit(solution)/shard_map/all_to_all | solution.py:162
  76.7 13.0 %all-to-all-start.3 = ((f32[32,1,577]{2,1,0:T(1,128)}), f32[32,1,577]{2,1,0:T(1,128)S(1)}, u32[]{:S(2)}, u32[]{:S(2)}) async-start(f32[32,1,577]{2,1,0:T(1,128)} %all_to_all.35), calls=%async_computation.3 | async-start | bytes 163840 | tf_op jit(solution)/shard_map/all_to_all | solution.py:192
  90.3 10.4 %all-to-all-start.4 = ((f32[8,1,65]{2,1,0:T(1,128)}), f32[8,1,65]{2,1,0:T(1,128)S(1)}, u32[]{:S(2)}, u32[]{:S(2)}) async-start(f32[8,1,65]{2,1,0:T(1,128)} %broadcast_in_dim.88), calls=%async_computation.4 | async-start | bytes 8192 | tf_op jit(solution)/shard_map/all_to_all | solution.py:194

commit v8 on v7

--- a/solution.py
+++ b/solution.py
@@ -117,7 +117,7 @@
     cap = needed_tile_lists.shape[1]
     rows_own = measured_anomaly.shape[0]
     rows_dev = rows_own * n_map
-    requests = lax.all_to_all(needed_tile_lists, "snd", 0, 0, tiled=True)
+    requests = lax.all_to_all(needed_tile_lists, "snd", 0, 0)
     live = requests >= 0
     nclass = category_sensitivity_effect.shape[0]
     own_fields = owner_fields(
@@ -135,9 +135,9 @@
     answer, block_placement_table, needed_tile_lists = lax.optimization_barrier(
         (answer, block_placement_table, needed_tile_lists)
     )
-    received = lax.all_to_all(
-        answer.reshape(n_snd, cap * 6 * tile), "snd", 0, 0, tiled=True
-    ).reshape(n_snd * cap, 6, tile)
+    received = lax.all_to_all(answer.reshape(n_snd, cap * 6, tile), "snd", 0, 0).reshape(
+        n_snd * cap, 6, tile
+    )
 
     block_row = block_placement_table[0]
     block_tile = block_placement_table[1]
@@ -160,7 +160,7 @@
     first = me_map * rows_own
     payload = jnp.concatenate([partial_rows, measured_anomaly, retrieval_precision], axis=0)
     swapped = lax.all_to_all(
-        jnp.broadcast_to(payload[None], (n_map,) + payload.shape), "map", 0, 0, tiled=True
+        jnp.broadcast_to(payload[None], (n_map,) + payload.shape), "map", 0, 0
     )
     model_rows = jnp.sum(swapped[:, :rows_dev], axis=0)
     anomaly_rows = swapped[:, rows_dev : rows_dev + rows_own].reshape(rows_dev, tile)
@@ -185,20 +185,22 @@
     )
     mine = jnp.concatenate([class_part.reshape(-1), misfit[None]])
     width = mine.shape[0]
+    mine = jnp.pad(mine, (0, tile - width))
     parcel = jnp.concatenate(
-        [outgoing.reshape(n_snd, cap * tile), jnp.broadcast_to(mine[None], (n_snd, width))],
+        [
+            outgoing.reshape(n_snd, cap, tile),
+            jnp.broadcast_to(mine[None, None], (n_snd, 1, tile)),
+        ],
         axis=1,
     )
-    incoming = lax.all_to_all(parcel, "snd", 0, 0, tiled=True)
-    column = jnp.sum(incoming[:, cap * tile :], axis=0)
-    gathered = lax.all_to_all(
-        jnp.broadcast_to(column[None], (n_map, width)), "map", 0, 0, tiled=True
-    )
-    totals = jnp.sum(gathered, axis=0)
+    incoming = lax.all_to_all(parcel, "snd", 0, 0)
+    column = jnp.sum(incoming[:, cap], axis=0)
+    gathered = lax.all_to_all(jnp.broadcast_to(column[None], (n_map, tile)), "map", 0, 0)
+    totals = jnp.sum(gathered, axis=0)[:width]
 
     target = jnp.where(live, requests, local_ids).reshape(-1)
     grad_tiles = jax.ops.segment_sum(
-        incoming[:, : cap * tile].reshape(n_snd * cap, tile), target, num_segments=local_ids + 1
+        incoming[:, :cap].reshape(n_snd * cap, tile), target, num_segments=local_ids + 1
     )[:local_ids]
     flux_grad = grad_tiles.reshape(epochs_each_device, locations_each_device)
 

time: 105 us -> 103 us (0.981)
  local copies, waits for them, and re-layouts: 12 us -> 10.9 us
    all_to_all x5 -> x3, local copies, waits for them, and re-layouts: 3.79 us -> 1.98 us  [shards(): requests = lax.all_to_all(needed_tile_lists, 'snd', 0, 0)]
where the time goes in v8:
time: 103 us
  starting transfers between devices  33.6 us (33%)
  waiting for transfers between devices  32.7 us (32%)
  local copies, waits for them, and re-layouts  10.9 us (11%)
  other arithmetic  9.7 us (9%)
  matrix products  9.24 us (9%)
  between operations  4.6 us (4%)
  Pallas kernels  1.97 us (2%)
    all_to_all x1, starting transfers between devices, shards(): requests = lax.all_to_all(needed_tile_lists, 'snd', 0, 0)  12 us
    all_to_all x1, waiting for transfers between devices, shards(): lax.all_to_all(answer.reshape(n_snd, cap * 6, tile), 'snd', 0, 0)  10.7 us
    all_to_all x1, starting transfers between devices, shards(): lax.all_to_all(jnp.broadcast_to(payload[None], (n_map,) + payload.shape),...  7.77 us
    all_to_all x1, waiting for transfers between devices, shards(): lax.all_to_all(jnp.broadcast_to(payload[None], (n_map,) + payload.shape),...  7.11 us
    all_to_all x1, waiting for transfers between devices, shards(): incoming = lax.all_to_all(parcel, 'snd', 0, 0)  6.82 us
    all_to_all x1, starting transfers between devices, shards(): lax.all_to_all(jnp.broadcast_to(column[None], (n_map, tile)), 'map', 0, 0)  5.73 us
    all_to_all x1, waiting for transfers between devices, shards(): requests = lax.all_to_all(needed_tile_lists, 'snd', 0, 0)  5.2 us
    dot_general x1, matrix products, shards(): jnp.einsum('bij,bj->bi', sensitivity_blocks, vectors, preferred_element_t...  4.43 us
  transfers between devices with their start and end apart: 5, of which 5 were waited for; matrix products, arithmetic and copies ran while one was open for 6% of the time, Pallas kernels for 2%

profile of v8, /device:TPU:1, one launch (start us, length us, event | category | flops | bytes accessed | tf_op | source)
XLA Modules:
  0.0 102.7 jit_solution(5568936267844861250)
XLA Ops:
  0.6 1.4 %copy.35 = s32[32,1,4]{2,1,0:T(1,128)} copy(s32[32,1,4]{0,2,1:T(4,128)} %bitcast.89) | data formatting | bytes 1024 | tf_op jit(solution)/shard_map/all_to_all | solution.py:120
  2.0 12.0 %all-to-all-start = ((s32[32,1,4]{2,1,0:T(1,128)}), s32[32,1,4]{2,1,0:T(1,128)S(1)}, u32[]{:S(2)}, u32[]{:S(2)}) async-start(s32[32,1,4]{2,1,0:T(1,128)} %copy.35), calls=%async_computation | async-start | bytes 32768 | tf_op jit(solution)/shard_map/all_to_all | solution.py:120
  14.0 2.0 %shard_map.138 = f32[6,2,8192]{2,1,0:T(2,128)} custom-call(f32[16]{0:T(128)} %cse_ref.1, f32[3,16]{1,0:T(4,128)} %rde_ref.1, s32[1,8192]{1,0:T(1,128)} %bitcast.87, f32[2,8192]{1,0:T(2,128)} %warm_ref.1, f32[2,8192]{1,0:T(2,128)} %wet_ref.1, f32[3,8192]{1,0:T(4,128)} %carbon_ref.1), custom_call_target="tpu_custom_call" | custom-call | tf_op jit(solution)/shard_map/pallas_call | solution.py:83
  16.0 1.3 %reshape.236 = f32[6,128,128]{2,1,0:T(8,128)S(1)} reshape(f32[6,2,8192]{2,1,0:T(2,128)} %shard_map.138) | data formatting | bytes 786432 | tf_op jit(solution)/shard_map/reshape | solution.py:130
  17.3 5.2 %all-to-all-done = s32[32,1,4]{2,1,0:T(1,128)S(1)} async-done(((s32[32,1,4]{2,1,0:T(1,128)}), s32[32,1,4]{2,1,0:T(1,128)S(1)}, u32[]{:S(2)}, u32[]{:S(2)}) %all-to-all-start) | async-done | bytes 544 | tf_op jit(solution)/shard_map/all_to_all | solution.py:120
  22.5 0.5 broadcast.210
  23.1 0.7 reduce.26
  23.8 0.1 eq.58
  23.9 0.4 fusion.7
  24.2 0.8 fusion.27
  25.0 0.8 compare_and_fusion.2
  25.8 0.7 fusion.24
  26.5 0.8 copy.36
  27.2 0.2 copy.37
  27.5 0.8 reshape.237
  28.3 4.0 %all-to-all-start.1 = ((f32[32,24,128]{2,1,0:T(8,128)}), f32[32,24,128]{2,1,0:T(8,128)S(1)}, u32[]{:S(2)}, u32[]{:S(2)}) async-start(f32[32,24,128]{2,1,0:T(8,128)} %reshape.237), calls=%async_computation.1 | async-start | bytes 786432 | tf_op jit(solution)/shard_map/all_to_all | solution.py:138
  32.3 0.6 gather_fusion
  33.0 0.7 iota_reduce_fusion
  33.7 0.7 slice_bitcast_fusion.2
  34.4 10.7 %all-to-all-done.1 = f32[32,24,128]{2,1,0:T(8,128)S(1)} async-done(((f32[32,24,128]{2,1,0:T(8,128)}), f32[32,24,128]{2,1,0:T(8,128)S(1)}, u32[]{:S(2)}, u32[]{:S(2)}) %all-to-all-start.1) | async-done | bytes 393248 | tf_op jit(solution)/shard_map/all_to_all | solution.py:138
  45.1 0.1 fusion.28
  45.3 0.6 gather_fusion.1
  45.9 0.1 fusion.11
  46.0 4.4 %fusion.4 = f32[128,1,128]{2,1,0:T(1,128)S(1)} fusion(bf16[128,128,128]{2,1,0:T(8,128)(2,1)} %param.11, bf16[128,128,1]{1,0,2:T(8,128)(2,1)S(1)} %fusion.11), kind=kOutput, calls=%fused_computation.14 | convolution fusion | flops 4194304 | bytes 4292608 | tf_op jit(solution)/shard_map/bij,bj->bi/dot_general | solution.py:151
  50.4 0.2 fusion.18
  50.7 0.7 broadcast_in_dim.79
  51.4 7.8 %all-to-all-start.2 = ((f32[8,80,128]{2,1,0:T(8,128)}), f32[8,80,128]{2,1,0:T(8,128)S(1)}, u32[]{:S(2)}, u32[]{:S(2)}) async-start(f32[8,80,128]{2,1,0:T(8,128)} %broadcast_in_dim.79), calls=%async_computation.2 | async-start | bytes 655360 | tf_op jit(solution)/shard_map/all_to_all | solution.py:162
  59.2 7.1 %all-to-all-done.2 = f32[8,80,128]{2,1,0:T(8,128)S(1)} async-done(((f32[8,80,128]{2,1,0:T(8,128)}), f32[8,80,128]{2,1,0:T(8,128)S(1)}, u32[]{:S(2)}, u32[]{:S(2)}) %all-to-all-start.2) | async-done | bytes 327712 | tf_op jit(solution)/shard_map/all_to_all | solution.py:162
  66.3 1.2 %fusion.20 = (f32[]{:T(128)}, f32[8,128]{1,0:T(8,128)}) fusion(f32[8,128]{1,0:T(8,128)S(1)} %copy-done.1, f32[8,128]{1,0:T(8,128)S(1)} %copy-done.2, f32[64,128]{1,0:T(8,128)S(1)} %slice_reduce_fusion, s32[]{:T(128)S(6)} %select_n.99), kind=kLoop, calls=%fused_computation.40 | loop fusion | flops 4095 | bytes 16392 | tf_op jit(solution)/shard_map/reduce_sum | solution.py:171
  67.5 0.7 gather_fusion.2
  68.2 0.1 select_bitcast_fusion
  68.3 3.4 %fusion.2 = f32[128,1,128]{2,1,0:T(1,128)S(1)} fusion(bf16[128,128,128]{2,1,0:T(8,128)(2,1)} %param.11, bf16[128,128,1]{1,0,2:T(8,128)(2,1)S(1)} %select_bitcast_fusion), kind=kOutput, calls=%fused_computation.12 | convolution fusion | flops 4194304 | bytes 4292608 | tf_op jit(solution)/shard_map/bij,bi->bj/dot_general | solution.py:174
  71.7 1.0 %scatter_custom_fusion = f32[128,128]{1,0:T(8,128)S(1)} fusion(s32[128]{0:T(128)S(1)} %get-tuple-element.15, f32[128,128]{1,0:T(8,128)S(1)} %bitcast.84, f32[]{:T(128)} %constant.97.clone.1), kind=kCustom, calls=%fused_computation.32 | custom fusion | flops 16384 | bytes 65540 | tf_op jit(solution)/shard_map/scatter-add | solution.py:177
  72.7 0.9 convolution_bitcast_fusion
  73.6 0.1 reshape.242
  74.5 0.7 pad_maximum_fusion
  75.1 4.0 %all-to-all-start.3 = ((f32[32,5,128]{2,1,0:T(8,128)}), f32[32,5,128]{2,1,0:T(8,128)S(1)}, u32[]{:S(2)}, u32[]{:S(2)}) async-start(f32[32,5,128]{2,1,0:T(8,128)} %pad_maximum_fusion), calls=%async_computation.3 | async-start | bytes 262144 | tf_op jit(solution)/shard_map/all_to_all | solution.py:196
  79.2 0.6 multiply_reduce_fusion
  80.5 0.6 multiply_reduce_fusion.1
  81.7 0.1 all_to_all.25
  81.8 6.8 %all-to-all-done.3 = f32[32,5,128]{2,1,0:T(8,128)S(1)} async-done(((f32[32,5,128]{2,1,0:T(8,128)}), f32[32,5,128]{2,1,0:T(8,128)S(1)}, u32[]{:S(2)}, u32[]{:S(2)}) %all-to-all-start.3) | async-done | bytes 81952 | tf_op jit(solution)/shard_map/all_to_all | solution.py:196
  88.7 0.6 broadcast_in_dim.88
  89.3 5.7 %all-to-all-start.4 = ((f32[8,1,128]{2,1,0:T(1,128)}), f32[8,1,128]{2,1,0:T(1,128)S(1)}, u32[]{:S(2)}, u32[]{:S(2)}) async-start(f32[8,1,128]{2,1,0:T(1,128)} %broadcast_in_dim.88), calls=%async_computation.4 | async-start | bytes 8192 | tf_op jit(solution)/shard_map/all_to_all | solution.py:198
  95.0 1.0 scatter_custom_fusion.1
  96.1 0.7 reshape.244
  96.7 2.9 %all-to-all-done.4 = f32[8,1,128]{2,1,0:T(1,128)S(1)} async-done(((f32[8,1,128]{2,1,0:T(1,128)}), f32[8,1,128]{2,1,0:T(1,128)S(1)}, u32[]{:S(2)}, u32[]{:S(2)}) %all-to-all-start.4) | async-done | bytes 4128 | tf_op jit(solution)/shard_map/all_to_all | solution.py:198
  99.6 0.6 slice.66
  101.0 0.6 fusion.21
  (25 shorter events, 0.4 us)
Async XLA Ops:
  2.0 20.5 %all-to-all-start = ((s32[32,1,4]{2,1,0:T(1,128)}), s32[32,1,4]{2,1,0:T(1,128)S(1)}, u32[]{:S(2)}, u32[]{:S(2)}) async-start(s32[32,1,4]{2,1,0:T(1,128)} %copy.35), calls=%async_computation | async-start | bytes 32768 | tf_op jit(solution)/shard_map/all_to_all | solution.py:120
  27.5 23.1 %copy-start.1 = (f32[8,128]{1,0:T(8,128)S(1)}, f32[8,128]{1,0:T(8,128)}, u32[]{:S(2)}) copy-start(f32[8,128]{1,0:T(8,128)} %param.21) | copy-start | bytes 12292
  27.5 23.1 %copy-start.2 = (f32[8,128]{1,0:T(8,128)S(1)}, f32[8,128]{1,0:T(8,128)}, u32[]{:S(2)}) copy-start(f32[8,128]{1,0:T(8,128)} %param.20) | copy-start | bytes 12292
  28.3 16.8 %all-to-all-start.1 = ((f32[32,24,128]{2,1,0:T(8,128)}), f32[32,24,128]{2,1,0:T(8,128)S(1)}, u32[]{:S(2)}, u32[]{:S(2)}) async-start(f32[32,24,128]{2,1,0:T(8,128)} %reshape.237), calls=%async_computation.1 | async-start | bytes 786432 | tf_op jit(solution)/shard_map/all_to_all | solution.py:138
  50.4 28.8 %copy-start = (f32[3,16]{1,0:T(4,128)S(1)}, f32[3,16]{1,0:T(4,128)}, u32[]{:S(2)}) copy-start(f32[3,16]{1,0:T(4,128)} %rde_ref.1) | copy-start | bytes 580
  50.4 30.0 %copy-start.3 = (f32[16]{0:T(128)S(1)}, f32[16]{0:T(128)}, u32[]{:S(2)}) copy-start(f32[16]{0:T(128)} %cse_ref.1) | copy-start | bytes 196
  51.4 14.9 %all-to-all-start.2 = ((f32[8,80,128]{2,1,0:T(8,128)}), f32[8,80,128]{2,1,0:T(8,128)S(1)}, u32[]{:S(2)}, u32[]{:S(2)}) async-start(f32[8,80,128]{2,1,0:T(8,128)} %broadcast_in_dim.79), calls=%async_computation.2 | async-start | bytes 655360 | tf_op jit(solution)/shard_map/all_to_all | solution.py:162
  75.1 13.5 %all-to-all-start.3 = ((f32[32,5,128]{2,1,0:T(8,128)}), f32[32,5,128]{2,1,0:T(8,128)S(1)}, u32[]{:S(2)}, u32[]{:S(2)}) async-start(f32[32,5,128]{2,1,0:T(8,128)} %pad_maximum_fusion), calls=%async_computation.3 | async-start | bytes 262144 | tf_op jit(solution)/shard_map/all_to_all | solution.py:196
  89.3 10.3 %all-to-all-start.4 = ((f32[8,1,128]{2,1,0:T(1,128)}), f32[8,1,128]{2,1,0:T(1,128)S(1)}, u32[]{:S(2)}, u32[]{:S(2)}) async-start(f32[8,1,128]{2,1,0:T(1,128)} %broadcast_in_dim.88), calls=%async_computation.4 | async-start | bytes 8192 | tf_op jit(solution)/shard_map/all_to_all | solution.py:198

commit v9 on v8

--- a/solution.py
+++ b/solution.py
@@ -117,7 +117,8 @@
     cap = needed_tile_lists.shape[1]
     rows_own = measured_anomaly.shape[0]
     rows_dev = rows_own * n_map
-    requests = lax.all_to_all(needed_tile_lists, "snd", 0, 0)
+    lanes = jnp.pad(needed_tile_lists, ((0, 0), (0, tile - cap)))[:, None, :]
+    requests = lax.all_to_all(lanes, "snd", 0, 0)[:, 0, :cap]
     live = requests >= 0
     nclass = category_sensitivity_effect.shape[0]
     own_fields = owner_fields(
@@ -144,10 +145,11 @@
     block_slot = block_placement_table[2]
     owner = block_slot // epochs_each_device
     wanted = (block_slot % epochs_each_device) * tiles_dev + block_tile
-    listed = jnp.take(needed_tile_lists, owner, axis=0)
+    listed = needed_tile_lists.at[owner].get(mode="promise_in_bounds")
     within = jnp.argmax(listed == wanted[:, None], axis=1).astype(jnp.int32)
     position = owner * cap + within
-    vectors = jnp.take(received[:, 0], position, axis=0).astype(jnp.bfloat16)
+    vectors = received[:, 0].at[position].get(mode="promise_in_bounds")
+    vectors = vectors.astype(jnp.bfloat16)
     contrib = jnp.einsum(
         "bij,bj->bi", sensitivity_blocks, vectors, preferred_element_type=jnp.float32
     )
@@ -170,11 +172,13 @@
     diff = model_xco2 - measured_anomaly
     misfit = 0.5 * jnp.sum(retrieval_precision * diff * diff)
 
-    back_rows = jnp.take(weighted_rows, block_row, axis=0)
+    back_rows = weighted_rows.at[block_row].get(mode="promise_in_bounds")
     block_grads = jnp.einsum(
         "bij,bi->bj", sensitivity_blocks, back_rows, preferred_element_type=jnp.float32
     )
-    outgoing = jax.ops.segment_sum(block_grads, position, num_segments=n_snd * cap)
+    outgoing = jax.ops.segment_sum(
+        block_grads, position, num_segments=n_snd * cap, mode="promise_in_bounds"
+    )
 
     class_hot = (
         received[:, 5][:, :, None] == jnp.arange(nclass, dtype=jnp.float32)[None, None, :]
@@ -200,7 +204,10 @@
 
     target = jnp.where(live, requests, local_ids).reshape(-1)
     grad_tiles = jax.ops.segment_sum(
-        incoming[:, :cap].reshape(n_snd * cap, tile), target, num_segments=local_ids + 1
+        incoming[:, :cap].reshape(n_snd * cap, tile),
+        target,
+        num_segments=local_ids + 1,
+        mode="promise_in_bounds",
     )[:local_ids]
     flux_grad = grad_tiles.reshape(epochs_each_device, locations_each_device)
 

time: 103 us -> 101 us (0.981)
  other arithmetic: 9.7 us -> 8.16 us
  local copies, waits for them, and re-layouts: 10.9 us -> 9.73 us
    all_to_all x3 -> x0, local copies, waits for them, and re-layouts: 1.98 us -> none  [shards(): requests = lax.all_to_all(needed_tile_lists, 'snd', 0, 0)]
where the time goes in v9:
time: 101 us
  starting transfers between devices  33.5 us (33%)
  waiting for transfers between devices  33.5 us (33%)
  local copies, waits for them, and re-layouts  9.73 us (10%)
  matrix products  9.24 us (9%)
  other arithmetic  8.16 us (8%)
  between operations  4.6 us (5%)
  Pallas kernels  1.97 us (2%)
    all_to_all x1, starting transfers between devices, shards(): requests = lax.all_to_all(lanes, 'snd', 0, 0)[:, 0, :cap]  12 us
    all_to_all x1, waiting for transfers between devices, shards(): lax.all_to_all(answer.reshape(n_snd, cap * 6, tile), 'snd', 0, 0)  11.5 us
    all_to_all x1, starting transfers between devices, shards(): lax.all_to_all(jnp.broadcast_to(payload[None], (n_map,) + payload.shape),...  7.68 us
    all_to_all x1, waiting for transfers between devices, shards(): lax.all_to_all(jnp.broadcast_to(payload[None], (n_map,) + payload.shape),...  7.11 us
    all_to_all x1, waiting for transfers between devices, shards(): incoming = lax.all_to_all(parcel, 'snd', 0, 0)  6.82 us
    all_to_all x1, starting transfers between devices, shards(): lax.all_to_all(jnp.broadcast_to(column[None], (n_map, tile)), 'map', 0, 0)  5.73 us
    all_to_all x1, waiting for transfers between devices, shards(): requests = lax.all_to_all(lanes, 'snd', 0, 0)[:, 0, :cap]  5.2 us
    dot_general x1, matrix products, shards(): jnp.einsum('bij,bj->bi', sensitivity_blocks, vectors, preferred_element_t...  4.43 us
  transfers between devices with their start and end apart: 5, of which 5 were waited for; matrix products, arithmetic and copies ran while one was open for 6% of the time, Pallas kernels for 2%

profile of v9, /device:TPU:1, one launch (start us, length us, event | category | flops | bytes accessed | tf_op | source)
XLA Modules:
  0.0 100.7 jit_solution(12136791787130106897)
XLA Ops:
  0.6 0.8 copy.35
  1.4 0.6 pad.8
  2.0 12.0 %all-to-all-start = ((s32[32,1,128]{2,1,0:T(1,128)}), s32[32,1,128]{2,1,0:T(1,128)S(1)}, u32[]{:S(2)}, u32[]{:S(2)}) async-start(s32[32,1,128]{2,1,0:T(1,128)} %bitcast), calls=%async_computation | async-start | bytes 32768 | tf_op jit(solution)/shard_map/all_to_all | solution.py:121
  14.1 2.0 %shard_map.138 = f32[6,2,8192]{2,1,0:T(2,128)} custom-call(f32[16]{0:T(128)} %cse_ref.1, f32[3,16]{1,0:T(4,128)} %rde_ref.1, s32[1,8192]{1,0:T(1,128)} %bitcast.92, f32[2,8192]{1,0:T(2,128)} %warm_ref.1, f32[2,8192]{1,0:T(2,128)} %wet_ref.1, f32[3,8192]{1,0:T(4,128)} %carbon_ref.1), custom_call_target="tpu_custom_call" | custom-call | tf_op jit(solution)/shard_map/pallas_call | solution.py:83
  16.0 1.3 %reshape.216 = f32[6,128,128]{2,1,0:T(8,128)S(1)} reshape(f32[6,2,8192]{2,1,0:T(2,128)} %shard_map.138) | data formatting | bytes 786432 | tf_op jit(solution)/shard_map/reshape | solution.py:131
  17.4 5.2 %all-to-all-done = s32[32,1,128]{2,1,0:T(1,128)S(1)} async-done(((s32[32,1,128]{2,1,0:T(1,128)}), s32[32,1,128]{2,1,0:T(1,128)S(1)}, u32[]{:S(2)}, u32[]{:S(2)}) %all-to-all-start) | async-done | bytes 16416 | tf_op jit(solution)/shard_map/all_to_all | solution.py:121
  22.6 0.1 fusion.28
  22.6 0.1 eq.58
  22.7 0.4 fusion.7
  23.1 0.8 fusion.23
  23.9 0.8 fusion.26
  24.7 0.8 copy.38
  25.4 0.2 copy.36
  25.7 0.8 reshape.217
  26.5 4.0 %all-to-all-start.1 = ((f32[32,24,128]{2,1,0:T(8,128)}), f32[32,24,128]{2,1,0:T(8,128)S(1)}, u32[]{:S(2)}, u32[]{:S(2)}) async-start(f32[32,24,128]{2,1,0:T(8,128)} %reshape.217), calls=%async_computation.1 | async-start | bytes 786432 | tf_op jit(solution)/shard_map/all_to_all | solution.py:139
  30.5 0.6 gather_fusion
  31.2 0.7 iota_reduce_fusion
  31.9 11.5 %all-to-all-done.1 = f32[32,24,128]{2,1,0:T(8,128)S(1)} async-done(((f32[32,24,128]{2,1,0:T(8,128)}), f32[32,24,128]{2,1,0:T(8,128)S(1)}, u32[]{:S(2)}, u32[]{:S(2)}) %all-to-all-start.1) | async-done | bytes 393248 | tf_op jit(solution)/shard_map/all_to_all | solution.py:139
  43.4 0.1 reshape.218
  43.4 0.1 fusion.27
  43.5 0.7 gather_fusion.1
  44.2 4.4 %fusion.4 = f32[128,1,128]{2,1,0:T(1,128)S(1)} fusion(bf16[128,128,128]{2,1,0:T(8,128)(2,1)} %param.11, bf16[128,128,1]{1,0,2:T(8,128)(2,1)S(1)} %bitcast.84), kind=kOutput, calls=%fused_computation.14 | convolution fusion | flops 4194304 | bytes 4292608 | tf_op jit(solution)/shard_map/bij,bj->bi/dot_general | solution.py:153
  48.6 0.2 fusion.17
  48.8 0.7 broadcast_in_dim.25
  49.6 7.7 %all-to-all-start.2 = ((f32[8,80,128]{2,1,0:T(8,128)}), f32[8,80,128]{2,1,0:T(8,128)S(1)}, u32[]{:S(2)}, u32[]{:S(2)}) async-start(f32[8,80,128]{2,1,0:T(8,128)} %broadcast_in_dim.25), calls=%async_computation.2 | async-start | bytes 655360 | tf_op jit(solution)/shard_map/all_to_all | solution.py:164
  57.3 7.1 %all-to-all-done.2 = f32[8,80,128]{2,1,0:T(8,128)S(1)} async-done(((f32[8,80,128]{2,1,0:T(8,128)}), f32[8,80,128]{2,1,0:T(8,128)S(1)}, u32[]{:S(2)}, u32[]{:S(2)}) %all-to-all-start.2) | async-done | bytes 327712 | tf_op jit(solution)/shard_map/all_to_all | solution.py:164
  64.4 1.2 %fusion.19 = (f32[]{:T(128)}, f32[8,128]{1,0:T(8,128)}) fusion(f32[8,128]{1,0:T(8,128)S(1)} %copy-done.1, f32[8,128]{1,0:T(8,128)S(1)} %copy-done.2, f32[64,128]{1,0:T(8,128)S(1)} %slice_reduce_fusion, s32[]{:T(128)S(6)} %select_n.71), kind=kLoop, calls=%fused_computation.37 | loop fusion | flops 4095 | bytes 16392 | tf_op jit(solution)/shard_map/reduce_sum | solution.py:173
  65.6 0.7 gather_fusion.2
  66.3 3.4 %fusion.2 = f32[128,1,128]{2,1,0:T(1,128)S(1)} fusion(bf16[128,128,128]{2,1,0:T(8,128)(2,1)} %param.11, bf16[128,128,1]{1,0,2:T(8,128)(2,1)S(1)} %bitcast.85), kind=kOutput, calls=%fused_computation.12 | convolution fusion | flops 4194304 | bytes 4292608 | tf_op jit(solution)/shard_map/bij,bi->bj/dot_general | solution.py:176
  69.7 1.0 %scatter_custom_fusion = f32[128,128]{1,0:T(8,128)S(1)} fusion(s32[128]{0:T(128)S(1)} %get-tuple-element.15, f32[128,128]{1,0:T(8,128)S(1)} %bitcast.88, f32[]{:T(128)} %constant.60.clone.1), kind=kCustom, calls=%fused_computation.28 | custom fusion | flops 16384 | bytes 65540 | tf_op jit(solution)/shard_map/scatter-add | solution.py:179
  70.7 0.9 convolution_bitcast_fusion
  71.6 0.1 reshape.222
  72.4 0.1 fusion.21
  72.5 0.7 pad_maximum_fusion
  73.1 4.0 %all-to-all-start.3 = ((f32[32,5,128]{2,1,0:T(8,128)}), f32[32,5,128]{2,1,0:T(8,128)S(1)}, u32[]{:S(2)}, u32[]{:S(2)}) async-start(f32[32,5,128]{2,1,0:T(8,128)} %pad_maximum_fusion), calls=%async_computation.3 | async-start | bytes 262144 | tf_op jit(solution)/shard_map/all_to_all | solution.py:200
  77.2 0.6 multiply_reduce_fusion
  78.5 0.6 multiply_reduce_fusion.1
  79.7 0.1 squeeze.25
  79.8 6.8 %all-to-all-done.3 = f32[32,5,128]{2,1,0:T(8,128)S(1)} async-done(((f32[32,5,128]{2,1,0:T(8,128)}), f32[32,5,128]{2,1,0:T(8,128)S(1)}, u32[]{:S(2)}, u32[]{:S(2)}) %all-to-all-start.3) | async-done | bytes 81952 | tf_op jit(solution)/shard_map/all_to_all | solution.py:200
  86.6 0.1 slice_reduce_fusion.1
  86.7 0.6 broadcast_in_dim.59
  87.3 5.7 %all-to-all-start.4 = ((f32[8,1,128]{2,1,0:T(1,128)}), f32[8,1,128]{2,1,0:T(1,128)S(1)}, u32[]{:S(2)}, u32[]{:S(2)}) async-start(f32[8,1,128]{2,1,0:T(1,128)} %broadcast_in_dim.59), calls=%async_computation.4 | async-start | bytes 8192 | tf_op jit(solution)/shard_map/all_to_all | solution.py:202
  93.0 1.0 %scatter_custom_fusion.1 = f32[129,128]{1,0:T(8,128)S(1)} fusion(s32[128]{0:T(128)S(1)} %fusion.25, f32[128,128]{1,0:T(8,128)S(1)} %bitcast.90, f32[]{:T(128)} %constant.60.clone.1), kind=kCustom, calls=%fused_computation.21 | custom fusion | flops 16384 | bytes 66052 | tf_op jit(solution)/shard_map/scatter-add | solution.py:206
  94.1 0.7 reshape.224
  94.7 2.9 %all-to-all-done.4 = f32[8,1,128]{2,1,0:T(1,128)S(1)} async-done(((f32[8,1,128]{2,1,0:T(1,128)}), f32[8,1,128]{2,1,0:T(1,128)S(1)}, u32[]{:S(2)}, u32[]{:S(2)}) %all-to-all-start.4) | async-done | bytes 4128 | tf_op jit(solution)/shard_map/all_to_all | solution.py:202
  97.6 0.6 slice.70
  98.2 0.1 reshape.225
  98.9 0.6 fusion.20
  (23 shorter events, 0.1 us)
Async XLA Ops:
  0.6 31.2 %copy-start.4 = (s32[3,128]{1,0:T(4,128)S(1)}, s32[3,128]{1,0:T(4,128)}, u32[]{:S(2)}) copy-start(s32[3,128]{1,0:T(4,128)} %param.12) | copy-start | bytes 4612
  2.0 20.6 %all-to-all-start = ((s32[32,1,128]{2,1,0:T(1,128)}), s32[32,1,128]{2,1,0:T(1,128)S(1)}, u32[]{:S(2)}, u32[]{:S(2)}) async-start(s32[32,1,128]{2,1,0:T(1,128)} %bitcast), calls=%async_computation | async-start | bytes 32768 | tf_op jit(solution)/shard_map/all_to_all | solution.py:121
  25.7 23.1 %copy-start.1 = (f32[8,128]{1,0:T(8,128)S(1)}, f32[8,128]{1,0:T(8,128)}, u32[]{:S(2)}) copy-start(f32[8,128]{1,0:T(8,128)} %param.21) | copy-start | bytes 12292
  25.7 23.1 %copy-start.2 = (f32[8,128]{1,0:T(8,128)S(1)}, f32[8,128]{1,0:T(8,128)}, u32[]{:S(2)}) copy-start(f32[8,128]{1,0:T(8,128)} %param.20) | copy-start | bytes 12292
  26.5 16.9 %all-to-all-start.1 = ((f32[32,24,128]{2,1,0:T(8,128)}), f32[32,24,128]{2,1,0:T(8,128)S(1)}, u32[]{:S(2)}, u32[]{:S(2)}) async-start(f32[32,24,128]{2,1,0:T(8,128)} %reshape.217), calls=%async_computation.1 | async-start | bytes 786432 | tf_op jit(solution)/shard_map/all_to_all | solution.py:139
  48.6 28.6 %copy-start = (f32[3,16]{1,0:T(4,128)S(1)}, f32[3,16]{1,0:T(4,128)}, u32[]{:S(2)}) copy-start(f32[3,16]{1,0:T(4,128)} %rde_ref.1) | copy-start | bytes 580
  48.6 29.8 %copy-start.3 = (f32[16]{0:T(128)S(1)}, f32[16]{0:T(128)}, u32[]{:S(2)}) copy-start(f32[16]{0:T(128)} %cse_ref.1) | copy-start | bytes 196
  49.6 14.8 %all-to-all-start.2 = ((f32[8,80,128]{2,1,0:T(8,128)}), f32[8,80,128]{2,1,0:T(8,128)S(1)}, u32[]{:S(2)}, u32[]{:S(2)}) async-start(f32[8,80,128]{2,1,0:T(8,128)} %broadcast_in_dim.25), calls=%async_computation.2 | async-start | bytes 655360 | tf_op jit(solution)/shard_map/all_to_all | solution.py:164
  73.1 13.5 %all-to-all-start.3 = ((f32[32,5,128]{2,1,0:T(8,128)}), f32[32,5,128]{2,1,0:T(8,128)S(1)}, u32[]{:S(2)}, u32[]{:S(2)}) async-start(f32[32,5,128]{2,1,0:T(8,128)} %pad_maximum_fusion), calls=%async_computation.3 | async-start | bytes 262144 | tf_op jit(solution)/shard_map/all_to_all | solution.py:200
  87.3 10.3 %all-to-all-start.4 = ((f32[8,1,128]{2,1,0:T(1,128)}), f32[8,1,128]{2,1,0:T(1,128)S(1)}, u32[]{:S(2)}, u32[]{:S(2)}) async-start(f32[8,1,128]{2,1,0:T(1,128)} %broadcast_in_dim.59), calls=%async_computation.4 | async-start | bytes 8192 | tf_op jit(solution)/shard_map/all_to_all | solution.py:202

commit v10 on v9

--- a/solution.py
+++ b/solution.py
@@ -129,13 +129,13 @@
         category_sensitivity_effect,
         reservoir_decay_effect,
     ).reshape(6, local_ids, tile)
+    own_fields, block_placement_table, needed_tile_lists = lax.optimization_barrier(
+        (own_fields, block_placement_table, needed_tile_lists)
+    )
     asked = (
         requests.reshape(-1)[:, None] == jnp.arange(local_ids, dtype=jnp.int32)[None, :]
     ).astype(jnp.float32)
     answer = jnp.einsum("rl,qlc->rqc", asked, own_fields, precision=lax.Precision.HIGHEST)
-    answer, block_placement_table, needed_tile_lists = lax.optimization_barrier(
-        (answer, block_placement_table, needed_tile_lists)
-    )
     received = lax.all_to_all(answer.reshape(n_snd, cap * 6, tile), "snd", 0, 0).reshape(
         n_snd * cap, 6, tile
     )

time: 101 us -> 102 us (level)
  starting transfers between devices: 33.5 us -> 36.3 us
  waiting for transfers between devices: 33.5 us -> 31.3 us
    all_to_all x1, waiting for transfers between devices: 5.2 us -> 2.24 us  [shards(): requests = lax.all_to_all(lanes, 'snd', 0, 0)[:, 0, :cap]]
    all_to_all x1, starting transfers between devices: 4.03 us -> 6.98 us  [shards(): lax.all_to_all(answer.reshape(n_snd, cap * 6, tile), 'snd', 0, 0)]
  transfers between devices with their start and end apart: 5 -> 5, of which waited for: 5 -> 5; matrix products, arithmetic and copies ran while one was open for 6% -> 8% of each run, Pallas kernels for 2% -> 2%
where the time goes in v10:
time: 102 us; the launch traced here: 101 us
  starting transfers between devices  36.3 us (36%)
  waiting for transfers between devices  31.3 us (31%)
  local copies, waits for them, and re-layouts  9.73 us (10%)
  matrix products  9.24 us (9%)
  other arithmetic  8.18 us (8%)
  between operations  4.6 us (5%)
  Pallas kernels  1.97 us (2%)
    all_to_all x1, waiting for transfers between devices, shards(): lax.all_to_all(answer.reshape(n_snd, cap * 6, tile), 'snd', 0, 0)  12.3 us
    all_to_all x1, starting transfers between devices, shards(): requests = lax.all_to_all(lanes, 'snd', 0, 0)[:, 0, :cap]  12 us
    all_to_all x1, starting transfers between devices, shards(): lax.all_to_all(jnp.broadcast_to(payload[None], (n_map,) + payload.shape),...  7.59 us
    all_to_all x1, waiting for transfers between devices, shards(): lax.all_to_all(jnp.broadcast_to(payload[None], (n_map,) + payload.shape),...  7.11 us
    all_to_all x1, starting transfers between devices, shards(): lax.all_to_all(answer.reshape(n_snd, cap * 6, tile), 'snd', 0, 0)  6.98 us
    all_to_all x1, waiting for transfers between devices, shards(): incoming = lax.all_to_all(parcel, 'snd', 0, 0)  6.82 us
    all_to_all x1, starting transfers between devices, shards(): lax.all_to_all(jnp.broadcast_to(column[None], (n_map, tile)), 'map', 0, 0)  5.73 us
    dot_general x1, matrix products, shards(): jnp.einsum('bij,bj->bi', sensitivity_blocks, vectors, preferred_element_t...  4.43 us
  transfers between devices with their start and end apart: 5, of which 5 were waited for; matrix products, arithmetic and copies ran while one was open for 8% of the time, Pallas kernels for 2%

profile of v10, /device:TPU:1, one launch (start us, length us, event | category | flops | bytes accessed | tf_op | source)
XLA Modules:
  0.0 101.3 jit_solution(12720277218985922851)
XLA Ops:
  0.6 0.8 copy.35
  1.4 0.6 pad.8
  2.0 12.0 %all-to-all-start = ((s32[32,1,128]{2,1,0:T(1,128)}), s32[32,1,128]{2,1,0:T(1,128)S(1)}, u32[]{:S(2)}, u32[]{:S(2)}) async-start(s32[32,1,128]{2,1,0:T(1,128)} %bitcast.2), calls=%async_computation | async-start | bytes 32768 | tf_op jit(solution)/shard_map/all_to_all | solution.py:121
  14.1 2.0 %shard_map.138 = f32[6,2,8192]{2,1,0:T(2,128)} custom-call(f32[16]{0:T(128)} %cse_ref.1, f32[3,16]{1,0:T(4,128)} %rde_ref.1, s32[1,8192]{1,0:T(1,128)} %bitcast.92, f32[2,8192]{1,0:T(2,128)} %warm_ref.1, f32[2,8192]{1,0:T(2,128)} %wet_ref.1, f32[3,8192]{1,0:T(4,128)} %carbon_ref.1), custom_call_target="tpu_custom_call" | custom-call | tf_op jit(solution)/shard_map/pallas_call | solution.py:83
  16.0 1.3 %reshape.216 = f32[6,128,128]{2,1,0:T(8,128)S(1)} reshape(f32[6,2,8192]{2,1,0:T(2,128)} %shard_map.138) | data formatting | bytes 786432 | tf_op jit(solution)/shard_map/reshape | solution.py:131
  17.4 0.8 fusion.23
  18.1 0.8 fusion.26
  18.9 0.8 copy.38
  19.7 0.6 gather_fusion
  20.3 2.2 %all-to-all-done = s32[32,1,128]{2,1,0:T(1,128)S(1)} async-done(((s32[32,1,128]{2,1,0:T(1,128)}), s32[32,1,128]{2,1,0:T(1,128)S(1)}, u32[]{:S(2)}, u32[]{:S(2)}) %all-to-all-start) | async-done | bytes 16416 | tf_op jit(solution)/shard_map/all_to_all | solution.py:121
  22.6 0.1 fusion.28
  22.6 0.1 eq.61
  22.7 0.4 fusion.7
  23.1 0.2 copy.36
  23.4 0.8 reshape.217
  24.2 7.0 %all-to-all-start.1 = ((f32[32,24,128]{2,1,0:T(8,128)}), f32[32,24,128]{2,1,0:T(8,128)S(1)}, u32[]{:S(2)}, u32[]{:S(2)}) async-start(f32[32,24,128]{2,1,0:T(8,128)} %reshape.217), calls=%async_computation.1 | async-start | bytes 786432 | tf_op jit(solution)/shard_map/all_to_all | solution.py:139
  31.2 0.7 iota_reduce_fusion
  31.9 12.3 %all-to-all-done.1 = f32[32,24,128]{2,1,0:T(8,128)S(1)} async-done(((f32[32,24,128]{2,1,0:T(8,128)}), f32[32,24,128]{2,1,0:T(8,128)S(1)}, u32[]{:S(2)}, u32[]{:S(2)}) %all-to-all-start.1) | async-done | bytes 393248 | tf_op jit(solution)/shard_map/all_to_all | solution.py:139
  44.2 0.1 reshape.218
  44.2 0.1 fusion.27
  44.4 0.7 gather_fusion.1
  45.0 4.4 %fusion.4 = f32[128,1,128]{2,1,0:T(1,128)S(1)} fusion(bf16[128,128,128]{2,1,0:T(8,128)(2,1)} %param.11, bf16[128,128,1]{1,0,2:T(8,128)(2,1)S(1)} %bitcast.84), kind=kOutput, calls=%fused_computation.14 | convolution fusion | flops 4194304 | bytes 4292608 | tf_op jit(solution)/shard_map/bij,bj->bi/dot_general | solution.py:153
  49.4 0.2 fusion.17
  49.7 0.7 broadcast_in_dim.25
  50.4 7.6 %all-to-all-start.2 = ((f32[8,80,128]{2,1,0:T(8,128)}), f32[8,80,128]{2,1,0:T(8,128)S(1)}, u32[]{:S(2)}, u32[]{:S(2)}) async-start(f32[8,80,128]{2,1,0:T(8,128)} %broadcast_in_dim.25), calls=%async_computation.2 | async-start | bytes 655360 | tf_op jit(solution)/shard_map/all_to_all | solution.py:164
  58.0 7.1 %all-to-all-done.2 = f32[8,80,128]{2,1,0:T(8,128)S(1)} async-done(((f32[8,80,128]{2,1,0:T(8,128)}), f32[8,80,128]{2,1,0:T(8,128)S(1)}, u32[]{:S(2)}, u32[]{:S(2)}) %all-to-all-start.2) | async-done | bytes 327712 | tf_op jit(solution)/shard_map/all_to_all | solution.py:164
  65.1 1.2 %fusion.19 = (f32[]{:T(128)}, f32[8,128]{1,0:T(8,128)}) fusion(f32[8,128]{1,0:T(8,128)S(1)} %copy-done.1, f32[8,128]{1,0:T(8,128)S(1)} %copy-done.2, f32[64,128]{1,0:T(8,128)S(1)} %slice_reduce_fusion, s32[]{:T(128)S(6)} %select_n.71), kind=kLoop, calls=%fused_computation.37 | loop fusion | flops 4095 | bytes 16392 | tf_op jit(solution)/shard_map/reduce_sum | solution.py:173
  66.3 0.7 gather_fusion.2
  67.1 3.4 %fusion.2 = f32[128,1,128]{2,1,0:T(1,128)S(1)} fusion(bf16[128,128,128]{2,1,0:T(8,128)(2,1)} %param.11, bf16[128,128,1]{1,0,2:T(8,128)(2,1)S(1)} %bitcast.85), kind=kOutput, calls=%fused_computation.12 | convolution fusion | flops 4194304 | bytes 4292608 | tf_op jit(solution)/shard_map/bij,bi->bj/dot_general | solution.py:176
  70.4 1.0 %scatter_custom_fusion = f32[128,128]{1,0:T(8,128)S(1)} fusion(s32[128]{0:T(128)S(1)} %get-tuple-element.15, f32[128,128]{1,0:T(8,128)S(1)} %bitcast.88, f32[]{:T(128)} %constant.60.clone.1), kind=kCustom, calls=%fused_computation.28 | custom fusion | flops 16384 | bytes 65540 | tf_op jit(solution)/shard_map/scatter-add | solution.py:179
  71.5 0.9 convolution_bitcast_fusion
  72.4 0.1 reshape.222
  73.1 0.1 fusion.21
  73.2 0.7 pad_maximum_fusion
  73.9 3.9 %all-to-all-start.3 = ((f32[32,5,128]{2,1,0:T(8,128)}), f32[32,5,128]{2,1,0:T(8,128)S(1)}, u32[]{:S(2)}, u32[]{:S(2)}) async-start(f32[32,5,128]{2,1,0:T(8,128)} %pad_maximum_fusion), calls=%async_computation.3 | async-start | bytes 262144 | tf_op jit(solution)/shard_map/all_to_all | solution.py:200
  77.8 0.6 multiply_reduce_fusion
  79.1 0.6 multiply_reduce_fusion.1
  80.3 0.1 squeeze.25
  80.5 6.8 %all-to-all-done.3 = f32[32,5,128]{2,1,0:T(8,128)S(1)} async-done(((f32[32,5,128]{2,1,0:T(8,128)}), f32[32,5,128]{2,1,0:T(8,128)S(1)}, u32[]{:S(2)}, u32[]{:S(2)}) %all-to-all-start.3) | async-done | bytes 81952 | tf_op jit(solution)/shard_map/all_to_all | solution.py:200
  87.3 0.1 slice_reduce_fusion.1
  87.3 0.6 broadcast_in_dim.59
  87.9 5.7 %all-to-all-start.4 = ((f32[8,1,128]{2,1,0:T(1,128)}), f32[8,1,128]{2,1,0:T(1,128)S(1)}, u32[]{:S(2)}, u32[]{:S(2)}) async-start(f32[8,1,128]{2,1,0:T(1,128)} %broadcast_in_dim.59), calls=%async_computation.4 | async-start | bytes 8192 | tf_op jit(solution)/shard_map/all_to_all | solution.py:202
  93.7 1.0 %scatter_custom_fusion.1 = f32[129,128]{1,0:T(8,128)S(1)} fusion(s32[128]{0:T(128)S(1)} %fusion.25, f32[128,128]{1,0:T(8,128)S(1)} %bitcast.90, f32[]{:T(128)} %constant.60.clone.1), kind=kCustom, calls=%fused_computation.21 | custom fusion | flops 16384 | bytes 66052 | tf_op jit(solution)/shard_map/scatter-add | solution.py:206
  94.7 0.7 reshape.224
  95.4 2.9 %all-to-all-done.4 = f32[8,1,128]{2,1,0:T(1,128)S(1)} async-done(((f32[8,1,128]{2,1,0:T(1,128)}), f32[8,1,128]{2,1,0:T(1,128)S(1)}, u32[]{:S(2)}, u32[]{:S(2)}) %all-to-all-start.4) | async-done | bytes 4128 | tf_op jit(solution)/shard_map/all_to_all | solution.py:202
  98.3 0.6 slice.70
  98.9 0.1 reshape.225
  99.6 0.6 fusion.20
  (23 shorter events, 0.1 us)
Async XLA Ops:
  0.6 31.2 %copy-start.4 = (s32[3,128]{1,0:T(4,128)S(1)}, s32[3,128]{1,0:T(4,128)}, u32[]{:S(2)}) copy-start(s32[3,128]{1,0:T(4,128)} %param.12) | copy-start | bytes 4612
  2.0 20.6 %all-to-all-start = ((s32[32,1,128]{2,1,0:T(1,128)}), s32[32,1,128]{2,1,0:T(1,128)S(1)}, u32[]{:S(2)}, u32[]{:S(2)}) async-start(s32[32,1,128]{2,1,0:T(1,128)} %bitcast.2), calls=%async_computation | async-start | bytes 32768 | tf_op jit(solution)/shard_map/all_to_all | solution.py:121
  23.1 26.5 %copy-start.1 = (f32[8,128]{1,0:T(8,128)S(1)}, f32[8,128]{1,0:T(8,128)}, u32[]{:S(2)}) copy-start(f32[8,128]{1,0:T(8,128)} %param.21) | copy-start | bytes 12292
  23.1 26.5 %copy-start.2 = (f32[8,128]{1,0:T(8,128)S(1)}, f32[8,128]{1,0:T(8,128)}, u32[]{:S(2)}) copy-start(f32[8,128]{1,0:T(8,128)} %param.20) | copy-start | bytes 12292
  24.2 20.0 %all-to-all-start.1 = ((f32[32,24,128]{2,1,0:T(8,128)}), f32[32,24,128]{2,1,0:T(8,128)S(1)}, u32[]{:S(2)}, u32[]{:S(2)}) async-start(f32[32,24,128]{2,1,0:T(8,128)} %reshape.217), calls=%async_computation.1 | async-start | bytes 786432 | tf_op jit(solution)/shard_map/all_to_all | solution.py:139
  49.4 28.4 %copy-start = (f32[3,16]{1,0:T(4,128)S(1)}, f32[3,16]{1,0:T(4,128)}, u32[]{:S(2)}) copy-start(f32[3,16]{1,0:T(4,128)} %rde_ref.1) | copy-start | bytes 580
  49.4 29.7 %copy-start.3 = (f32[16]{0:T(128)S(1)}, f32[16]{0:T(128)}, u32[]{:S(2)}) copy-start(f32[16]{0:T(128)} %cse_ref.1) | copy-start | bytes 196
  50.4 14.7 %all-to-all-start.2 = ((f32[8,80,128]{2,1,0:T(8,128)}), f32[8,80,128]{2,1,0:T(8,128)S(1)}, u32[]{:S(2)}, u32[]{:S(2)}) async-start(f32[8,80,128]{2,1,0:T(8,128)} %broadcast_in_dim.25), calls=%async_computation.2 | async-start | bytes 655360 | tf_op jit(solution)/shard_map/all_to_all | solution.py:164
  73.9 13.4 %all-to-all-start.3 = ((f32[32,5,128]{2,1,0:T(8,128)}), f32[32,5,128]{2,1,0:T(8,128)S(1)}, u32[]{:S(2)}, u32[]{:S(2)}) async-start(f32[32,5,128]{2,1,0:T(8,128)} %pad_maximum_fusion), calls=%async_computation.3 | async-start | bytes 262144 | tf_op jit(solution)/shard_map/all_to_all | solution.py:200
  87.9 10.3 %all-to-all-start.4 = ((f32[8,1,128]{2,1,0:T(1,128)}), f32[8,1,128]{2,1,0:T(1,128)S(1)}, u32[]{:S(2)}, u32[]{:S(2)}) async-start(f32[8,1,128]{2,1,0:T(1,128)} %broadcast_in_dim.59), calls=%async_computation.4 | async-start | bytes 8192 | tf_op jit(solution)/shard_map/all_to_all | solution.py:202

commit v11 on v10

--- a/solution.py
+++ b/solution.py
@@ -167,10 +167,11 @@
     model_rows = jnp.sum(swapped[:, :rows_dev], axis=0)
     anomaly_rows = swapped[:, rows_dev : rows_dev + rows_own].reshape(rows_dev, tile)
     precision_rows = swapped[:, rows_dev + rows_own :].reshape(rows_dev, tile)
-    weighted_rows = ((model_rows - anomaly_rows) * precision_rows).astype(jnp.bfloat16)
+    diff_rows = model_rows - anomaly_rows
+    weighted_rows = (diff_rows * precision_rows).astype(jnp.bfloat16)
     model_xco2 = lax.dynamic_slice(model_rows, (first, 0), (rows_own, tile))
-    diff = model_xco2 - measured_anomaly
-    misfit = 0.5 * jnp.sum(retrieval_precision * diff * diff)
+    shard_misfit = 0.5 * jnp.sum(precision_rows * diff_rows * diff_rows)
+    misfit = jnp.where(me_map == 0, shard_misfit, 0.0)
 
     back_rows = weighted_rows.at[block_row].get(mode="promise_in_bounds")
     block_grads = jnp.einsum(

time: 102 us -> 101 us (level)
    all_to_all x1, waiting for transfers between devices: 7.11 us -> 4.48 us  [shards(): lax.all_to_all(jnp.broadcast_to(payload[None], (n_map,) + payload.shape),...]
    all_to_all x1, waiting for transfers between devices: 6.82 us -> 9.44 us  [shards(): incoming = lax.all_to_all(parcel, 'snd', 0, 0)]
  transfers between devices with their start and end apart: 5 -> 5, of which waited for: 5 -> 5; matrix products, arithmetic and copies ran while one was open for 8% -> 9% of each run, Pallas kernels for 2% -> 2%
where the time goes in v11:
time: 101 us
  starting transfers between devices  36.3 us (36%)
  waiting for transfers between devices  30.7 us (30%)
  local copies, waits for them, and re-layouts  10.3 us (10%)
  matrix products  9.24 us (9%)
  other arithmetic  7.6 us (8%)
  between operations  4.62 us (5%)
  Pallas kernels  1.97 us (2%)
    all_to_all x1, waiting for transfers between devices, shards(): lax.all_to_all(answer.reshape(n_snd, cap * 6, tile), 'snd', 0, 0)  12.3 us
    all_to_all x1, starting transfers between devices, shards(): requests = lax.all_to_all(lanes, 'snd', 0, 0)[:, 0, :cap]  12 us
    all_to_all x1, waiting for transfers between devices, shards(): incoming = lax.all_to_all(parcel, 'snd', 0, 0)  9.44 us
    all_to_all x1, starting transfers between devices, shards(): lax.all_to_all(jnp.broadcast_to(payload[None], (n_map,) + payload.shape),...  7.6 us
    all_to_all x1, starting transfers between devices, shards(): lax.all_to_all(answer.reshape(n_snd, cap * 6, tile), 'snd', 0, 0)  6.99 us
    all_to_all x1, starting transfers between devices, shards(): lax.all_to_all(jnp.broadcast_to(column[None], (n_map, tile)), 'map', 0, 0)  5.73 us
    all_to_all x1, waiting for transfers between devices, shards(): lax.all_to_all(jnp.broadcast_to(payload[None], (n_map,) + payload.shape),...  4.48 us
    dot_general x1, matrix products, shards(): jnp.einsum('bij,bj->bi', sensitivity_blocks, vectors, preferred_element_t...  4.43 us
  transfers between devices with their start and end apart: 5, of which 5 were waited for; matrix products, arithmetic and copies ran while one was open for 9% of the time, Pallas kernels for 2%

profile of v11, /device:TPU:1, one launch (start us, length us, event | category | flops | bytes accessed | tf_op | source)
XLA Modules:
  0.0 100.8 jit_solution(4000264345031630310)
XLA Ops:
  0.6 0.8 copy.35
  1.4 0.6 pad.8
  2.0 12.0 %all-to-all-start = ((s32[32,1,128]{2,1,0:T(1,128)}), s32[32,1,128]{2,1,0:T(1,128)S(1)}, u32[]{:S(2)}, u32[]{:S(2)}) async-start(s32[32,1,128]{2,1,0:T(1,128)} %bitcast.2), calls=%async_computation | async-start | bytes 32768 | tf_op jit(solution)/shard_map/all_to_all | solution.py:121
  14.1 2.0 %shard_map.138 = f32[6,2,8192]{2,1,0:T(2,128)} custom-call(f32[16]{0:T(128)} %cse_ref.1, f32[3,16]{1,0:T(4,128)} %rde_ref.1, s32[1,8192]{1,0:T(1,128)} %bitcast.92, f32[2,8192]{1,0:T(2,128)} %warm_ref.1, f32[2,8192]{1,0:T(2,128)} %wet_ref.1, f32[3,8192]{1,0:T(4,128)} %carbon_ref.1), custom_call_target="tpu_custom_call" | custom-call | tf_op jit(solution)/shard_map/pallas_call | solution.py:83
  16.0 1.3 %reshape.217 = f32[6,128,128]{2,1,0:T(8,128)S(1)} reshape(f32[6,2,8192]{2,1,0:T(2,128)} %shard_map.138) | data formatting | bytes 786432 | tf_op jit(solution)/shard_map/reshape | solution.py:131
  17.4 0.8 fusion.21
  18.1 0.8 fusion.24
  18.9 0.8 copy.38
  19.7 0.6 gather_fusion
  20.3 2.2 %all-to-all-done = s32[32,1,128]{2,1,0:T(1,128)S(1)} async-done(((s32[32,1,128]{2,1,0:T(1,128)}), s32[32,1,128]{2,1,0:T(1,128)S(1)}, u32[]{:S(2)}, u32[]{:S(2)}) %all-to-all-start) | async-done | bytes 16416 | tf_op jit(solution)/shard_map/all_to_all | solution.py:121
  22.6 0.1 fusion.26
  22.6 0.1 eq.64
  22.7 0.4 fusion.7
  23.1 0.2 copy.36
  23.4 0.8 reshape.218
  24.2 7.0 %all-to-all-start.1 = ((f32[32,24,128]{2,1,0:T(8,128)}), f32[32,24,128]{2,1,0:T(8,128)S(1)}, u32[]{:S(2)}, u32[]{:S(2)}) async-start(f32[32,24,128]{2,1,0:T(8,128)} %reshape.218), calls=%async_computation.1 | async-start | bytes 786432 | tf_op jit(solution)/shard_map/all_to_all | solution.py:139
  31.2 0.7 iota_reduce_fusion
  31.9 12.3 %all-to-all-done.1 = f32[32,24,128]{2,1,0:T(8,128)S(1)} async-done(((f32[32,24,128]{2,1,0:T(8,128)}), f32[32,24,128]{2,1,0:T(8,128)S(1)}, u32[]{:S(2)}, u32[]{:S(2)}) %all-to-all-start.1) | async-done | bytes 393248 | tf_op jit(solution)/shard_map/all_to_all | solution.py:139
  44.2 0.1 reshape.219
  44.3 0.1 fusion.25
  44.4 0.7 gather_fusion.1
  45.0 4.4 %fusion.4 = f32[128,1,128]{2,1,0:T(1,128)S(1)} fusion(bf16[128,128,128]{2,1,0:T(8,128)(2,1)} %param.11, bf16[128,128,1]{1,0,2:T(8,128)(2,1)S(1)} %bitcast.84), kind=kOutput, calls=%fused_computation.14 | convolution fusion | flops 4194304 | bytes 4292608 | tf_op jit(solution)/shard_map/bij,bj->bi/dot_general | solution.py:153
  49.5 0.2 fusion.16
  49.7 0.7 broadcast_in_dim.25
  50.4 7.6 %all-to-all-start.2 = ((f32[8,80,128]{2,1,0:T(8,128)}), f32[8,80,128]{2,1,0:T(8,128)S(1)}, u32[]{:S(2)}, u32[]{:S(2)}) async-start(f32[8,80,128]{2,1,0:T(8,128)} %broadcast_in_dim.25), calls=%async_computation.2 | async-start | bytes 655360 | tf_op jit(solution)/shard_map/all_to_all | solution.py:164
  58.0 0.6 multiply_reduce_fusion
  59.3 0.6 multiply_reduce_fusion.1
  60.6 0.1 squeeze.25
  60.7 4.5 %all-to-all-done.2 = f32[8,80,128]{2,1,0:T(8,128)S(1)} async-done(((f32[8,80,128]{2,1,0:T(8,128)}), f32[8,80,128]{2,1,0:T(8,128)S(1)}, u32[]{:S(2)}, u32[]{:S(2)}) %all-to-all-start.2) | async-done | bytes 327712 | tf_op jit(solution)/shard_map/all_to_all | solution.py:164
  65.2 0.7 gather_fusion.2
  65.9 3.4 %fusion.2 = f32[128,1,128]{2,1,0:T(1,128)S(1)} fusion(bf16[128,128,128]{2,1,0:T(8,128)(2,1)} %param.11, bf16[128,128,1]{1,0,2:T(8,128)(2,1)S(1)} %bitcast.85), kind=kOutput, calls=%fused_computation.12 | convolution fusion | flops 4194304 | bytes 4292608 | tf_op jit(solution)/shard_map/bij,bi->bj/dot_general | solution.py:177
  69.3 1.0 %scatter_custom_fusion = f32[128,128]{1,0:T(8,128)S(1)} fusion(s32[128]{0:T(128)S(1)} %get-tuple-element.13, f32[128,128]{1,0:T(8,128)S(1)} %bitcast.88, f32[]{:T(128)} %constant.60.clone.1), kind=kCustom, calls=%fused_computation.29 | custom fusion | flops 16384 | bytes 65540 | tf_op jit(solution)/shard_map/scatter-add | solution.py:180
  70.3 0.9 convolution_bitcast_fusion
  71.2 0.1 reshape.223
  71.3 0.6 fusion.11
  72.6 0.1 fusion.19
  72.7 0.7 pad_maximum_fusion
  73.3 3.9 %all-to-all-start.3 = ((f32[32,5,128]{2,1,0:T(8,128)}), f32[32,5,128]{2,1,0:T(8,128)S(1)}, u32[]{:S(2)}, u32[]{:S(2)}) async-start(f32[32,5,128]{2,1,0:T(8,128)} %pad_maximum_fusion), calls=%async_computation.3 | async-start | bytes 262144 | tf_op jit(solution)/shard_map/all_to_all | solution.py:201
  77.3 9.4 %all-to-all-done.3 = f32[32,5,128]{2,1,0:T(8,128)S(1)} async-done(((f32[32,5,128]{2,1,0:T(8,128)}), f32[32,5,128]{2,1,0:T(8,128)S(1)}, u32[]{:S(2)}, u32[]{:S(2)}) %all-to-all-start.3) | async-done | bytes 81952 | tf_op jit(solution)/shard_map/all_to_all | solution.py:201
  86.8 0.6 broadcast_in_dim.59
  87.4 5.7 %all-to-all-start.4 = ((f32[8,1,128]{2,1,0:T(1,128)}), f32[8,1,128]{2,1,0:T(1,128)S(1)}, u32[]{:S(2)}, u32[]{:S(2)}) async-start(f32[8,1,128]{2,1,0:T(1,128)} %broadcast_in_dim.59), calls=%async_computation.4 | async-start | bytes 8192 | tf_op jit(solution)/shard_map/all_to_all | solution.py:203
  93.1 0.6 constant_dynamic-slice_fusion
  93.7 1.0 %scatter_custom_fusion.1 = f32[129,128]{1,0:T(8,128)S(1)} fusion(s32[128]{0:T(128)S(1)} %fusion.23, f32[128,128]{1,0:T(8,128)S(1)} %bitcast.90, f32[]{:T(128)} %constant.60.clone.1), kind=kCustom, calls=%fused_computation.22 | custom fusion | flops 16384 | bytes 66052 | tf_op jit(solution)/shard_map/scatter-add | solution.py:207
  94.8 0.7 reshape.225
  95.4 2.3 %all-to-all-done.4 = f32[8,1,128]{2,1,0:T(1,128)S(1)} async-done(((f32[8,1,128]{2,1,0:T(1,128)}), f32[8,1,128]{2,1,0:T(1,128)S(1)}, u32[]{:S(2)}, u32[]{:S(2)}) %all-to-all-start.4) | async-done | bytes 4128 | tf_op jit(solution)/shard_map/all_to_all | solution.py:203
  97.7 0.6 slice.70
  98.3 0.1 reshape.226
  99.0 0.6 fusion.18
  (24 shorter events, 0.2 us)
Async XLA Ops:
  0.6 31.3 %copy-start.4 = (s32[3,128]{1,0:T(4,128)S(1)}, s32[3,128]{1,0:T(4,128)}, u32[]{:S(2)}) copy-start(s32[3,128]{1,0:T(4,128)} %param.12) | copy-start | bytes 4612
  2.0 20.6 %all-to-all-start = ((s32[32,1,128]{2,1,0:T(1,128)}), s32[32,1,128]{2,1,0:T(1,128)S(1)}, u32[]{:S(2)}, u32[]{:S(2)}) async-start(s32[32,1,128]{2,1,0:T(1,128)} %bitcast.2), calls=%async_computation | async-start | bytes 32768 | tf_op jit(solution)/shard_map/all_to_all | solution.py:121
  23.1 26.6 %copy-start.1 = (f32[8,128]{1,0:T(8,128)S(1)}, f32[8,128]{1,0:T(8,128)}, u32[]{:S(2)}) copy-start(f32[8,128]{1,0:T(8,128)} %param.21) | copy-start | bytes 12292
  23.1 26.5 %copy-start.2 = (f32[8,128]{1,0:T(8,128)S(1)}, f32[8,128]{1,0:T(8,128)}, u32[]{:S(2)}) copy-start(f32[8,128]{1,0:T(8,128)} %param.20) | copy-start | bytes 12292
  23.4 34.6 %copy-start = (f32[3,16]{1,0:T(4,128)S(1)}, f32[3,16]{1,0:T(4,128)}, u32[]{:S(2)}) copy-start(f32[3,16]{1,0:T(4,128)} %rde_ref.1) | copy-start | bytes 580
  23.4 35.9 %copy-start.3 = (f32[16]{0:T(128)S(1)}, f32[16]{0:T(128)}, u32[]{:S(2)}) copy-start(f32[16]{0:T(128)} %cse_ref.1) | copy-start | bytes 196
  24.2 20.0 %all-to-all-start.1 = ((f32[32,24,128]{2,1,0:T(8,128)}), f32[32,24,128]{2,1,0:T(8,128)S(1)}, u32[]{:S(2)}, u32[]{:S(2)}) async-start(f32[32,24,128]{2,1,0:T(8,128)} %reshape.218), calls=%async_computation.1 | async-start | bytes 786432 | tf_op jit(solution)/shard_map/all_to_all | solution.py:139
  50.4 14.7 %all-to-all-start.2 = ((f32[8,80,128]{2,1,0:T(8,128)}), f32[8,80,128]{2,1,0:T(8,128)S(1)}, u32[]{:S(2)}, u32[]{:S(2)}) async-start(f32[8,80,128]{2,1,0:T(8,128)} %broadcast_in_dim.25), calls=%async_computation.2 | async-start | bytes 655360 | tf_op jit(solution)/shard_map/all_to_all | solution.py:164
  73.3 13.4 %all-to-all-start.3 = ((f32[32,5,128]{2,1,0:T(8,128)}), f32[32,5,128]{2,1,0:T(8,128)S(1)}, u32[]{:S(2)}, u32[]{:S(2)}) async-start(f32[32,5,128]{2,1,0:T(8,128)} %pad_maximum_fusion), calls=%async_computation.3 | async-start | bytes 262144 | tf_op jit(solution)/shard_map/all_to_all | solution.py:201
  87.4 10.3 %all-to-all-start.4 = ((f32[8,1,128]{2,1,0:T(1,128)}), f32[8,1,128]{2,1,0:T(1,128)S(1)}, u32[]{:S(2)}, u32[]{:S(2)}) async-start(f32[8,1,128]{2,1,0:T(1,128)} %broadcast_in_dim.59), calls=%async_computation.4 | async-start | bytes 8192 | tf_op jit(solution)/shard_map/all_to_all | solution.py:203

commit v12 on v11

--- a/solution.py
+++ b/solution.py
@@ -188,7 +188,17 @@
     class_part = jnp.einsum(
         "pqc,pck->qk", weighted_fields, class_hot, precision=lax.Precision.HIGHEST
     )
-    mine = jnp.concatenate([class_part.reshape(-1), misfit[None]])
+    prior = (
+        jnp.concatenate([category_sensitivity_effect[None, :], reservoir_decay_effect], axis=0)
+        / PRIOR_VAR
+    )
+    prior_cost = (
+        0.5 * jnp.sum(category_sensitivity_effect * category_sensitivity_effect) / PRIOR_VAR
+        + 0.5 * jnp.sum(reservoir_decay_effect * reservoir_decay_effect) / PRIOR_VAR
+    )
+    first_device = (me_map == 0) & (lax.axis_index("snd") == 0)
+    priors = jnp.where(first_device, jnp.concatenate([prior.reshape(-1), prior_cost[None]]), 0.0)
+    mine = jnp.concatenate([class_part.reshape(-1), misfit[None]]) + priors
     width = mine.shape[0]
     mine = jnp.pad(mine, (0, tile - width))
     parcel = jnp.concatenate(
@@ -212,18 +222,8 @@
     )[:local_ids]
     flux_grad = grad_tiles.reshape(epochs_each_device, locations_each_device)
 
-    class_total = totals[:-1].reshape(4, nclass)
-    total_misfit = totals[-1]
-    prior = (
-        jnp.concatenate([category_sensitivity_effect[None, :], reservoir_decay_effect], axis=0)
-        / PRIOR_VAR
-    )
-    class_grad = class_total + prior
-    cost = (
-        total_misfit
-        + 0.5 * jnp.sum(category_sensitivity_effect * category_sensitivity_effect) / PRIOR_VAR
-        + 0.5 * jnp.sum(reservoir_decay_effect * reservoir_decay_effect) / PRIOR_VAR
-    )
+    class_grad = totals[:-1].reshape(4, nclass)
+    cost = totals[-1]
     return (model_xco2, flux_grad, class_grad, cost)
 
 

time: 101 us -> 100 us (0.990)
  between operations: 4.62 us -> 2.82 us
where the time goes in v12:
time: 100 us; the launch traced here: 99.7 us
  starting transfers between devices  37 us (37%)
  waiting for transfers between devices  30 us (30%)
  local copies, waits for them, and re-layouts  11 us (11%)
  matrix products  9.24 us (9%)
  other arithmetic  7.71 us (8%)
  between operations  2.82 us (3%)
  Pallas kernels  1.97 us (2%)
    all_to_all x1, waiting for transfers between devices, shards(): lax.all_to_all(answer.reshape(n_snd, cap * 6, tile), 'snd', 0, 0)  12.3 us
    all_to_all x1, starting transfers between devices, shards(): requests = lax.all_to_all(lanes, 'snd', 0, 0)[:, 0, :cap]  12 us
    all_to_all x1, waiting for transfers between devices, shards(): incoming = lax.all_to_all(parcel, 'snd', 0, 0)  9.44 us
    all_to_all x1, starting transfers between devices, shards(): lax.all_to_all(answer.reshape(n_snd, cap * 6, tile), 'snd', 0, 0)  7.78 us
    all_to_all x1, starting transfers between devices, shards(): lax.all_to_all(jnp.broadcast_to(payload[None], (n_map,) + payload.shape),...  7.56 us
    all_to_all x1, starting transfers between devices, shards(): lax.all_to_all(jnp.broadcast_to(column[None], (n_map, tile)), 'map', 0, 0)  5.73 us
    all_to_all x1, waiting for transfers between devices, shards(): lax.all_to_all(jnp.broadcast_to(payload[None], (n_map,) + payload.shape),...  4.49 us
    dot_general x1, matrix products, shards(): jnp.einsum('bij,bj->bi', sensitivity_blocks, vectors, preferred_element_t...  4.43 us
  transfers between devices with their start and end apart: 5, of which 5 were waited for; matrix products, arithmetic and copies ran while one was open for 9% of the time, Pallas kernels for 2%

profile of v12, /device:TPU:1, one launch (start us, length us, event | category | flops | bytes accessed | tf_op | source)
XLA Modules:
  0.0 99.7 jit_solution(8649819997328797928)
XLA Ops:
  0.6 0.8 copy.35
  1.4 0.6 pad.8
  2.0 12.0 %all-to-all-start = ((s32[32,1,128]{2,1,0:T(1,128)}), s32[32,1,128]{2,1,0:T(1,128)S(1)}, u32[]{:S(2)}, u32[]{:S(2)}) async-start(s32[32,1,128]{2,1,0:T(1,128)} %bitcast.2), calls=%async_computation | async-start | bytes 32768 | tf_op jit(solution)/shard_map/all_to_all | solution.py:121
  14.1 2.0 %shard_map.138 = f32[6,2,8192]{2,1,0:T(2,128)} custom-call(f32[16]{0:T(128)} %cse_ref.1, f32[3,16]{1,0:T(4,128)} %rde_ref.1, s32[1,8192]{1,0:T(1,128)} %bitcast.93, f32[2,8192]{1,0:T(2,128)} %warm_ref.1, f32[2,8192]{1,0:T(2,128)} %wet_ref.1, f32[3,8192]{1,0:T(4,128)} %carbon_ref.1), custom_call_target="tpu_custom_call" | custom-call | tf_op jit(solution)/shard_map/pallas_call | solution.py:83
  16.0 1.3 %reshape.221 = f32[6,128,128]{2,1,0:T(8,128)S(1)} reshape(f32[6,2,8192]{2,1,0:T(2,128)} %shard_map.138) | data formatting | bytes 786432 | tf_op jit(solution)/shard_map/reshape | solution.py:131
  17.4 0.8 fusion.20
  18.1 0.8 fusion.23
  18.9 0.7 maximum_multiply_fusion
  19.6 0.1 div.38
  19.7 0.8 copy.38
  20.5 0.6 gather_fusion
  21.1 1.5 %all-to-all-done = s32[32,1,128]{2,1,0:T(1,128)S(1)} async-done(((s32[32,1,128]{2,1,0:T(1,128)}), s32[32,1,128]{2,1,0:T(1,128)S(1)}, u32[]{:S(2)}, u32[]{:S(2)}) %all-to-all-start) | async-done | bytes 16416 | tf_op jit(solution)/shard_map/all_to_all | solution.py:121
  22.6 0.1 eq.68
  22.7 0.4 fusion.7
  23.1 0.2 copy.36
  23.4 0.8 reshape.222
  24.2 7.8 %all-to-all-start.1 = ((f32[32,24,128]{2,1,0:T(8,128)}), f32[32,24,128]{2,1,0:T(8,128)S(1)}, u32[]{:S(2)}, u32[]{:S(2)}) async-start(f32[32,24,128]{2,1,0:T(8,128)} %reshape.222), calls=%async_computation.1 | async-start | bytes 786432 | tf_op jit(solution)/shard_map/all_to_all | solution.py:139
  32.0 0.7 iota_reduce_fusion
  32.7 12.3 %all-to-all-done.1 = f32[32,24,128]{2,1,0:T(8,128)S(1)} async-done(((f32[32,24,128]{2,1,0:T(8,128)}), f32[32,24,128]{2,1,0:T(8,128)S(1)}, u32[]{:S(2)}, u32[]{:S(2)}) %all-to-all-start.1) | async-done | bytes 393248 | tf_op jit(solution)/shard_map/all_to_all | solution.py:139
  45.0 0.1 reshape.223
  45.1 0.1 fusion.24
  45.2 0.7 gather_fusion.1
  45.8 4.4 %fusion.4 = f32[128,1,128]{2,1,0:T(1,128)S(1)} fusion(bf16[128,128,128]{2,1,0:T(8,128)(2,1)} %param.11, bf16[128,128,1]{1,0,2:T(8,128)(2,1)S(1)} %bitcast.85), kind=kOutput, calls=%fused_computation.14 | convolution fusion | flops 4194304 | bytes 4292608 | tf_op jit(solution)/shard_map/bij,bj->bi/dot_general | solution.py:153
  50.3 0.2 fusion.16
  50.5 0.7 broadcast_in_dim.59
  51.2 7.6 %all-to-all-start.2 = ((f32[8,80,128]{2,1,0:T(8,128)}), f32[8,80,128]{2,1,0:T(8,128)S(1)}, u32[]{:S(2)}, u32[]{:S(2)}) async-start(f32[8,80,128]{2,1,0:T(8,128)} %broadcast_in_dim.59), calls=%async_computation.2 | async-start | bytes 655360 | tf_op jit(solution)/shard_map/all_to_all | solution.py:164
  58.8 0.6 multiply_reduce_fusion.1
  59.4 0.6 multiply_reduce_fusion
  61.3 0.1 squeeze.25
  61.4 4.5 %all-to-all-done.2 = f32[8,80,128]{2,1,0:T(8,128)S(1)} async-done(((f32[8,80,128]{2,1,0:T(8,128)}), f32[8,80,128]{2,1,0:T(8,128)S(1)}, u32[]{:S(2)}, u32[]{:S(2)}) %all-to-all-start.2) | async-done | bytes 327712 | tf_op jit(solution)/shard_map/all_to_all | solution.py:164
  65.9 0.7 gather_fusion.2
  66.7 3.4 %fusion.2 = f32[128,1,128]{2,1,0:T(1,128)S(1)} fusion(bf16[128,128,128]{2,1,0:T(8,128)(2,1)} %param.11, bf16[128,128,1]{1,0,2:T(8,128)(2,1)S(1)} %bitcast.86), kind=kOutput, calls=%fused_computation.12 | convolution fusion | flops 4194304 | bytes 4292608 | tf_op jit(solution)/shard_map/bij,bi->bj/dot_general | solution.py:177
  70.0 0.6 fusion.11
  71.3 1.0 %scatter_custom_fusion = f32[128,128]{1,0:T(8,128)S(1)} fusion(s32[128]{0:T(128)S(1)} %get-tuple-element.13, f32[128,128]{1,0:T(8,128)S(1)} %bitcast.89, f32[]{:T(128)} %constant.63.clone.1), kind=kCustom, calls=%fused_computation.29 | custom fusion | flops 16384 | bytes 65540 | tf_op jit(solution)/shard_map/scatter-add | solution.py:180
  72.3 0.9 convolution_bitcast_fusion
  73.2 0.1 reshape.227
  73.3 0.1 fusion.18
  73.4 0.7 pad_maximum_fusion
  74.1 3.9 %all-to-all-start.3 = ((f32[32,5,128]{2,1,0:T(8,128)}), f32[32,5,128]{2,1,0:T(8,128)S(1)}, u32[]{:S(2)}, u32[]{:S(2)}) async-start(f32[32,5,128]{2,1,0:T(8,128)} %pad_maximum_fusion), calls=%async_computation.3 | async-start | bytes 262144 | tf_op jit(solution)/shard_map/all_to_all | solution.py:211
  78.1 9.4 %all-to-all-done.3 = f32[32,5,128]{2,1,0:T(8,128)S(1)} async-done(((f32[32,5,128]{2,1,0:T(8,128)}), f32[32,5,128]{2,1,0:T(8,128)S(1)}, u32[]{:S(2)}, u32[]{:S(2)}) %all-to-all-start.3) | async-done | bytes 81952 | tf_op jit(solution)/shard_map/all_to_all | solution.py:211
  87.5 0.6 broadcast_in_dim.69
  88.1 5.7 %all-to-all-start.4 = ((f32[8,1,128]{2,1,0:T(1,128)}), f32[8,1,128]{2,1,0:T(1,128)S(1)}, u32[]{:S(2)}, u32[]{:S(2)}) async-start(f32[8,1,128]{2,1,0:T(1,128)} %broadcast_in_dim.69), calls=%async_computation.4 | async-start | bytes 8192 | tf_op jit(solution)/shard_map/all_to_all | solution.py:213
  93.9 0.6 constant_dynamic-slice_fusion
  94.5 1.0 %scatter_custom_fusion.1 = f32[129,128]{1,0:T(8,128)S(1)} fusion(s32[128]{0:T(128)S(1)} %fusion.22, f32[128,128]{1,0:T(8,128)S(1)} %bitcast.91, f32[]{:T(128)} %constant.63.clone.1), kind=kCustom, calls=%fused_computation.22 | custom fusion | flops 16384 | bytes 66052 | tf_op jit(solution)/shard_map/scatter-add | solution.py:217
  95.5 0.7 reshape.229
  96.2 2.3 %all-to-all-done.4 = f32[8,1,128]{2,1,0:T(1,128)S(1)} async-done(((f32[8,1,128]{2,1,0:T(1,128)}), f32[8,1,128]{2,1,0:T(1,128)S(1)}, u32[]{:S(2)}, u32[]{:S(2)}) %all-to-all-start.4) | async-done | bytes 4128 | tf_op jit(solution)/shard_map/all_to_all | solution.py:213
  98.5 0.6 slice.70
  99.1 0.7 reshape.230
  (26 shorter events, 0.3 us)
Async XLA Ops:
  0.6 32.0 %copy-start.4 = (s32[3,128]{1,0:T(4,128)S(1)}, s32[3,128]{1,0:T(4,128)}, u32[]{:S(2)}) copy-start(s32[3,128]{1,0:T(4,128)} %param.12) | copy-start | bytes 4612
  2.0 20.6 %all-to-all-start = ((s32[32,1,128]{2,1,0:T(1,128)}), s32[32,1,128]{2,1,0:T(1,128)S(1)}, u32[]{:S(2)}, u32[]{:S(2)}) async-start(s32[32,1,128]{2,1,0:T(1,128)} %bitcast.2), calls=%async_computation | async-start | bytes 32768 | tf_op jit(solution)/shard_map/all_to_all | solution.py:121
  23.1 27.4 %copy-start.1 = (f32[8,128]{1,0:T(8,128)S(1)}, f32[8,128]{1,0:T(8,128)}, u32[]{:S(2)}) copy-start(f32[8,128]{1,0:T(8,128)} %param.21) | copy-start | bytes 12292
  23.1 27.4 %copy-start.2 = (f32[8,128]{1,0:T(8,128)S(1)}, f32[8,128]{1,0:T(8,128)}, u32[]{:S(2)}) copy-start(f32[8,128]{1,0:T(8,128)} %param.20) | copy-start | bytes 12292
  23.4 35.4 %copy-start.3 = (f32[16]{0:T(128)S(1)}, f32[16]{0:T(128)}, u32[]{:S(2)}) copy-start(f32[16]{0:T(128)} %cse_ref.1) | copy-start | bytes 196
  23.4 36.0 %copy-start = (f32[3,16]{1,0:T(4,128)S(1)}, f32[3,16]{1,0:T(4,128)}, u32[]{:S(2)}) copy-start(f32[3,16]{1,0:T(4,128)} %rde_ref.1) | copy-start | bytes 580
  24.2 20.8 %all-to-all-start.1 = ((f32[32,24,128]{2,1,0:T(8,128)}), f32[32,24,128]{2,1,0:T(8,128)S(1)}, u32[]{:S(2)}, u32[]{:S(2)}) async-start(f32[32,24,128]{2,1,0:T(8,128)} %reshape.222), calls=%async_computation.1 | async-start | bytes 786432 | tf_op jit(solution)/shard_map/all_to_all | solution.py:139
  51.2 14.7 %all-to-all-start.2 = ((f32[8,80,128]{2,1,0:T(8,128)}), f32[8,80,128]{2,1,0:T(8,128)S(1)}, u32[]{:S(2)}, u32[]{:S(2)}) async-start(f32[8,80,128]{2,1,0:T(8,128)} %broadcast_in_dim.59), calls=%async_computation.2 | async-start | bytes 655360 | tf_op jit(solution)/shard_map/all_to_all | solution.py:164
  74.1 13.4 %all-to-all-start.3 = ((f32[32,5,128]{2,1,0:T(8,128)}), f32[32,5,128]{2,1,0:T(8,128)S(1)}, u32[]{:S(2)}, u32[]{:S(2)}) async-start(f32[32,5,128]{2,1,0:T(8,128)} %pad_maximum_fusion), calls=%async_computation.3 | async-start | bytes 262144 | tf_op jit(solution)/shard_map/all_to_all | solution.py:211
  88.1 10.3 %all-to-all-start.4 = ((f32[8,1,128]{2,1,0:T(1,128)}), f32[8,1,128]{2,1,0:T(1,128)S(1)}, u32[]{:S(2)}, u32[]{:S(2)}) async-start(f32[8,1,128]{2,1,0:T(1,128)} %broadcast_in_dim.69), calls=%async_computation.4 | async-start | bytes 8192 | tf_op jit(solution)/shard_map/all_to_all | solution.py:213

commit v13 on v12

--- a/solution.py
+++ b/solution.py
@@ -8,6 +8,7 @@
 BASELINE_CELSIUS = 15.0
 LOG_BASE_Q = 0.6931471805599453
 PRIOR_VAR = 0.09
+FIELDS = 8
 
 
 def ground_efflux_forward(
@@ -67,6 +68,8 @@
         )
         for q, value in enumerate(fields):
             out_ref[q, t : t + 1, :] = value
+        for q in range(len(fields), out_ref.shape[0]):
+            out_ref[q, t : t + 1, :] = jnp.zeros_like(category)
 
 
 def owner_fields(
@@ -82,7 +85,7 @@
     vmem = pl.BlockSpec(memory_space=pltpu.VMEM)
     return pl.pallas_call(
         _fields_kernel,
-        out_shape=jax.ShapeDtypeStruct((6, epochs, cells), jnp.float32),
+        out_shape=jax.ShapeDtypeStruct((FIELDS, epochs, cells), jnp.float32),
         in_specs=[smem, smem, vmem, vmem, vmem, vmem],
         out_specs=vmem,
     )(
@@ -128,7 +131,7 @@
         location_category,
         category_sensitivity_effect,
         reservoir_decay_effect,
-    ).reshape(6, local_ids, tile)
+    ).reshape(FIELDS, local_ids, tile)
     own_fields, block_placement_table, needed_tile_lists = lax.optimization_barrier(
         (own_fields, block_placement_table, needed_tile_lists)
     )
@@ -136,8 +139,8 @@
         requests.reshape(-1)[:, None] == jnp.arange(local_ids, dtype=jnp.int32)[None, :]
     ).astype(jnp.float32)
     answer = jnp.einsum("rl,qlc->rqc", asked, own_fields, precision=lax.Precision.HIGHEST)
-    received = lax.all_to_all(answer.reshape(n_snd, cap * 6, tile), "snd", 0, 0).reshape(
-        n_snd * cap, 6, tile
+    received = lax.all_to_all(answer.reshape(n_snd, cap * FIELDS, tile), "snd", 0, 0).reshape(
+        n_snd * cap, FIELDS, tile
     )
 
     block_row = block_placement_table[0]

time: 100 us -> 101 us (1.010)
  waiting for transfers between devices: 30 us -> 34.2 us
  starting transfers between devices: 37 us -> 34.8 us
  other arithmetic: 7.71 us -> 6.27 us
    all_to_all x1, starting transfers between devices: 7.78 us -> 5.03 us  [shards(): lax.all_to_all(answer.reshape(n_snd, cap * FIELDS, tile), 'snd', 0, 0)]
    all_to_all x1, waiting for transfers between devices: 1.46 us -> 4.2 us  [shards(): requests = lax.all_to_all(lanes, 'snd', 0, 0)[:, 0, :cap]]
    all_to_all x1, waiting for transfers between devices: 12.3 us -> 13.8 us  [shards(): lax.all_to_all(answer.reshape(n_snd, cap * FIELDS, tile), 'snd', 0, 0)]
  transfers between devices with their start and end apart: 5 -> 5, of which waited for: 5 -> 5; matrix products, arithmetic and copies ran while one was open for 9% -> 7% of each run, Pallas kernels for 2% -> 2%
where the time goes in v13:
time: 101 us; the launch traced here: 99.9 us
  starting transfers between devices  34.8 us (34%)
  waiting for transfers between devices  34.2 us (34%)
  local copies, waits for them, and re-layouts  10.5 us (10%)
  matrix products  9.28 us (9%)
  other arithmetic  6.27 us (6%)
  between operations  2.85 us (3%)
  Pallas kernels  2.03 us (2%)
    all_to_all x1, waiting for transfers between devices, shards(): lax.all_to_all(answer.reshape(n_snd, cap * FIELDS, tile), 'snd', 0, 0)  13.8 us
    all_to_all x1, starting transfers between devices, shards(): requests = lax.all_to_all(lanes, 'snd', 0, 0)[:, 0, :cap]  12 us
    all_to_all x1, waiting for transfers between devices, shards(): incoming = lax.all_to_all(parcel, 'snd', 0, 0)  9.44 us
    all_to_all x1, starting transfers between devices, shards(): lax.all_to_all(jnp.broadcast_to(payload[None], (n_map,) + payload.shape),...  7.67 us
    all_to_all x1, starting transfers between devices, shards(): lax.all_to_all(jnp.broadcast_to(column[None], (n_map, tile)), 'map', 0, 0)  5.73 us
    all_to_all x1, starting transfers between devices, shards(): lax.all_to_all(answer.reshape(n_snd, cap * FIELDS, tile), 'snd', 0, 0)  5.03 us
    all_to_all x1, waiting for transfers between devices, shards(): lax.all_to_all(jnp.broadcast_to(payload[None], (n_map,) + payload.shape),...  4.5 us
    dot_general x1, matrix products, shards(): jnp.einsum('bij,bj->bi', sensitivity_blocks, vectors, preferred_element_t...  4.43 us
  transfers between devices with their start and end apart: 5, of which 5 were waited for; matrix products, arithmetic and copies ran while one was open for 7% of the time, Pallas kernels for 2%

profile of v13, /device:TPU:1, one launch (start us, length us, event | category | flops | bytes accessed | tf_op | source)
XLA Modules:
  0.0 99.9 jit_solution(1072082874438845574)
XLA Ops:
  0.6 0.0 copy-start
  0.7 0.0 copy-start.5
  0.7 0.8 copy.35
  1.5 0.6 pad.8
  2.1 12.0 %all-to-all-start = ((s32[32,1,128]{2,1,0:T(1,128)}), s32[32,1,128]{2,1,0:T(1,128)S(1)}, u32[]{:S(2)}, u32[]{:S(2)}) async-start(s32[32,1,128]{2,1,0:T(1,128)} %bitcast.2), calls=%async_computation | async-start | bytes 32768 | tf_op jit(solution)/shard_map/all_to_all | solution.py:124
  14.1 2.0 %shard_map.138 = f32[8,2,8192]{2,1,0:T(2,128)} custom-call(f32[16]{0:T(128)} %cse_ref.1, f32[3,16]{1,0:T(4,128)} %rde_ref.1, s32[1,8192]{1,0:T(1,128)} %bitcast.97, f32[2,8192]{1,0:T(2,128)} %warm_ref.1, f32[2,8192]{1,0:T(2,128)} %wet_ref.1, f32[3,8192]{1,0:T(4,128)} %carbon_ref.1), custom_call_target="tpu_custom_call" | custom-call | tf_op jit(solution)/shard_map/pallas_call | solution.py:86
  16.1 1.5 %reshape.221 = f32[8,128,128]{2,1,0:T(8,128)S(1)} reshape(f32[8,2,8192]{2,1,0:T(2,128)} %shard_map.138) | data formatting | bytes 1048576 | tf_op jit(solution)/shard_map/reshape | solution.py:134
  17.6 0.8 fusion.23
  18.4 4.2 %all-to-all-done = s32[32,1,128]{2,1,0:T(1,128)S(1)} async-done(((s32[32,1,128]{2,1,0:T(1,128)}), s32[32,1,128]{2,1,0:T(1,128)S(1)}, u32[]{:S(2)}, u32[]{:S(2)}) %all-to-all-start) | async-done | bytes 16416 | tf_op jit(solution)/shard_map/all_to_all | solution.py:124
  22.6 0.1 fusion.25
  22.7 0.1 eq.68
  22.8 0.4 fusion.7
  23.2 1.1 %copy.36 = f32[128,8,128]{2,1,0:T(8,128)} copy(f32[128,8,128]{2,0,1:T(8,128)S(1)} %fusion.7) | data formatting | bytes 1048576 | tf_op jit(solution)/shard_map/rl,qlc->rqc/dot_general | solution.py:141
  24.3 5.0 %all-to-all-start.1 = ((f32[32,32,128]{2,1,0:T(8,128)}), f32[32,32,128]{2,1,0:T(8,128)S(1)}, u32[]{:S(2)}, u32[]{:S(2)}) async-start(f32[32,32,128]{2,1,0:T(8,128)} %bitcast.4), calls=%async_computation.1 | async-start | bytes 1048576 | tf_op jit(solution)/shard_map/all_to_all | solution.py:142
  29.4 0.1 div.38
  29.5 0.1 copy.38
  29.6 0.6 gather_fusion
  30.3 0.7 iota_reduce_fusion
  31.0 13.8 %all-to-all-done.1 = f32[32,32,128]{2,1,0:T(8,128)S(1)} async-done(((f32[32,32,128]{2,1,0:T(8,128)}), f32[32,32,128]{2,1,0:T(8,128)S(1)}, u32[]{:S(2)}, u32[]{:S(2)}) %all-to-all-start.1) | async-done | bytes 524320 | tf_op jit(solution)/shard_map/all_to_all | solution.py:142
  44.8 0.1 fusion.24
  44.9 0.6 gather_fusion.1
  45.5 4.4 %fusion.4 = f32[128,1,128]{2,1,0:T(1,128)S(1)} fusion(bf16[128,128,128]{2,1,0:T(8,128)(2,1)} %param.11, bf16[128,128,1]{1,0,2:T(8,128)(2,1)S(1)} %bitcast.89), kind=kOutput, calls=%fused_computation.14 | convolution fusion | flops 4194304 | bytes 4292608 | tf_op jit(solution)/shard_map/bij,bj->bi/dot_general | solution.py:156
  49.9 0.2 fusion.16
  50.2 0.7 broadcast_in_dim.59
  50.9 7.7 %all-to-all-start.2 = ((f32[8,80,128]{2,1,0:T(8,128)}), f32[8,80,128]{2,1,0:T(8,128)S(1)}, u32[]{:S(2)}, u32[]{:S(2)}) async-start(f32[8,80,128]{2,1,0:T(8,128)} %broadcast_in_dim.59), calls=%async_computation.2 | async-start | bytes 655360 | tf_op jit(solution)/shard_map/all_to_all | solution.py:167
  58.6 0.6 multiply_reduce_fusion.1
  59.2 0.6 multiply_reduce_fusion
  61.1 0.1 squeeze.25
  61.2 4.5 %all-to-all-done.2 = f32[8,80,128]{2,1,0:T(8,128)S(1)} async-done(((f32[8,80,128]{2,1,0:T(8,128)}), f32[8,80,128]{2,1,0:T(8,128)S(1)}, u32[]{:S(2)}, u32[]{:S(2)}) %all-to-all-start.2) | async-done | bytes 327712 | tf_op jit(solution)/shard_map/all_to_all | solution.py:167
  65.7 0.7 gather_fusion.2
  66.4 3.4 %fusion.2 = f32[128,1,128]{2,1,0:T(1,128)S(1)} fusion(bf16[128,128,128]{2,1,0:T(8,128)(2,1)} %param.11, bf16[128,128,1]{1,0,2:T(8,128)(2,1)S(1)} %bitcast.90), kind=kOutput, calls=%fused_computation.12 | convolution fusion | flops 4194304 | bytes 4292608 | tf_op jit(solution)/shard_map/bij,bi->bj/dot_general | solution.py:180
  69.8 0.6 fusion.11
  71.1 1.0 %scatter_custom_fusion = f32[128,128]{1,0:T(8,128)S(1)} fusion(s32[128]{0:T(128)S(1)} %get-tuple-element.13, f32[128,128]{1,0:T(8,128)S(1)} %bitcast.93, f32[]{:T(128)} %constant.63.clone.1), kind=kCustom, calls=%fused_computation.29 | custom fusion | flops 16384 | bytes 65540 | tf_op jit(solution)/shard_map/scatter-add | solution.py:183
  72.1 0.9 convolution_bitcast_fusion
  73.0 0.1 reshape.227
  73.1 0.1 fusion.18
  73.2 0.7 pad_maximum_fusion
  73.9 4.3 %all-to-all-start.3 = ((f32[32,5,128]{2,1,0:T(8,128)}), f32[32,5,128]{2,1,0:T(8,128)S(1)}, u32[]{:S(2)}, u32[]{:S(2)}) async-start(f32[32,5,128]{2,1,0:T(8,128)} %pad_maximum_fusion), calls=%async_computation.3 | async-start | bytes 262144 | tf_op jit(solution)/shard_map/all_to_all | solution.py:214
  78.2 9.4 %all-to-all-done.3 = f32[32,5,128]{2,1,0:T(8,128)S(1)} async-done(((f32[32,5,128]{2,1,0:T(8,128)}), f32[32,5,128]{2,1,0:T(8,128)S(1)}, u32[]{:S(2)}, u32[]{:S(2)}) %all-to-all-start.3) | async-done | bytes 81952 | tf_op jit(solution)/shard_map/all_to_all | solution.py:214
  87.6 0.1 slice_reduce_fusion.1
  87.7 0.6 broadcast_in_dim.69
  88.3 5.7 %all-to-all-start.4 = ((f32[8,1,128]{2,1,0:T(1,128)}), f32[8,1,128]{2,1,0:T(1,128)S(1)}, u32[]{:S(2)}, u32[]{:S(2)}) async-start(f32[8,1,128]{2,1,0:T(1,128)} %broadcast_in_dim.69), calls=%async_computation.4 | async-start | bytes 8192 | tf_op jit(solution)/shard_map/all_to_all | solution.py:216
  94.0 0.6 constant_dynamic-slice_fusion
  94.6 1.0 %scatter_custom_fusion.1 = f32[129,128]{1,0:T(8,128)S(1)} fusion(s32[128]{0:T(128)S(1)} %fusion.22, f32[128,128]{1,0:T(8,128)S(1)} %bitcast.95, f32[]{:T(128)} %constant.63.clone.1), kind=kCustom, calls=%fused_computation.22 | custom fusion | flops 16384 | bytes 66052 | tf_op jit(solution)/shard_map/scatter-add | solution.py:220
  95.7 0.7 reshape.229
  96.3 2.3 %all-to-all-done.4 = f32[8,1,128]{2,1,0:T(1,128)S(1)} async-done(((f32[8,1,128]{2,1,0:T(1,128)}), f32[8,1,128]{2,1,0:T(1,128)S(1)}, u32[]{:S(2)}, u32[]{:S(2)}) %all-to-all-start.4) | async-done | bytes 4128 | tf_op jit(solution)/shard_map/all_to_all | solution.py:216
  98.6 0.6 slice.70
  99.2 0.7 reshape.230
  (26 shorter events, 0.2 us)
Async XLA Ops:
  0.6 28.9 %copy-start.1 = (s32[32,4]{0,1:T(4,128)S(1)}, s32[32,4]{0,1:T(4,128)}, u32[]{:S(2)}) copy-start(s32[32,4]{0,1:T(4,128)} %param.13) | copy-start | bytes 1540
  0.6 28.7 %copy-start = (f32[3,16]{1,0:T(4,128)S(1)}, f32[3,16]{1,0:T(4,128)}, u32[]{:S(2)}) copy-start(f32[3,16]{1,0:T(4,128)} %rde_ref.1) | copy-start | bytes 580
  0.7 28.7 %copy-start.4 = (f32[16]{0:T(128)S(1)}, f32[16]{0:T(128)}, u32[]{:S(2)}) copy-start(f32[16]{0:T(128)} %cse_ref.1) | copy-start | bytes 196
  0.7 29.6 %copy-start.5 = (s32[3,128]{1,0:T(4,128)S(1)}, s32[3,128]{1,0:T(4,128)}, u32[]{:S(2)}) copy-start(s32[3,128]{1,0:T(4,128)} %param.12) | copy-start | bytes 4612
  2.1 20.6 %all-to-all-start = ((s32[32,1,128]{2,1,0:T(1,128)}), s32[32,1,128]{2,1,0:T(1,128)S(1)}, u32[]{:S(2)}, u32[]{:S(2)}) async-start(s32[32,1,128]{2,1,0:T(1,128)} %bitcast.2), calls=%async_computation | async-start | bytes 32768 | tf_op jit(solution)/shard_map/all_to_all | solution.py:124
  22.8 27.3 %copy-start.2 = (f32[8,128]{1,0:T(8,128)S(1)}, f32[8,128]{1,0:T(8,128)}, u32[]{:S(2)}) copy-start(f32[8,128]{1,0:T(8,128)} %param.21) | copy-start | bytes 12292
  22.8 27.3 %copy-start.3 = (f32[8,128]{1,0:T(8,128)S(1)}, f32[8,128]{1,0:T(8,128)}, u32[]{:S(2)}) copy-start(f32[8,128]{1,0:T(8,128)} %param.20) | copy-start | bytes 12292
  24.3 20.4 %all-to-all-start.1 = ((f32[32,32,128]{2,1,0:T(8,128)}), f32[32,32,128]{2,1,0:T(8,128)S(1)}, u32[]{:S(2)}, u32[]{:S(2)}) async-start(f32[32,32,128]{2,1,0:T(8,128)} %bitcast.4), calls=%async_computation.1 | async-start | bytes 1048576 | tf_op jit(solution)/shard_map/all_to_all | solution.py:142
  50.9 14.8 %all-to-all-start.2 = ((f32[8,80,128]{2,1,0:T(8,128)}), f32[8,80,128]{2,1,0:T(8,128)S(1)}, u32[]{:S(2)}, u32[]{:S(2)}) async-start(f32[8,80,128]{2,1,0:T(8,128)} %broadcast_in_dim.59), calls=%async_computation.2 | async-start | bytes 655360 | tf_op jit(solution)/shard_map/all_to_all | solution.py:167
  73.9 13.7 %all-to-all-start.3 = ((f32[32,5,128]{2,1,0:T(8,128)}), f32[32,5,128]{2,1,0:T(8,128)S(1)}, u32[]{:S(2)}, u32[]{:S(2)}) async-start(f32[32,5,128]{2,1,0:T(8,128)} %pad_maximum_fusion), calls=%async_computation.3 | async-start | bytes 262144 | tf_op jit(solution)/shard_map/all_to_all | solution.py:214
  88.3 10.3 %all-to-all-start.4 = ((f32[8,1,128]{2,1,0:T(1,128)}), f32[8,1,128]{2,1,0:T(1,128)S(1)}, u32[]{:S(2)}, u32[]{:S(2)}) async-start(f32[8,1,128]{2,1,0:T(1,128)} %broadcast_in_dim.69), calls=%async_computation.4 | async-start | bytes 8192 | tf_op jit(solution)/shard_map/all_to_all | solution.py:216

commit v14 on v12

--- a/solution.py
+++ b/solution.py
@@ -129,13 +129,13 @@
         category_sensitivity_effect,
         reservoir_decay_effect,
     ).reshape(6, local_ids, tile)
-    own_fields, block_placement_table, needed_tile_lists = lax.optimization_barrier(
-        (own_fields, block_placement_table, needed_tile_lists)
-    )
     asked = (
         requests.reshape(-1)[:, None] == jnp.arange(local_ids, dtype=jnp.int32)[None, :]
     ).astype(jnp.float32)
     answer = jnp.einsum("rl,qlc->rqc", asked, own_fields, precision=lax.Precision.HIGHEST)
+    answer, block_placement_table, needed_tile_lists = lax.optimization_barrier(
+        (answer, block_placement_table, needed_tile_lists)
+    )
     received = lax.all_to_all(answer.reshape(n_snd, cap * 6, tile), "snd", 0, 0).reshape(
         n_snd * cap, 6, tile
     )

time: 100 us -> 99.9 us (level)
  starting transfers between devices: 37 us -> 34.2 us
  waiting for transfers between devices: 30 us -> 32.3 us
    all_to_all x1, waiting for transfers between devices: 1.46 us -> 4.42 us  [shards(): requests = lax.all_to_all(lanes, 'snd', 0, 0)[:, 0, :cap]]
    all_to_all x1, starting transfers between devices: 7.78 us -> 4.95 us  [shards(): lax.all_to_all(answer.reshape(n_snd, cap * 6, tile), 'snd', 0, 0)]
  transfers between devices with their start and end apart: 5 -> 5, of which waited for: 5 -> 5; matrix products, arithmetic and copies ran while one was open for 9% -> 7% of each run, Pallas kernels for 2% -> 2%
where the time goes in v14:
time: 99.9 us; the launch traced here: 99.2 us
  starting transfers between devices  34.2 us (34%)
  waiting for transfers between devices  32.3 us (32%)
  local copies, waits for them, and re-layouts  11 us (11%)
  matrix products  9.24 us (9%)
  other arithmetic  7.7 us (8%)
  between operations  2.81 us (3%)
  Pallas kernels  1.97 us (2%)
    all_to_all x1, starting transfers between devices, shards(): requests = lax.all_to_all(lanes, 'snd', 0, 0)[:, 0, :cap]  12 us
    all_to_all x1, waiting for transfers between devices, shards(): lax.all_to_all(answer.reshape(n_snd, cap * 6, tile), 'snd', 0, 0)  11.7 us
    all_to_all x1, waiting for transfers between devices, shards(): incoming = lax.all_to_all(parcel, 'snd', 0, 0)  9.44 us
    all_to_all x1, starting transfers between devices, shards(): lax.all_to_all(jnp.broadcast_to(payload[None], (n_map,) + payload.shape),...  7.58 us
    all_to_all x1, starting transfers between devices, shards(): lax.all_to_all(jnp.broadcast_to(column[None], (n_map, tile)), 'map', 0, 0)  5.73 us
    all_to_all x1, starting transfers between devices, shards(): lax.all_to_all(answer.reshape(n_snd, cap * 6, tile), 'snd', 0, 0)  4.95 us
    all_to_all x1, waiting for transfers between devices, shards(): lax.all_to_all(jnp.broadcast_to(payload[None], (n_map,) + payload.shape),...  4.49 us
    dot_general x1, matrix products, shards(): jnp.einsum('bij,bj->bi', sensitivity_blocks, vectors, preferred_element_t...  4.43 us
  transfers between devices with their start and end apart: 5, of which 5 were waited for; matrix products, arithmetic and copies ran while one was open for 7% of the time, Pallas kernels for 2%

profile of v14, /device:TPU:1, one launch (start us, length us, event | category | flops | bytes accessed | tf_op | source)
XLA Modules:
  0.0 99.2 jit_solution(13141197778011378582)
XLA Ops:
  0.6 0.8 copy.35
  1.4 0.6 pad.8
  2.0 12.0 %all-to-all-start = ((s32[32,1,128]{2,1,0:T(1,128)}), s32[32,1,128]{2,1,0:T(1,128)S(1)}, u32[]{:S(2)}, u32[]{:S(2)}) async-start(s32[32,1,128]{2,1,0:T(1,128)} %bitcast), calls=%async_computation | async-start | bytes 32768 | tf_op jit(solution)/shard_map/all_to_all | solution.py:121
  14.1 0.7 maximum_multiply_fusion
  14.8 0.1 div.38
  14.8 2.0 %shard_map.138 = f32[6,2,8192]{2,1,0:T(2,128)} custom-call(f32[16]{0:T(128)} %cse_ref.1, f32[3,16]{1,0:T(4,128)} %rde_ref.1, s32[1,8192]{1,0:T(1,128)} %bitcast.93, f32[2,8192]{1,0:T(2,128)} %warm_ref.1, f32[2,8192]{1,0:T(2,128)} %wet_ref.1, f32[3,8192]{1,0:T(4,128)} %carbon_ref.1), custom_call_target="tpu_custom_call" | custom-call | tf_op jit(solution)/shard_map/pallas_call | solution.py:83
  16.8 1.3 %reshape.221 = f32[6,128,128]{2,1,0:T(8,128)S(1)} reshape(f32[6,2,8192]{2,1,0:T(2,128)} %shard_map.138) | data formatting | bytes 786432 | tf_op jit(solution)/shard_map/reshape | solution.py:131
  18.2 4.4 %all-to-all-done = s32[32,1,128]{2,1,0:T(1,128)S(1)} async-done(((s32[32,1,128]{2,1,0:T(1,128)}), s32[32,1,128]{2,1,0:T(1,128)S(1)}, u32[]{:S(2)}, u32[]{:S(2)}) %all-to-all-start) | async-done | bytes 16416 | tf_op jit(solution)/shard_map/all_to_all | solution.py:121
  22.6 0.1 eq.65
  22.7 0.4 fusion.7
  23.1 0.8 fusion.20
  23.9 0.8 fusion.23
  24.7 0.8 copy.38
  25.4 0.2 copy.36
  25.7 0.8 reshape.222
  26.5 4.9 %all-to-all-start.1 = ((f32[32,24,128]{2,1,0:T(8,128)}), f32[32,24,128]{2,1,0:T(8,128)S(1)}, u32[]{:S(2)}, u32[]{:S(2)}) async-start(f32[32,24,128]{2,1,0:T(8,128)} %reshape.222), calls=%async_computation.1 | async-start | bytes 786432 | tf_op jit(solution)/shard_map/all_to_all | solution.py:139
  31.4 0.6 gather_fusion
  32.1 0.7 iota_reduce_fusion
  32.8 11.7 %all-to-all-done.1 = f32[32,24,128]{2,1,0:T(8,128)S(1)} async-done(((f32[32,24,128]{2,1,0:T(8,128)}), f32[32,24,128]{2,1,0:T(8,128)S(1)}, u32[]{:S(2)}, u32[]{:S(2)}) %all-to-all-start.1) | async-done | bytes 393248 | tf_op jit(solution)/shard_map/all_to_all | solution.py:139
  44.5 0.1 reshape.223
  44.5 0.1 fusion.24
  44.7 0.7 gather_fusion.1
  45.3 4.4 %fusion.4 = f32[128,1,128]{2,1,0:T(1,128)S(1)} fusion(bf16[128,128,128]{2,1,0:T(8,128)(2,1)} %param.11, bf16[128,128,1]{1,0,2:T(8,128)(2,1)S(1)} %bitcast.85), kind=kOutput, calls=%fused_computation.14 | convolution fusion | flops 4194304 | bytes 4292608 | tf_op jit(solution)/shard_map/bij,bj->bi/dot_general | solution.py:153
  49.7 0.2 fusion.16
  50.0 0.7 broadcast_in_dim.59
  50.7 7.6 %all-to-all-start.2 = ((f32[8,80,128]{2,1,0:T(8,128)}), f32[8,80,128]{2,1,0:T(8,128)S(1)}, u32[]{:S(2)}, u32[]{:S(2)}) async-start(f32[8,80,128]{2,1,0:T(8,128)} %broadcast_in_dim.59), calls=%async_computation.2 | async-start | bytes 655360 | tf_op jit(solution)/shard_map/all_to_all | solution.py:164
  58.3 0.6 multiply_reduce_fusion.1
  58.9 0.6 multiply_reduce_fusion
  60.8 0.1 squeeze.25
  60.9 4.5 %all-to-all-done.2 = f32[8,80,128]{2,1,0:T(8,128)S(1)} async-done(((f32[8,80,128]{2,1,0:T(8,128)}), f32[8,80,128]{2,1,0:T(8,128)S(1)}, u32[]{:S(2)}, u32[]{:S(2)}) %all-to-all-start.2) | async-done | bytes 327712 | tf_op jit(solution)/shard_map/all_to_all | solution.py:164
  65.4 0.7 gather_fusion.2
  66.1 3.4 %fusion.2 = f32[128,1,128]{2,1,0:T(1,128)S(1)} fusion(bf16[128,128,128]{2,1,0:T(8,128)(2,1)} %param.11, bf16[128,128,1]{1,0,2:T(8,128)(2,1)S(1)} %bitcast.86), kind=kOutput, calls=%fused_computation.12 | convolution fusion | flops 4194304 | bytes 4292608 | tf_op jit(solution)/shard_map/bij,bi->bj/dot_general | solution.py:177
  69.5 0.6 fusion.11
  70.8 1.0 %scatter_custom_fusion = f32[128,128]{1,0:T(8,128)S(1)} fusion(s32[128]{0:T(128)S(1)} %get-tuple-element.13, f32[128,128]{1,0:T(8,128)S(1)} %bitcast.89, f32[]{:T(128)} %constant.63.clone.1), kind=kCustom, calls=%fused_computation.29 | custom fusion | flops 16384 | bytes 65540 | tf_op jit(solution)/shard_map/scatter-add | solution.py:180
  71.8 0.9 convolution_bitcast_fusion
  72.7 0.1 reshape.227
  72.8 0.1 fusion.18
  72.9 0.7 pad_maximum_fusion
  73.6 3.9 %all-to-all-start.3 = ((f32[32,5,128]{2,1,0:T(8,128)}), f32[32,5,128]{2,1,0:T(8,128)S(1)}, u32[]{:S(2)}, u32[]{:S(2)}) async-start(f32[32,5,128]{2,1,0:T(8,128)} %pad_maximum_fusion), calls=%async_computation.3 | async-start | bytes 262144 | tf_op jit(solution)/shard_map/all_to_all | solution.py:211
  77.5 9.4 %all-to-all-done.3 = f32[32,5,128]{2,1,0:T(8,128)S(1)} async-done(((f32[32,5,128]{2,1,0:T(8,128)}), f32[32,5,128]{2,1,0:T(8,128)S(1)}, u32[]{:S(2)}, u32[]{:S(2)}) %all-to-all-start.3) | async-done | bytes 81952 | tf_op jit(solution)/shard_map/all_to_all | solution.py:211
  87.0 0.6 broadcast_in_dim.69
  87.6 5.7 %all-to-all-start.4 = ((f32[8,1,128]{2,1,0:T(1,128)}), f32[8,1,128]{2,1,0:T(1,128)S(1)}, u32[]{:S(2)}, u32[]{:S(2)}) async-start(f32[8,1,128]{2,1,0:T(1,128)} %broadcast_in_dim.69), calls=%async_computation.4 | async-start | bytes 8192 | tf_op jit(solution)/shard_map/all_to_all | solution.py:213
  93.4 0.6 constant_dynamic-slice_fusion
  94.0 1.0 %scatter_custom_fusion.1 = f32[129,128]{1,0:T(8,128)S(1)} fusion(s32[128]{0:T(128)S(1)} %fusion.22, f32[128,128]{1,0:T(8,128)S(1)} %bitcast.91, f32[]{:T(128)} %constant.63.clone.1), kind=kCustom, calls=%fused_computation.22 | custom fusion | flops 16384 | bytes 66052 | tf_op jit(solution)/shard_map/scatter-add | solution.py:217
  95.0 0.7 reshape.229
  95.7 2.3 %all-to-all-done.4 = f32[8,1,128]{2,1,0:T(1,128)S(1)} async-done(((f32[8,1,128]{2,1,0:T(1,128)}), f32[8,1,128]{2,1,0:T(1,128)S(1)}, u32[]{:S(2)}, u32[]{:S(2)}) %all-to-all-start.4) | async-done | bytes 4128 | tf_op jit(solution)/shard_map/all_to_all | solution.py:213
  98.0 0.6 slice.70
  98.6 0.7 reshape.230
  (26 shorter events, 0.3 us)
Async XLA Ops:
  0.6 32.2 %copy-start.4 = (s32[3,128]{1,0:T(4,128)S(1)}, s32[3,128]{1,0:T(4,128)}, u32[]{:S(2)}) copy-start(s32[3,128]{1,0:T(4,128)} %param.12) | copy-start | bytes 4612
  2.0 20.6 %all-to-all-start = ((s32[32,1,128]{2,1,0:T(1,128)}), s32[32,1,128]{2,1,0:T(1,128)S(1)}, u32[]{:S(2)}, u32[]{:S(2)}) async-start(s32[32,1,128]{2,1,0:T(1,128)} %bitcast), calls=%async_computation | async-start | bytes 32768 | tf_op jit(solution)/shard_map/all_to_all | solution.py:121
  25.7 24.3 %copy-start.1 = (f32[8,128]{1,0:T(8,128)S(1)}, f32[8,128]{1,0:T(8,128)}, u32[]{:S(2)}) copy-start(f32[8,128]{1,0:T(8,128)} %param.21) | copy-start | bytes 12292
  25.7 24.3 %copy-start.2 = (f32[8,128]{1,0:T(8,128)S(1)}, f32[8,128]{1,0:T(8,128)}, u32[]{:S(2)}) copy-start(f32[8,128]{1,0:T(8,128)} %param.20) | copy-start | bytes 12292
  26.5 31.8 %copy-start.3 = (f32[16]{0:T(128)S(1)}, f32[16]{0:T(128)}, u32[]{:S(2)}) copy-start(f32[16]{0:T(128)} %cse_ref.1) | copy-start | bytes 196
  26.5 32.4 %copy-start = (f32[3,16]{1,0:T(4,128)S(1)}, f32[3,16]{1,0:T(4,128)}, u32[]{:S(2)}) copy-start(f32[3,16]{1,0:T(4,128)} %rde_ref.1) | copy-start | bytes 580
  26.5 18.0 %all-to-all-start.1 = ((f32[32,24,128]{2,1,0:T(8,128)}), f32[32,24,128]{2,1,0:T(8,128)S(1)}, u32[]{:S(2)}, u32[]{:S(2)}) async-start(f32[32,24,128]{2,1,0:T(8,128)} %reshape.222), calls=%async_computation.1 | async-start | bytes 786432 | tf_op jit(solution)/shard_map/all_to_all | solution.py:139
  50.7 14.7 %all-to-all-start.2 = ((f32[8,80,128]{2,1,0:T(8,128)}), f32[8,80,128]{2,1,0:T(8,128)S(1)}, u32[]{:S(2)}, u32[]{:S(2)}) async-start(f32[8,80,128]{2,1,0:T(8,128)} %broadcast_in_dim.59), calls=%async_computation.2 | async-start | bytes 655360 | tf_op jit(solution)/shard_map/all_to_all | solution.py:164
  73.6 13.4 %all-to-all-start.3 = ((f32[32,5,128]{2,1,0:T(8,128)}), f32[32,5,128]{2,1,0:T(8,128)S(1)}, u32[]{:S(2)}, u32[]{:S(2)}) async-start(f32[32,5,128]{2,1,0:T(8,128)} %pad_maximum_fusion), calls=%async_computation.3 | async-start | bytes 262144 | tf_op jit(solution)/shard_map/all_to_all | solution.py:211
  87.6 10.3 %all-to-all-start.4 = ((f32[8,1,128]{2,1,0:T(1,128)}), f32[8,1,128]{2,1,0:T(1,128)S(1)}, u32[]{:S(2)}, u32[]{:S(2)}) async-start(f32[8,1,128]{2,1,0:T(1,128)} %broadcast_in_dim.69), calls=%async_computation.4 | async-start | bytes 8192 | tf_op jit(solution)/shard_map/all_to_all | solution.py:213

commit v15 on v14

--- a/solution.py
+++ b/solution.py
@@ -197,21 +197,31 @@
         + 0.5 * jnp.sum(reservoir_decay_effect * reservoir_decay_effect) / PRIOR_VAR
     )
     first_device = (me_map == 0) & (lax.axis_index("snd") == 0)
-    priors = jnp.where(first_device, jnp.concatenate([prior.reshape(-1), prior_cost[None]]), 0.0)
-    mine = jnp.concatenate([class_part.reshape(-1), misfit[None]]) + priors
-    width = mine.shape[0]
-    mine = jnp.pad(mine, (0, tile - width))
+    class_rows = class_part + jnp.where(first_device, prior, 0.0)
+    cost_part = misfit + jnp.where(first_device, prior_cost, 0.0)
+    mine = jnp.concatenate(
+        [
+            jnp.pad(class_rows, ((0, 0), (0, tile - nclass))),
+            jnp.pad(cost_part[None, None], ((0, 0), (0, tile - 1))),
+        ],
+        axis=0,
+    )
+    sums = mine.shape[0]
     parcel = jnp.concatenate(
         [
             outgoing.reshape(n_snd, cap, tile),
-            jnp.broadcast_to(mine[None, None], (n_snd, 1, tile)),
+            jnp.broadcast_to(mine[None], (n_snd, sums, tile)),
         ],
         axis=1,
     )
     incoming = lax.all_to_all(parcel, "snd", 0, 0)
-    column = jnp.sum(incoming[:, cap], axis=0)
-    gathered = lax.all_to_all(jnp.broadcast_to(column[None], (n_map, tile)), "map", 0, 0)
-    totals = jnp.sum(gathered, axis=0)[:width]
+    column = jnp.sum(incoming[:, cap:], axis=0)
+    gathered = lax.all_to_all(
+        jnp.broadcast_to(column[None], (n_map, sums, tile)), "map", 0, 0
+    )
+    totals = jnp.sum(gathered, axis=0)
+    class_grad = totals[: sums - 1, :nclass]
+    cost = totals[sums - 1, 0]
 
     target = jnp.where(live, requests, local_ids).reshape(-1)
     grad_tiles = jax.ops.segment_sum(
@@ -222,8 +232,6 @@
     )[:local_ids]
     flux_grad = grad_tiles.reshape(epochs_each_device, locations_each_device)
 
-    class_grad = totals[:-1].reshape(4, nclass)
-    cost = totals[-1]
     return (model_xco2, flux_grad, class_grad, cost)
 
 

time: 99.9 us -> 101 us (1.011)
  waiting for transfers between devices: 32.3 us -> 34 us
  transfers between devices with their start and end apart: 5 -> 5, of which waited for: 5 -> 5; matrix products, arithmetic and copies ran while one was open for 7% -> 6% of each run, Pallas kernels for 2% -> 2%
where the time goes in v15:
time: 101 us; the launch traced here: 100 us
  starting transfers between devices  34.6 us (34%)
  waiting for transfers between devices  34 us (34%)
  local copies, waits for them, and re-layouts  10.7 us (11%)
  matrix products  9.27 us (9%)
  other arithmetic  6.97 us (7%)
  between operations  2.84 us (3%)
  Pallas kernels  1.97 us (2%)
    all_to_all x1, starting transfers between devices, shards(): requests = lax.all_to_all(lanes, 'snd', 0, 0)[:, 0, :cap]  12 us
    all_to_all x1, waiting for transfers between devices, shards(): lax.all_to_all(answer.reshape(n_snd, cap * 6, tile), 'snd', 0, 0)  11.5 us
    all_to_all x1, waiting for transfers between devices, shards(): incoming = lax.all_to_all(parcel, 'snd', 0, 0)  10.3 us
    all_to_all x1, starting transfers between devices, shards(): lax.all_to_all(jnp.broadcast_to(payload[None], (n_map,) + payload.shape),...  7.66 us
    all_to_all x1, starting transfers between devices, shards(): lax.all_to_all(jnp.broadcast_to(column[None], (n_map, sums, tile)), 'map'...  6.65 us
    all_to_all x1, waiting for transfers between devices, shards(): requests = lax.all_to_all(lanes, 'snd', 0, 0)[:, 0, :cap]  5.19 us
    all_to_all x1, waiting for transfers between devices, shards(): lax.all_to_all(jnp.broadcast_to(payload[None], (n_map,) + payload.shape),...  4.59 us
    dot_general x1, matrix products, shards(): jnp.einsum('bij,bj->bi', sensitivity_blocks, vectors, preferred_element_t...  4.43 us
  transfers between devices with their start and end apart: 5, of which 5 were waited for; matrix products, arithmetic and copies ran while one was open for 6% of the time, Pallas kernels for 2%

profile of v15, /device:TPU:1, one launch (start us, length us, event | category | flops | bytes accessed | tf_op | source)
XLA Modules:
  0.0 100.3 jit_solution(9797496689061110464)
XLA Ops:
  0.6 0.0 copy-start.3
  0.6 0.8 copy.35
  1.4 0.6 pad.12
  2.0 12.0 %all-to-all-start = ((s32[32,1,128]{2,1,0:T(1,128)}), s32[32,1,128]{2,1,0:T(1,128)S(1)}, u32[]{:S(2)}, u32[]{:S(2)}) async-start(s32[32,1,128]{2,1,0:T(1,128)} %bitcast), calls=%async_computation | async-start | bytes 32768 | tf_op jit(solution)/shard_map/all_to_all | solution.py:121
  14.1 2.0 %shard_map.138 = f32[6,2,8192]{2,1,0:T(2,128)} custom-call(f32[16]{0:T(128)} %cse_ref.1, f32[3,16]{1,0:T(4,128)} %rde_ref.1, s32[1,8192]{1,0:T(1,128)} %bitcast.92, f32[2,8192]{1,0:T(2,128)} %warm_ref.1, f32[2,8192]{1,0:T(2,128)} %wet_ref.1, f32[3,8192]{1,0:T(4,128)} %carbon_ref.1), custom_call_target="tpu_custom_call" | custom-call | tf_op jit(solution)/shard_map/pallas_call | solution.py:83
  16.0 1.3 %reshape.196 = f32[6,128,128]{2,1,0:T(8,128)S(1)} reshape(f32[6,2,8192]{2,1,0:T(2,128)} %shard_map.138) | data formatting | bytes 786432 | tf_op jit(solution)/shard_map/reshape | solution.py:131
  17.4 5.2 %all-to-all-done = s32[32,1,128]{2,1,0:T(1,128)S(1)} async-done(((s32[32,1,128]{2,1,0:T(1,128)}), s32[32,1,128]{2,1,0:T(1,128)S(1)}, u32[]{:S(2)}, u32[]{:S(2)}) %all-to-all-start) | async-done | bytes 16416 | tf_op jit(solution)/shard_map/all_to_all | solution.py:121
  22.6 0.1 fusion.26
  22.6 0.1 eq.65
  22.7 0.4 fusion.8
  23.1 0.8 fusion.21
  23.9 0.8 fusion.24
  24.7 0.8 copy.38
  25.4 0.2 copy.36
  25.7 0.0 copy-start.1
  25.7 0.0 copy-start.2
  25.7 0.8 reshape.197
  26.5 4.2 %all-to-all-start.1 = ((f32[32,24,128]{2,1,0:T(8,128)}), f32[32,24,128]{2,1,0:T(8,128)S(1)}, u32[]{:S(2)}, u32[]{:S(2)}) async-start(f32[32,24,128]{2,1,0:T(8,128)} %reshape.197), calls=%async_computation.1 | async-start | bytes 786432 | tf_op jit(solution)/shard_map/all_to_all | solution.py:139
  30.7 0.6 gather_fusion
  31.3 0.7 iota_reduce_fusion
  32.1 11.5 %all-to-all-done.1 = f32[32,24,128]{2,1,0:T(8,128)S(1)} async-done(((f32[32,24,128]{2,1,0:T(8,128)}), f32[32,24,128]{2,1,0:T(8,128)S(1)}, u32[]{:S(2)}, u32[]{:S(2)}) %all-to-all-start.1) | async-done | bytes 393248 | tf_op jit(solution)/shard_map/all_to_all | solution.py:139
  43.5 0.1 reshape.198
  43.6 0.1 fusion.25
  43.7 0.6 gather_fusion.1
  44.3 4.4 %fusion.5 = f32[128,1,128]{2,1,0:T(1,128)S(1)} fusion(bf16[128,128,128]{2,1,0:T(8,128)(2,1)} %param.11, bf16[128,128,1]{1,0,2:T(8,128)(2,1)S(1)} %bitcast.84), kind=kOutput, calls=%fused_computation.16 | convolution fusion | flops 4194304 | bytes 4292608 | tf_op jit(solution)/shard_map/bij,bj->bi/dot_general | solution.py:153
  48.8 0.2 fusion.17
  49.0 0.7 broadcast_in_dim.56
  49.7 7.7 %all-to-all-start.2 = ((f32[8,80,128]{2,1,0:T(8,128)}), f32[8,80,128]{2,1,0:T(8,128)S(1)}, u32[]{:S(2)}, u32[]{:S(2)}) async-start(f32[8,80,128]{2,1,0:T(8,128)} %broadcast_in_dim.56), calls=%async_computation.2 | async-start | bytes 655360 | tf_op jit(solution)/shard_map/all_to_all | solution.py:164
  57.4 0.6 multiply_reduce_fusion.1
  58.0 0.6 multiply_reduce_fusion
  59.9 4.6 %all-to-all-done.2 = f32[8,80,128]{2,1,0:T(8,128)S(1)} async-done(((f32[8,80,128]{2,1,0:T(8,128)}), f32[8,80,128]{2,1,0:T(8,128)S(1)}, u32[]{:S(2)}, u32[]{:S(2)}) %all-to-all-start.2) | async-done | bytes 327712 | tf_op jit(solution)/shard_map/all_to_all | solution.py:164
  64.5 0.6 fusion.12
  65.8 0.7 gather_fusion.2
  66.5 3.4 %fusion.3 = f32[128,1,128]{2,1,0:T(1,128)S(1)} fusion(bf16[128,128,128]{2,1,0:T(8,128)(2,1)} %param.11, bf16[128,128,1]{1,0,2:T(8,128)(2,1)S(1)} %bitcast.85), kind=kOutput, calls=%fused_computation.14 | convolution fusion | flops 4194304 | bytes 4292608 | tf_op jit(solution)/shard_map/bij,bi->bj/dot_general | solution.py:177
  69.9 1.0 %scatter_custom_fusion = f32[128,128]{1,0:T(8,128)S(1)} fusion(s32[128]{0:T(128)S(1)} %get-tuple-element.13, f32[128,128]{1,0:T(8,128)S(1)} %bitcast.88, f32[]{:T(128)} %constant.63.clone.1), kind=kCustom, calls=%fused_computation.31 | custom fusion | flops 16384 | bytes 65540 | tf_op jit(solution)/shard_map/scatter-add | solution.py:180
  71.0 0.9 fusion
  71.9 0.7 pad_maximum_fusion
  72.6 4.0 %all-to-all-start.3 = ((f32[32,9,128]{2,1,0:T(8,128)}), f32[32,9,128]{2,1,0:T(8,128)S(1)}, u32[]{:S(2)}, u32[]{:S(2)}) async-start(f32[32,9,128]{2,1,0:T(8,128)} %pad_maximum_fusion), calls=%async_computation.3 | async-start | bytes 524288 | tf_op jit(solution)/shard_map/all_to_all | solution.py:217
  76.7 0.1 squeeze.24
  76.8 10.3 %all-to-all-done.3 = f32[32,9,128]{2,1,0:T(8,128)S(1)} async-done(((f32[32,9,128]{2,1,0:T(8,128)}), f32[32,9,128]{2,1,0:T(8,128)S(1)}, u32[]{:S(2)}, u32[]{:S(2)}) %all-to-all-start.3) | async-done | bytes 147488 | tf_op jit(solution)/shard_map/all_to_all | solution.py:217
  87.2 0.6 broadcast_in_dim.65
  87.8 6.6 %all-to-all-start.4 = ((f32[8,5,128]{2,1,0:T(8,128)}), f32[8,5,128]{2,1,0:T(8,128)S(1)}, u32[]{:S(2)}, u32[]{:S(2)}) async-start(f32[8,5,128]{2,1,0:T(8,128)} %broadcast_in_dim.65), calls=%async_computation.4 | async-start | bytes 65536 | tf_op jit(solution)/shard_map/all_to_all | solution.py:219
  94.4 0.6 constant_dynamic-slice_fusion
  95.0 1.0 %scatter_custom_fusion.1 = f32[129,128]{1,0:T(8,128)S(1)} fusion(s32[128]{0:T(128)S(1)} %fusion.23, f32[128,128]{1,0:T(8,128)S(1)} %bitcast.90, f32[]{:T(128)} %constant.63.clone.1), kind=kCustom, calls=%fused_computation.24 | custom fusion | flops 16384 | bytes 66052 | tf_op jit(solution)/shard_map/scatter-add | solution.py:227
  96.1 0.7 reshape.203
  96.8 2.4 %all-to-all-done.4 = f32[8,5,128]{2,1,0:T(8,128)S(1)} async-done(((f32[8,5,128]{2,1,0:T(8,128)}), f32[8,5,128]{2,1,0:T(8,128)S(1)}, u32[]{:S(2)}, u32[]{:S(2)}) %all-to-all-start.4) | async-done | bytes 20512 | tf_op jit(solution)/shard_map/all_to_all | solution.py:219
  99.2 0.5 slice.59
  99.7 0.6 slice.58
  (22 shorter events, 0.2 us)
Async XLA Ops:
  0.6 31.4 %copy-start.3 = (s32[3,128]{1,0:T(4,128)S(1)}, s32[3,128]{1,0:T(4,128)}, u32[]{:S(2)}) copy-start(s32[3,128]{1,0:T(4,128)} %param.12) | copy-start | bytes 4612
  2.0 20.6 %all-to-all-start = ((s32[32,1,128]{2,1,0:T(1,128)}), s32[32,1,128]{2,1,0:T(1,128)S(1)}, u32[]{:S(2)}, u32[]{:S(2)}) async-start(s32[32,1,128]{2,1,0:T(1,128)} %bitcast), calls=%async_computation | async-start | bytes 32768 | tf_op jit(solution)/shard_map/all_to_all | solution.py:121
  25.7 23.3 %copy-start.1 = (f32[8,128]{1,0:T(8,128)S(1)}, f32[8,128]{1,0:T(8,128)}, u32[]{:S(2)}) copy-start(f32[8,128]{1,0:T(8,128)} %param.21) | copy-start | bytes 12292
  25.7 23.3 %copy-start.2 = (f32[8,128]{1,0:T(8,128)S(1)}, f32[8,128]{1,0:T(8,128)}, u32[]{:S(2)}) copy-start(f32[8,128]{1,0:T(8,128)} %param.20) | copy-start | bytes 12292
  26.5 30.9 %copy-start.4 = (f32[16]{0:T(128)S(1)}, f32[16]{0:T(128)}, u32[]{:S(2)}) copy-start(f32[16]{0:T(128)} %cse_ref.1) | copy-start | bytes 196
  26.5 31.5 %copy-start = (f32[3,16]{1,0:T(4,128)S(1)}, f32[3,16]{1,0:T(4,128)}, u32[]{:S(2)}) copy-start(f32[3,16]{1,0:T(4,128)} %rde_ref.1) | copy-start | bytes 580
  26.5 17.0 %all-to-all-start.1 = ((f32[32,24,128]{2,1,0:T(8,128)}), f32[32,24,128]{2,1,0:T(8,128)S(1)}, u32[]{:S(2)}, u32[]{:S(2)}) async-start(f32[32,24,128]{2,1,0:T(8,128)} %reshape.197), calls=%async_computation.1 | async-start | bytes 786432 | tf_op jit(solution)/shard_map/all_to_all | solution.py:139
  49.7 14.8 %all-to-all-start.2 = ((f32[8,80,128]{2,1,0:T(8,128)}), f32[8,80,128]{2,1,0:T(8,128)S(1)}, u32[]{:S(2)}, u32[]{:S(2)}) async-start(f32[8,80,128]{2,1,0:T(8,128)} %broadcast_in_dim.56), calls=%async_computation.2 | async-start | bytes 655360 | tf_op jit(solution)/shard_map/all_to_all | solution.py:164
  72.6 14.5 %all-to-all-start.3 = ((f32[32,9,128]{2,1,0:T(8,128)}), f32[32,9,128]{2,1,0:T(8,128)S(1)}, u32[]{:S(2)}, u32[]{:S(2)}) async-start(f32[32,9,128]{2,1,0:T(8,128)} %pad_maximum_fusion), calls=%async_computation.3 | async-start | bytes 524288 | tf_op jit(solution)/shard_map/all_to_all | solution.py:217
  87.8 11.4 %all-to-all-start.4 = ((f32[8,5,128]{2,1,0:T(8,128)}), f32[8,5,128]{2,1,0:T(8,128)S(1)}, u32[]{:S(2)}, u32[]{:S(2)}) async-start(f32[8,5,128]{2,1,0:T(8,128)} %broadcast_in_dim.65), calls=%async_computation.4 | async-start | bytes 65536 | tf_op jit(solution)/shard_map/all_to_all | solution.py:219

commit v16 on v14

--- a/solution.py
+++ b/solution.py
@@ -117,8 +117,11 @@
     cap = needed_tile_lists.shape[1]
     rows_own = measured_anomaly.shape[0]
     rows_dev = rows_own * n_map
-    lanes = jnp.pad(needed_tile_lists, ((0, 0), (0, tile - cap)))[:, None, :]
-    requests = lax.all_to_all(lanes, "snd", 0, 0)[:, 0, :cap]
+    spread = jnp.eye(cap, tile, dtype=jnp.float32)
+    lanes = jnp.dot(
+        needed_tile_lists.astype(jnp.float32), spread, precision=lax.Precision.HIGHEST
+    )
+    requests = lax.all_to_all(lanes[:, None, :], "snd", 0, 0)[:, 0, :cap].astype(jnp.int32)
     live = requests >= 0
     nclass = category_sensitivity_effect.shape[0]
     own_fields = owner_fields(

time: 99.9 us -> 104 us (1.041)
  starting transfers between devices: 34.2 us -> 37.9 us
  matrix products: 9.24 us -> 10.7 us
  local copies, waits for them, and re-layouts: 11 us -> 9.56 us
  waiting for transfers between devices: 32.3 us -> 30.9 us
  other arithmetic: 7.7 us -> 9.09 us
    all_to_all x1, waiting for transfers between devices: 4.42 us -> 0.57 us  [shards(): lax.all_to_all(lanes[:, None, :], 'snd', 0, 0)[:, 0, :cap].astype(jnp.int32)]
    all_to_all x1, starting transfers between devices: 4.95 us -> 8.65 us  [shards(): lax.all_to_all(answer.reshape(n_snd, cap * 6, tile), 'snd', 0, 0)]
    all_to_all x1, waiting for transfers between devices: 4.49 us -> 6.98 us  [shards(): lax.all_to_all(jnp.broadcast_to(payload[None], (n_map,) + payload.shape),...]
    dot_general x0 -> x1, matrix products: none -> 1.5 us  [shards(): jnp.dot(needed_tile_lists.astype(jnp.float32), spread, precision=lax.Prec...]
  transfers between devices with their start and end apart: 5 -> 5, of which waited for: 5 -> 5; matrix products, arithmetic and copies ran while one was open for 7% -> 8% of each run, Pallas kernels for 2% -> 2%
where the time goes in v16:
time: 104 us; the launch traced here: 103 us
  starting transfers between devices  37.9 us (36%)
  waiting for transfers between devices  30.9 us (30%)
  matrix products  10.7 us (10%)
  local copies, waits for them, and re-layouts  9.56 us (9%)
  other arithmetic  9.09 us (9%)
  between operations  2.81 us (3%)
  Pallas kernels  1.97 us (2%)
    all_to_all x1, starting transfers between devices, shards(): lax.all_to_all(lanes[:, None, :], 'snd', 0, 0)[:, 0, :cap].astype(jnp.int32)  12 us
    all_to_all x1, waiting for transfers between devices, shards(): lax.all_to_all(answer.reshape(n_snd, cap * 6, tile), 'snd', 0, 0)  11.6 us
    all_to_all x1, waiting for transfers between devices, shards(): incoming = lax.all_to_all(parcel, 'snd', 0, 0)  9.44 us
    all_to_all x1, starting transfers between devices, shards(): lax.all_to_all(answer.reshape(n_snd, cap * 6, tile), 'snd', 0, 0)  8.65 us
    all_to_all x1, starting transfers between devices, shards(): lax.all_to_all(jnp.broadcast_to(payload[None], (n_map,) + payload.shape),...  7.6 us
    all_to_all x1, waiting for transfers between devices, shards(): lax.all_to_all(jnp.broadcast_to(payload[None], (n_map,) + payload.shape),...  6.98 us
    all_to_all x1, starting transfers between devices, shards(): lax.all_to_all(jnp.broadcast_to(column[None], (n_map, tile)), 'map', 0, 0)  5.73 us
    dot_general x1, matrix products, shards(): jnp.einsum('bij,bj->bi', sensitivity_blocks, vectors, preferred_element_t...  4.43 us
  transfers between devices with their start and end apart: 5, of which 5 were waited for; matrix products, arithmetic and copies ran while one was open for 8% of the time, Pallas kernels for 2%

profile of v16, /device:TPU:1, one launch (start us, length us, event | category | flops | bytes accessed | tf_op | source)
XLA Modules:
  0.0 103.0 jit_solution(11467378845198829576)
XLA Ops:
  0.6 1.5 %fusion.18 = f32[128,32]{0,1:T(8,128)} fusion(s32[32,4]{0,1:T(4,128)} %param.13), kind=kOutput, calls=%fused_computation.47 | convolution fusion | flops 197248 | bytes 16896 | tf_op jit(solution)/shard_map/dot_general | solution.py:121
  2.1 12.0 %all-to-all-start = ((f32[32,1,128]{2,1,0:T(1,128)}), f32[32,1,128]{2,1,0:T(1,128)S(1)}, u32[]{:S(2)}, u32[]{:S(2)}) async-start(f32[32,1,128]{2,1,0:T(1,128)} %bitcast.2), calls=%async_computation | async-start | bytes 32768 | tf_op jit(solution)/shard_map/all_to_all | solution.py:124
  14.2 1.3 %multiply_reduce_fusion = f32[]{:T(128)} fusion(f32[3,16]{1,0:T(4,128)} %rde_ref.1), kind=kLoop, calls=%fused_computation.46 | loop fusion | flops 95 | bytes 196 | tf_op jit(solution)/shard_map/reduce_sum | solution.py:200
  15.5 1.3 %multiply_reduce_fusion.1 = f32[]{:T(128)} fusion(f32[16]{0:T(128)} %cse_ref.1), kind=kLoop, calls=%fused_computation.68 | loop fusion | flops 31 | bytes 68 | tf_op jit(solution)/shard_map/reduce_sum | solution.py:199
  16.7 0.7 maximum_multiply_fusion
  17.4 0.1 div.38
  17.5 2.0 %shard_map.138 = f32[6,2,8192]{2,1,0:T(2,128)} custom-call(f32[16]{0:T(128)} %cse_ref.1, f32[3,16]{1,0:T(4,128)} %rde_ref.1, s32[1,8192]{1,0:T(1,128)} %bitcast.97, f32[2,8192]{1,0:T(2,128)} %warm_ref.1, f32[2,8192]{1,0:T(2,128)} %wet_ref.1, f32[3,8192]{1,0:T(4,128)} %carbon_ref.1), custom_call_target="tpu_custom_call" | custom-call | tf_op jit(solution)/shard_map/pallas_call | solution.py:83
  19.5 1.3 %reshape.222 = f32[6,128,128]{2,1,0:T(8,128)S(1)} reshape(f32[6,2,8192]{2,1,0:T(2,128)} %shard_map.138) | data formatting | bytes 786432 | tf_op jit(solution)/shard_map/reshape | solution.py:134
  22.1 0.6 all-to-all-done
  22.7 0.1 fusion.26
  22.7 0.1 convert_element_type.36
  22.9 0.4 fusion.7
  23.2 0.8 fusion.22
  24.0 0.8 fusion.25
  24.8 0.8 copy.34
  25.6 0.2 copy.32
  25.8 0.8 reshape.223
  26.6 8.6 %all-to-all-start.1 = ((f32[32,24,128]{2,1,0:T(8,128)}), f32[32,24,128]{2,1,0:T(8,128)S(1)}, u32[]{:S(2)}, u32[]{:S(2)}) async-start(f32[32,24,128]{2,1,0:T(8,128)} %reshape.223), calls=%async_computation.1 | async-start | bytes 786432 | tf_op jit(solution)/shard_map/all_to_all | solution.py:142
  35.3 0.6 gather_fusion
  35.9 0.7 iota_reduce_fusion
  36.6 11.6 %all-to-all-done.1 = f32[32,24,128]{2,1,0:T(8,128)S(1)} async-done(((f32[32,24,128]{2,1,0:T(8,128)}), f32[32,24,128]{2,1,0:T(8,128)S(1)}, u32[]{:S(2)}, u32[]{:S(2)}) %all-to-all-start.1) | async-done | bytes 393248 | tf_op jit(solution)/shard_map/all_to_all | solution.py:142
  48.3 0.1 reshape.224
  48.4 0.1 fusion.27
  48.5 0.6 gather_fusion.1
  49.1 4.4 %fusion.4 = f32[128,1,128]{2,1,0:T(1,128)S(1)} fusion(bf16[128,128,128]{2,1,0:T(8,128)(2,1)} %param.11, bf16[128,128,1]{1,0,2:T(8,128)(2,1)S(1)} %bitcast.89), kind=kOutput, calls=%fused_computation.14 | convolution fusion | flops 4194304 | bytes 4292608 | tf_op jit(solution)/shard_map/bij,bj->bi/dot_general | solution.py:156
  53.5 0.2 fusion.16
  53.8 0.7 broadcast_in_dim.59
  54.5 7.6 %all-to-all-start.2 = ((f32[8,80,128]{2,1,0:T(8,128)}), f32[8,80,128]{2,1,0:T(8,128)S(1)}, u32[]{:S(2)}, u32[]{:S(2)}) async-start(f32[8,80,128]{2,1,0:T(8,128)} %broadcast_in_dim.59), calls=%async_computation.2 | async-start | bytes 655360 | tf_op jit(solution)/shard_map/all_to_all | solution.py:167
  62.1 0.1 convert_element_type.38
  62.2 7.0 %all-to-all-done.2 = f32[8,80,128]{2,1,0:T(8,128)S(1)} async-done(((f32[8,80,128]{2,1,0:T(8,128)}), f32[8,80,128]{2,1,0:T(8,128)S(1)}, u32[]{:S(2)}, u32[]{:S(2)}) %all-to-all-start.2) | async-done | bytes 327712 | tf_op jit(solution)/shard_map/all_to_all | solution.py:167
  69.3 0.7 gather_fusion.2
  70.0 3.4 %fusion.2 = f32[128,1,128]{2,1,0:T(1,128)S(1)} fusion(bf16[128,128,128]{2,1,0:T(8,128)(2,1)} %param.11, bf16[128,128,1]{1,0,2:T(8,128)(2,1)S(1)} %bitcast.90), kind=kOutput, calls=%fused_computation.12 | convolution fusion | flops 4194304 | bytes 4292608 | tf_op jit(solution)/shard_map/bij,bi->bj/dot_general | solution.py:180
  73.3 0.6 fusion.11
  74.6 1.0 scatter_custom_fusion
  75.7 0.9 convolution_bitcast_fusion
  76.5 0.1 reshape.228
  76.6 0.1 fusion.20
  76.7 0.7 pad_maximum_fusion
  77.4 3.9 %all-to-all-start.3 = ((f32[32,5,128]{2,1,0:T(8,128)}), f32[32,5,128]{2,1,0:T(8,128)S(1)}, u32[]{:S(2)}, u32[]{:S(2)}) async-start(f32[32,5,128]{2,1,0:T(8,128)} %pad_maximum_fusion), calls=%async_computation.3 | async-start | bytes 262144 | tf_op jit(solution)/shard_map/all_to_all | solution.py:214
  81.4 9.4 %all-to-all-done.3 = f32[32,5,128]{2,1,0:T(8,128)S(1)} async-done(((f32[32,5,128]{2,1,0:T(8,128)}), f32[32,5,128]{2,1,0:T(8,128)S(1)}, u32[]{:S(2)}, u32[]{:S(2)}) %all-to-all-start.3) | async-done | bytes 81952 | tf_op jit(solution)/shard_map/all_to_all | solution.py:214
  90.9 0.6 broadcast_in_dim.69
  91.5 5.7 %all-to-all-start.4 = ((f32[8,1,128]{2,1,0:T(1,128)}), f32[8,1,128]{2,1,0:T(1,128)S(1)}, u32[]{:S(2)}, u32[]{:S(2)}) async-start(f32[8,1,128]{2,1,0:T(1,128)} %broadcast_in_dim.69), calls=%async_computation.4 | async-start | bytes 8192 | tf_op jit(solution)/shard_map/all_to_all | solution.py:216
  97.2 0.6 constant_dynamic-slice_fusion
  97.8 1.0 scatter_custom_fusion.1
  98.8 0.7 reshape.230
  99.5 2.3 %all-to-all-done.4 = f32[8,1,128]{2,1,0:T(1,128)S(1)} async-done(((f32[8,1,128]{2,1,0:T(1,128)}), f32[8,1,128]{2,1,0:T(1,128)S(1)}, u32[]{:S(2)}, u32[]{:S(2)}) %all-to-all-start.4) | async-done | bytes 4128 | tf_op jit(solution)/shard_map/all_to_all | solution.py:216
  101.8 0.6 slice.70
  102.4 0.7 reshape.231
  (22 shorter events, 0.2 us)
Async XLA Ops:
  0.6 36.0 %copy-start.2 = (s32[3,128]{1,0:T(4,128)S(1)}, s32[3,128]{1,0:T(4,128)}, u32[]{:S(2)}) copy-start(s32[3,128]{1,0:T(4,128)} %param.12) | copy-start | bytes 4612
  2.1 20.6 %all-to-all-start = ((f32[32,1,128]{2,1,0:T(1,128)}), f32[32,1,128]{2,1,0:T(1,128)S(1)}, u32[]{:S(2)}, u32[]{:S(2)}) async-start(f32[32,1,128]{2,1,0:T(1,128)} %bitcast.2), calls=%async_computation | async-start | bytes 32768 | tf_op jit(solution)/shard_map/all_to_all | solution.py:124
  25.8 27.9 %copy-start = (f32[8,128]{1,0:T(8,128)S(1)}, f32[8,128]{1,0:T(8,128)}, u32[]{:S(2)}) copy-start(f32[8,128]{1,0:T(8,128)} %param.21) | copy-start | bytes 12292
  25.8 27.9 %copy-start.1 = (f32[8,128]{1,0:T(8,128)S(1)}, f32[8,128]{1,0:T(8,128)}, u32[]{:S(2)}) copy-start(f32[8,128]{1,0:T(8,128)} %param.20) | copy-start | bytes 12292
  26.6 21.7 %all-to-all-start.1 = ((f32[32,24,128]{2,1,0:T(8,128)}), f32[32,24,128]{2,1,0:T(8,128)S(1)}, u32[]{:S(2)}, u32[]{:S(2)}) async-start(f32[32,24,128]{2,1,0:T(8,128)} %reshape.223), calls=%async_computation.1 | async-start | bytes 786432 | tf_op jit(solution)/shard_map/all_to_all | solution.py:142
  54.5 14.7 %all-to-all-start.2 = ((f32[8,80,128]{2,1,0:T(8,128)}), f32[8,80,128]{2,1,0:T(8,128)S(1)}, u32[]{:S(2)}, u32[]{:S(2)}) async-start(f32[8,80,128]{2,1,0:T(8,128)} %broadcast_in_dim.59), calls=%async_computation.2 | async-start | bytes 655360 | tf_op jit(solution)/shard_map/all_to_all | solution.py:167
  77.4 13.4 %all-to-all-start.3 = ((f32[32,5,128]{2,1,0:T(8,128)}), f32[32,5,128]{2,1,0:T(8,128)S(1)}, u32[]{:S(2)}, u32[]{:S(2)}) async-start(f32[32,5,128]{2,1,0:T(8,128)} %pad_maximum_fusion), calls=%async_computation.3 | async-start | bytes 262144 | tf_op jit(solution)/shard_map/all_to_all | solution.py:214
  91.5 10.3 %all-to-all-start.4 = ((f32[8,1,128]{2,1,0:T(1,128)}), f32[8,1,128]{2,1,0:T(1,128)S(1)}, u32[]{:S(2)}, u32[]{:S(2)}) async-start(f32[8,1,128]{2,1,0:T(1,128)} %broadcast_in_dim.69), calls=%async_computation.4 | async-start | bytes 8192 | tf_op jit(solution)/shard_map/all_to_all | solution.py:216

commit v17 on v14

--- a/solution.py
+++ b/solution.py
@@ -156,13 +156,27 @@
     row_hot = (jnp.arange(rows_dev, dtype=jnp.int32)[:, None] == block_row[None, :]).astype(
         jnp.float32
     )
-    partial_rows = jnp.dot(row_hot, contrib, precision=lax.Precision.HIGHEST)
 
     me_map = lax.axis_index("map")
     first = me_map * rows_own
-    payload = jnp.concatenate([partial_rows, measured_anomaly, retrieval_precision], axis=0)
+    extra = 2 * rows_own
+    picks = jnp.concatenate(
+        [
+            jnp.concatenate([row_hot, jnp.zeros((rows_dev, extra), jnp.float32)], axis=1),
+            jnp.concatenate(
+                [jnp.zeros((extra, row_hot.shape[1]), jnp.float32), jnp.eye(extra, dtype=jnp.float32)],
+                axis=1,
+            ),
+        ],
+        axis=0,
+    )
+    picks = jnp.broadcast_to(picks[None], (n_map,) + picks.shape).reshape(-1, picks.shape[1])
+    sources = jnp.concatenate([contrib, measured_anomaly, retrieval_precision], axis=0)
     swapped = lax.all_to_all(
-        jnp.broadcast_to(payload[None], (n_map,) + payload.shape), "map", 0, 0
+        jnp.dot(picks, sources, precision=lax.Precision.HIGHEST).reshape(n_map, -1, tile),
+        "map",
+        0,
+        0,
     )
     model_rows = jnp.sum(swapped[:, :rows_dev], axis=0)
     anomaly_rows = swapped[:, rows_dev : rows_dev + rows_own].reshape(rows_dev, tile)

time: 99.9 us -> 101 us (1.011)
  matrix products: 9.24 us -> 11.3 us
    dot_general x1, matrix products: 0.19 us -> 2.25 us  [shards(): jnp.dot(picks, sources, precision=lax.Precision.HIGHEST)]
where the time goes in v17:
time: 101 us
  starting transfers between devices  34.3 us (34%)
  waiting for transfers between devices  32.1 us (32%)
  matrix products  11.3 us (11%)
  local copies, waits for them, and re-layouts  10.3 us (10%)
  other arithmetic  7.87 us (8%)
  between operations  2.79 us (3%)
  Pallas kernels  1.97 us (2%)
    all_to_all x1, starting transfers between devices, shards(): requests = lax.all_to_all(lanes, 'snd', 0, 0)[:, 0, :cap]  12 us
    all_to_all x1, waiting for transfers between devices, shards(): lax.all_to_all(answer.reshape(n_snd, cap * 6, tile), 'snd', 0, 0)  11.5 us
    all_to_all x1, waiting for transfers between devices, shards(): incoming = lax.all_to_all(parcel, 'snd', 0, 0)  9.44 us
    all_to_all x1, starting transfers between devices, shards(): lax.all_to_all(jnp.dot(picks, sources, precision=lax.Precision.HIGHEST).r...  7.6 us
    all_to_all x1, starting transfers between devices, shards(): lax.all_to_all(jnp.broadcast_to(column[None], (n_map, tile)), 'map', 0, 0)  5.73 us
    all_to_all x1, starting transfers between devices, shards(): lax.all_to_all(answer.reshape(n_snd, cap * 6, tile), 'snd', 0, 0)  4.96 us
    all_to_all x1, waiting for transfers between devices, shards(): lax.all_to_all(jnp.dot(picks, sources, precision=lax.Precision.HIGHEST).r...  4.49 us
    dot_general x1, matrix products, shards(): jnp.einsum('bij,bj->bi', sensitivity_blocks, vectors, preferred_element_t...  4.43 us
  transfers between devices with their start and end apart: 5, of which 5 were waited for; matrix products, arithmetic and copies ran while one was open for 7% of the time, Pallas kernels for 2%

profile of v17, /device:TPU:1, one launch (start us, length us, event | category | flops | bytes accessed | tf_op | source)
XLA Modules:
  0.0 100.5 jit_solution(3372573960375534689)
XLA Ops:
  0.6 0.8 copy.35
  1.4 0.6 pad.12
  2.0 12.0 %all-to-all-start = ((s32[32,1,128]{2,1,0:T(1,128)}), s32[32,1,128]{2,1,0:T(1,128)S(1)}, u32[]{:S(2)}, u32[]{:S(2)}) async-start(s32[32,1,128]{2,1,0:T(1,128)} %bitcast), calls=%async_computation | async-start | bytes 32768 | tf_op jit(solution)/shard_map/all_to_all | solution.py:121
  14.1 0.7 maximum_multiply_fusion
  14.8 0.1 div.38
  14.9 2.0 %shard_map.138 = f32[6,2,8192]{2,1,0:T(2,128)} custom-call(f32[16]{0:T(128)} %cse_ref.1, f32[3,16]{1,0:T(4,128)} %rde_ref.1, s32[1,8192]{1,0:T(1,128)} %bitcast.95, f32[2,8192]{1,0:T(2,128)} %warm_ref.1, f32[2,8192]{1,0:T(2,128)} %wet_ref.1, f32[3,8192]{1,0:T(4,128)} %carbon_ref.1), custom_call_target="tpu_custom_call" | custom-call | tf_op jit(solution)/shard_map/pallas_call | solution.py:83
  16.8 1.3 %reshape.225 = f32[6,128,128]{2,1,0:T(8,128)S(1)} reshape(f32[6,2,8192]{2,1,0:T(2,128)} %shard_map.138) | data formatting | bytes 786432 | tf_op jit(solution)/shard_map/reshape | solution.py:131
  18.2 4.4 %all-to-all-done = s32[32,1,128]{2,1,0:T(1,128)S(1)} async-done(((s32[32,1,128]{2,1,0:T(1,128)}), s32[32,1,128]{2,1,0:T(1,128)S(1)}, u32[]{:S(2)}, u32[]{:S(2)}) %all-to-all-start) | async-done | bytes 16416 | tf_op jit(solution)/shard_map/all_to_all | solution.py:121
  22.6 0.1 eq.68
  22.7 0.4 fusion.14
  23.1 0.8 fusion.25
  23.9 0.8 fusion.28
  24.7 0.8 copy.38
  25.4 0.2 copy.36
  25.7 0.8 reshape.226
  26.5 5.0 %all-to-all-start.1 = ((f32[32,24,128]{2,1,0:T(8,128)}), f32[32,24,128]{2,1,0:T(8,128)S(1)}, u32[]{:S(2)}, u32[]{:S(2)}) async-start(f32[32,24,128]{2,1,0:T(8,128)} %reshape.226), calls=%async_computation.1 | async-start | bytes 786432 | tf_op jit(solution)/shard_map/all_to_all | solution.py:139
  31.4 0.6 gather_fusion
  32.1 0.7 iota_reduce_fusion
  32.8 0.1 iota_compare_fusion.3
  32.9 0.1 fusion.8
  33.0 11.5 %all-to-all-done.1 = f32[32,24,128]{2,1,0:T(8,128)S(1)} async-done(((f32[32,24,128]{2,1,0:T(8,128)}), f32[32,24,128]{2,1,0:T(8,128)S(1)}, u32[]{:S(2)}, u32[]{:S(2)}) %all-to-all-start.1) | async-done | bytes 393248 | tf_op jit(solution)/shard_map/all_to_all | solution.py:139
  44.5 0.1 fusion.30
  44.6 0.6 gather_fusion.1
  45.3 4.4 %fusion.11 = f32[128,1,128]{2,1,0:T(1,128)S(1)} fusion(bf16[128,128,128]{2,1,0:T(8,128)(2,1)} %param.11, bf16[128,128,1]{1,0,2:T(8,128)(2,1)S(1)} %bitcast.87), kind=kOutput, calls=%fused_computation.23 | convolution fusion | flops 4194304 | bytes 4292608 | tf_op jit(solution)/shard_map/bij,bj->bi/dot_general | solution.py:153
  49.7 2.2 %fusion.1 = f32[8,80,128]{2,1,0:T(8,128)} fusion(f32[80,144]{0,1:T(8,128)S(1)} %fusion.8, f32[8,128]{1,0:T(8,128)S(1)} %copy-done.1, f32[8,128]{1,0:T(8,128)S(1)} %copy-done.2, f32[128,128]{1,0:T(8,128)S(1)} %bitcast.89), kind=kOutput, calls=%fused_computation.8 | convolution fusion | flops 141594624 | bytes 447488 | tf_op jit(solution)/shard_map/dot_general | solution.py:176
  52.0 7.6 %all-to-all-start.2 = ((f32[8,80,128]{2,1,0:T(8,128)}), f32[8,80,128]{2,1,0:T(8,128)S(1)}, u32[]{:S(2)}, u32[]{:S(2)}) async-start(f32[8,80,128]{2,1,0:T(8,128)} %fusion.1), calls=%async_computation.2 | async-start | bytes 655360 | tf_op jit(solution)/shard_map/all_to_all | solution.py:175
  59.6 0.6 multiply_reduce_fusion.1
  60.2 0.6 multiply_reduce_fusion
  62.1 0.1 squeeze.25
  62.2 4.5 %all-to-all-done.2 = f32[8,80,128]{2,1,0:T(8,128)S(1)} async-done(((f32[8,80,128]{2,1,0:T(8,128)}), f32[8,80,128]{2,1,0:T(8,128)S(1)}, u32[]{:S(2)}, u32[]{:S(2)}) %all-to-all-start.2) | async-done | bytes 327712 | tf_op jit(solution)/shard_map/all_to_all | solution.py:175
  66.7 0.7 gather_fusion.2
  67.4 3.4 %fusion.9 = f32[128,1,128]{2,1,0:T(1,128)S(1)} fusion(bf16[128,128,128]{2,1,0:T(8,128)(2,1)} %param.11, bf16[128,128,1]{1,0,2:T(8,128)(2,1)S(1)} %bitcast.88), kind=kOutput, calls=%fused_computation.21 | convolution fusion | flops 4194304 | bytes 4292608 | tf_op jit(solution)/shard_map/bij,bi->bj/dot_general | solution.py:191
  70.8 0.6 fusion.18
  72.1 1.0 %scatter_custom_fusion = f32[128,128]{1,0:T(8,128)S(1)} fusion(s32[128]{0:T(128)S(1)} %get-tuple-element.13, f32[128,128]{1,0:T(8,128)S(1)} %bitcast.91, f32[]{:T(128)} %constant.66.clone.1), kind=kCustom, calls=%fused_computation.38 | custom fusion | flops 16384 | bytes 65540 | tf_op jit(solution)/shard_map/scatter-add | solution.py:194
  73.1 0.9 convolution_bitcast_fusion
  74.0 0.1 reshape.231
  74.1 0.1 fusion.23
  74.2 0.7 pad_maximum_fusion
  74.9 3.9 %all-to-all-start.3 = ((f32[32,5,128]{2,1,0:T(8,128)}), f32[32,5,128]{2,1,0:T(8,128)S(1)}, u32[]{:S(2)}, u32[]{:S(2)}) async-start(f32[32,5,128]{2,1,0:T(8,128)} %pad_maximum_fusion), calls=%async_computation.3 | async-start | bytes 262144 | tf_op jit(solution)/shard_map/all_to_all | solution.py:225
  78.8 9.4 %all-to-all-done.3 = f32[32,5,128]{2,1,0:T(8,128)S(1)} async-done(((f32[32,5,128]{2,1,0:T(8,128)}), f32[32,5,128]{2,1,0:T(8,128)S(1)}, u32[]{:S(2)}, u32[]{:S(2)}) %all-to-all-start.3) | async-done | bytes 81952 | tf_op jit(solution)/shard_map/all_to_all | solution.py:225
  88.3 0.6 broadcast_in_dim.71
  88.9 5.7 %all-to-all-start.4 = ((f32[8,1,128]{2,1,0:T(1,128)}), f32[8,1,128]{2,1,0:T(1,128)S(1)}, u32[]{:S(2)}, u32[]{:S(2)}) async-start(f32[8,1,128]{2,1,0:T(1,128)} %broadcast_in_dim.71), calls=%async_computation.4 | async-start | bytes 8192 | tf_op jit(solution)/shard_map/all_to_all | solution.py:227
  94.7 0.6 constant_dynamic-slice_fusion
  95.3 1.0 %scatter_custom_fusion.1 = f32[129,128]{1,0:T(8,128)S(1)} fusion(s32[128]{0:T(128)S(1)} %fusion.27, f32[128,128]{1,0:T(8,128)S(1)} %bitcast.93, f32[]{:T(128)} %constant.66.clone.1), kind=kCustom, calls=%fused_computation.31 | custom fusion | flops 16384 | bytes 66052 | tf_op jit(solution)/shard_map/scatter-add | solution.py:231
  96.3 0.7 reshape.233
  97.0 2.3 %all-to-all-done.4 = f32[8,1,128]{2,1,0:T(1,128)S(1)} async-done(((f32[8,1,128]{2,1,0:T(1,128)}), f32[8,1,128]{2,1,0:T(1,128)S(1)}, u32[]{:S(2)}, u32[]{:S(2)}) %all-to-all-start.4) | async-done | bytes 4128 | tf_op jit(solution)/shard_map/all_to_all | solution.py:227
  99.3 0.6 slice.70
  99.9 0.7 reshape.234
  (27 shorter events, 0.3 us)
Async XLA Ops:
  0.6 32.2 %copy-start.4 = (s32[3,128]{1,0:T(4,128)S(1)}, s32[3,128]{1,0:T(4,128)}, u32[]{:S(2)}) copy-start(s32[3,128]{1,0:T(4,128)} %param.12) | copy-start | bytes 4612
  2.0 20.6 %all-to-all-start = ((s32[32,1,128]{2,1,0:T(1,128)}), s32[32,1,128]{2,1,0:T(1,128)S(1)}, u32[]{:S(2)}, u32[]{:S(2)}) async-start(s32[32,1,128]{2,1,0:T(1,128)} %bitcast), calls=%async_computation | async-start | bytes 32768 | tf_op jit(solution)/shard_map/all_to_all | solution.py:121
  25.7 24.1 %copy-start.1 = (f32[8,128]{1,0:T(8,128)S(1)}, f32[8,128]{1,0:T(8,128)}, u32[]{:S(2)}) copy-start(f32[8,128]{1,0:T(8,128)} %param.21) | copy-start | bytes 12292
  25.7 24.0 %copy-start.2 = (f32[8,128]{1,0:T(8,128)S(1)}, f32[8,128]{1,0:T(8,128)}, u32[]{:S(2)}) copy-start(f32[8,128]{1,0:T(8,128)} %param.20) | copy-start | bytes 12292
  26.5 33.1 %copy-start.3 = (f32[16]{0:T(128)S(1)}, f32[16]{0:T(128)}, u32[]{:S(2)}) copy-start(f32[16]{0:T(128)} %cse_ref.1) | copy-start | bytes 196
  26.5 33.7 %copy-start = (f32[3,16]{1,0:T(4,128)S(1)}, f32[3,16]{1,0:T(4,128)}, u32[]{:S(2)}) copy-start(f32[3,16]{1,0:T(4,128)} %rde_ref.1) | copy-start | bytes 580
  26.5 18.0 %all-to-all-start.1 = ((f32[32,24,128]{2,1,0:T(8,128)}), f32[32,24,128]{2,1,0:T(8,128)S(1)}, u32[]{:S(2)}, u32[]{:S(2)}) async-start(f32[32,24,128]{2,1,0:T(8,128)} %reshape.226), calls=%async_computation.1 | async-start | bytes 786432 | tf_op jit(solution)/shard_map/all_to_all | solution.py:139
  52.0 14.7 %all-to-all-start.2 = ((f32[8,80,128]{2,1,0:T(8,128)}), f32[8,80,128]{2,1,0:T(8,128)S(1)}, u32[]{:S(2)}, u32[]{:S(2)}) async-start(f32[8,80,128]{2,1,0:T(8,128)} %fusion.1), calls=%async_computation.2 | async-start | bytes 655360 | tf_op jit(solution)/shard_map/all_to_all | solution.py:175
  74.9 13.4 %all-to-all-start.3 = ((f32[32,5,128]{2,1,0:T(8,128)}), f32[32,5,128]{2,1,0:T(8,128)S(1)}, u32[]{:S(2)}, u32[]{:S(2)}) async-start(f32[32,5,128]{2,1,0:T(8,128)} %pad_maximum_fusion), calls=%async_computation.3 | async-start | bytes 262144 | tf_op jit(solution)/shard_map/all_to_all | solution.py:225
  88.9 10.3 %all-to-all-start.4 = ((f32[8,1,128]{2,1,0:T(1,128)}), f32[8,1,128]{2,1,0:T(1,128)S(1)}, u32[]{:S(2)}, u32[]{:S(2)}) async-start(f32[8,1,128]{2,1,0:T(1,128)} %broadcast_in_dim.71), calls=%async_computation.4 | async-start | bytes 8192 | tf_op jit(solution)/shard_map/all_to_all | solution.py:227
